TPU v7x, 128 devices: a whole 4x4x4 slice. The times are simulated.
128 devices in a mesh: own: 32 (over y, z, core), vir: 4 (over x).
Axes of the slice: x: 4, y: 4, z: 4, core: 2. Of those that a mesh axis runs over, the one named last changes fastest.
Arguments:
- amplitudes: float32 [384, 512, 1024], P('vir', 'own'), may hold values from -6 to 6
- pair_live: int32 [384, 512], P('vir', 'own'), may hold values 0 or 1
- ladder_integrals: float32 [1024, 1024], P('own'), may hold values from -0.1875 to 0.1875
- cycle_integrals: float32 [512, 32, 128], P('vir'), may hold values from -0.046875 to 0.046875
Outputs:
- ladder_part: float32 [384, 512, 1024], P('vir', 'own')
- cycle_part: float32 [384, 32, 128], P('vir', 'own')
All inputs are finite; a program needn't handle non-finite values. No bound on the sum of `pair_live` on one device may be relied on, other than what follows from the above.
Results may differ from a plain program's by a relative error of at most 0.00007.
Values sent between devices are 32-bit elements; how exact they have to be, the bound alone decides.
No kernel may reach another device: no remote copies, remote signals or barrier semaphores. Data moves between devices by JAX's collectives and lax.ppermute only.
A program may use at most 128 MiB of HBM per device.

v0:
```python
import jax
import jax.numpy as jnp
from jax import lax
from jax.sharding import PartitionSpec as P


def cycle_product(relaid, integrals):
    rows = relaid.shape[0]
    kblock = relaid.shape[1]
    virtuals = integrals.shape[1]
    split = relaid.reshape(rows, kblock, relaid.shape[2] // virtuals, virtuals)
    return jnp.einsum(
        "ikac,kcm->iam",
        split,
        integrals,
        precision=lax.Precision.HIGHEST,
        preferred_element_type=jnp.float32,
    )


def local(amplitudes, pair_live, ladder_integrals, cycle_integrals):
    live = pair_live.astype(jnp.float32)
    screened = amplitudes * live[:, :, None]
    first_rows = screened.shape[0]
    second_rows = screened.shape[1]
    width = screened.shape[2]
    flat = screened.reshape(first_rows * second_rows, width)
    ladder = jnp.dot(
        flat,
        lax.all_gather(ladder_integrals, "own", axis=0, tiled=True),
        precision=lax.Precision.HIGHEST,
        preferred_element_type=jnp.float32,
    )
    ladder_part = ladder.reshape(first_rows, second_rows, width) * live[:, :, None]
    relaid = lax.all_to_all(
        lax.all_to_all(screened, "own", split_axis=2, concat_axis=1, tiled=True),
        "vir",
        split_axis=1,
        concat_axis=0,
        tiled=True,
    )
    partial_value = cycle_product(relaid, cycle_integrals)
    cycle_part = lax.psum_scatter(partial_value, "vir", scatter_dimension=0, tiled=True)
    return (ladder_part, cycle_part)


def solution(mesh):
    placed = (P("vir", "own", None), P("vir", "own"), P("own", None), P("vir", None, None))
    return jax.shard_map(
        local,
        mesh=mesh,
        in_specs=placed,
        out_specs=(P("vir", "own", None), P("vir", "own", None)),
        check_vma=False,
    )
```

profile of v0, /device:TPU:48, one launch (start us, length us, event | category | flops | bytes accessed | tf_op | source)
XLA Modules:
  0.0 320.9 jit_solution(6343029211390134006)
XLA Ops:
  8.0 0.0 copy-start
  8.0 0.8 convert_element_type.3
  8.9 0.1 copy.24
  9.0 6.0 %broadcast_multiply_fusion.1 = f32[96,16,1024]{2,1,0:T(8,128)} fusion(f32[96,16,1024]{2,1,0:T(8,128)} %param.4, f32[96,16]{1,0:T(8,128)S(1)} %copy.24), kind=kLoop, calls=%fused_computation.3 | loop fusion | flops 1572864 | bytes 12589056 | tf_op jit(solution)/shard_map/mul | solution.py:23
  14.9 8.5 %copy.25 = f32[96,16,1024]{0,1,2:T(8,128)} copy(f32[96,16,1024]{2,1,0:T(8,128)} %broadcast_multiply_fusion.1) | data formatting | bytes 12582912 | tf_op jit(solution)/shard_map/mul | solution.py:23
  23.4 8.0 %all-to-all-start = ((f32[96,16,1024]{0,1,2:T(8,128)}), f32[96,16,1024]{0,1,2:T(8,128)}, u32[]{:S(2)}, u32[]{:S(2)}) async-start(f32[96,16,1024]{0,1,2:T(8,128)} %copy.25), calls=%async_computation | async-start | bytes 16777216 | tf_op jit(solution)/shard_map/all_to_all | solution.py:36
  31.5 0.0 all-gather.2.cloned.1.call-start
  31.5 0.7 all-gather.2.cloned.1.call-update
  32.2 0.0 reduce-scatter.2.cloned.1.call-start
  32.3 129.5 %all-to-all-done = f32[96,16,1024]{0,1,2:T(8,128)} async-done(((f32[96,16,1024]{0,1,2:T(8,128)}), f32[96,16,1024]{0,1,2:T(8,128)}, u32[]{:S(2)}, u32[]{:S(2)}) %all-to-all-start) | async-done | bytes 6291488 | tf_op jit(solution)/shard_map/all_to_all | solution.py:36
  161.8 6.8 %copy.27 = f32[96,32,16,32]{0,3,2,1:T(8,128)S(1)} copy(f32[96,32,16,32]{0,2,3,1:T(8,128)} %bitcast.3) | data formatting | bytes 12582912 | tf_op jit(solution)/shard_map/all_to_all | solution.py:36
  168.6 97.6 %all_to_all.33 = f32[96,512,32]{0,2,1:T(8,128)} all-to-all(f32[96,512,32]{0,2,1:T(8,128)S(1)} %bitcast.18), channel_id=1, replica_groups=mesh['own'=32,'vir'=4] {'vir'}, dimensions={1} | all-to-all | bytes 12582912 | tf_op jit(solution)/shard_map/all_to_all | solution.py:35
  266.3 8.7 %copy.33 = f32[96,4,128,32]{2,1,3,0:T(4,128)} copy(f32[96,4,128,32]{0,3,2,1:T(8,128)} %bitcast.17) | data formatting | bytes 12582912 | tf_op jit(solution)/shard_map/all_to_all | solution.py:35
  275.0 6.4 %copy.29 = f32[4,96,128,32]{2,1,0,3:T(8,128)S(1)} copy(f32[4,96,128,32]{2,0,3,1:T(4,128)} %bitcast.19) | data formatting | bytes 12582912 | tf_op jit(solution)/shard_map/all_to_all | solution.py:35
  281.4 0.0 copy-done
  281.4 6.6 %fusion.6 = f32[384,1,128]{2,0,1:T(8,128)} fusion(f32[384,128,32]{1,0,2:T(8,128)S(1)} %bitcast.20, f32[128,32,128]{2,1,0:T(8,128)S(1)} %copy-done), kind=kOutput, calls=%fused_computation.6 | convolution fusion | flops 2415919104 | bytes 8585216 | tf_op jit(solution)/shard_map/ikac,kcm->iam/dot_general | solution.py:12
  288.0 0.0 reduce-scatter.2.cloned.1.call-update
  288.1 0.0 all-gather.2.cloned.1.call-done
  288.1 25.4 %broadcast_multiply_fusion = f32[96,16,1024]{2,1,0:T(8,128)} fusion(f32[96,16]{1,0:T(8,128)S(1)} %copy.24, f32[1024,1024]{1,0:T(8,128)} %all-gather.2.cloned.1.call-done, f32[96,16,1024]{2,1,0:T(8,128)} %param.4), kind=kOutput, calls=%fused_computation.2 | convolution fusion | flops 19330498560 | bytes 16783360 | tf_op jit(solution)/shard_map/dot_general | solution.py:28
  313.5 0.0 reduce-scatter.2.cloned.1.call-done
Async XLA Ops:
  8.0 273.4 %copy-start = (f32[128,32,128]{2,1,0:T(8,128)S(1)}, f32[128,32,128]{2,1,0:T(8,128)}, u32[]{:S(2)}) copy-start(f32[128,32,128]{2,1,0:T(8,128)} %param.7) | copy-start | bytes 6291460
  23.4 138.4 %all-to-all-start = ((f32[96,16,1024]{0,1,2:T(8,128)}), f32[96,16,1024]{0,1,2:T(8,128)}, u32[]{:S(2)}, u32[]{:S(2)}) async-start(f32[96,16,1024]{0,1,2:T(8,128)} %copy.25), calls=%async_computation | async-start | bytes 16777216 | tf_op jit(solution)/shard_map/all_to_all | solution.py:36
  31.5 256.6 %all-gather.2.cloned.1.call-start = ((), (), s32[]{:S(2)}) async-start(), calls=%async_computation.3 | async-start | bytes 4325376 | tf_op jit(solution)/shard_map/all_gather | solution.py:30
  32.2 281.2 %reduce-scatter.2.cloned.1.call-start = ((), (), s32[]{:S(2)}) async-start(), calls=%async_computation.4 | async-start | bytes 245760 | tf_op jit(solution)/shard_map/reduce_scatter | solution.py:43
Sparse Core Ops, SparseCore 0:
  34.5 106.7 all-gather.1
Sparse Core Ops, SparseCore 1:
  288.1 18.5 reduce-scatter.1
where the time goes:
time: 321 us
  waiting for transfers between devices  130 us (40%)
  blocking collectives  97.6 us (30%)
  matrix products  32 us (10%)
  local copies, waits for them, and re-layouts  30.5 us (10%)
  between operations  15.5 us (5%)
  starting transfers between devices  8.13 us (3%)
  other arithmetic  6.82 us (2%)
    all_to_all x1, waiting for transfers between devices, local(): lax.all_to_all(screened, 'own', split_axis=2, concat_axis=1, tiled=True)  130 us
    all_to_all x1, blocking collectives, local(): lax.all_to_all(lax.all_to_all(screened, 'own', split_axis=2, concat_axis=...  97.6 us
    dot_general x1, matrix products, local(): jnp.dot(flat, lax.all_gather(ladder_integrals, 'own', axis=0, tiled=True)...  25.4 us
    all_to_all x2, local copies, waits for them, and re-layouts, local(): lax.all_to_all(lax.all_to_all(screened, 'own', split_axis=2, concat_axis=...  15.1 us
    mul x1, local copies, waits for them, and re-layouts, local(): screened = amplitudes * live[:, :, None]  8.49 us
    all_to_all x1, starting transfers between devices, local(): lax.all_to_all(screened, 'own', split_axis=2, concat_axis=1, tiled=True)  8.04 us
    all_to_all x1, local copies, waits for them, and re-layouts, local(): lax.all_to_all(screened, 'own', split_axis=2, concat_axis=1, tiled=True)  6.83 us
    dot_general x1, matrix products, cycle_product(): jnp.einsum('ikac,kcm->iam', split, integrals, precision=lax.Precision.HIG...  6.63 us
  transfers between devices with their start and end apart: 3, of which 1 were waited for; matrix products, arithmetic and copies ran while one was open for 17% of the time, Pallas kernels for 0%

commit v1 on v0

v1 whole, which is shorter than its diff:
```python
import jax
import jax.numpy as jnp
from jax import lax
from jax.sharding import PartitionSpec as P


def cycle_piece(cycle_integrals, kblock):
    own = lax.axis_index("own")
    held = cycle_integrals.shape[0]
    start = own * kblock
    piece = lax.dynamic_slice_in_dim(cycle_integrals, start % held, kblock, axis=0)
    pieces = lax.all_gather(piece, "vir")
    return lax.dynamic_index_in_dim(pieces, start // held, axis=0, keepdims=False)


def local(amplitudes, pair_live, ladder_integrals, cycle_integrals):
    live = pair_live.astype(jnp.float32)
    screened = amplitudes * live[:, :, None]
    first_rows = screened.shape[0]
    second_rows = screened.shape[1]
    width = screened.shape[2]
    virtuals = cycle_integrals.shape[1]

    weights = cycle_piece(cycle_integrals, second_rows)
    split = screened.reshape(first_rows, second_rows, width // virtuals, virtuals)
    partial_value = jnp.einsum(
        "ikac,kcm->iam",
        split,
        weights,
        precision=lax.Precision.HIGHEST,
        preferred_element_type=jnp.float32,
    )
    cycle_part = lax.psum_scatter(partial_value, "own", scatter_dimension=1, tiled=True)

    flat = screened.reshape(first_rows * second_rows, width)
    ladder = jnp.dot(
        flat,
        lax.all_gather(ladder_integrals, "own", axis=0, tiled=True),
        precision=lax.Precision.HIGHEST,
        preferred_element_type=jnp.float32,
    )
    ladder_part = ladder.reshape(first_rows, second_rows, width) * live[:, :, None]
    return (ladder_part, cycle_part)


def solution(mesh):
    placed = (P("vir", "own", None), P("vir", "own"), P("own", None), P("vir", None, None))
    return jax.shard_map(
        local,
        mesh=mesh,
        in_specs=placed,
        out_specs=(P("vir", "own", None), P("vir", "own", None)),
        check_vma=False,
    )
```

time: 321 us -> 174 us (0.54)
  the two profiles are of different devices: /device:TPU:48 before, /device:TPU:1 now
where the time goes in v1:
time: 174 us; the launch traced here: 172 us
  waiting for transfers between devices  99.8 us (57%)
  matrix products  41.6 us (24%)
  between operations  13.8 us (8%)
  local copies, waits for them, and re-layouts  10.5 us (6%)
  other arithmetic  6.67 us (4%)
    reduce_scatter x1, waiting for transfers between devices, local(): lax.psum_scatter(partial_value, 'own', scatter_dimension=1, tiled=True)  54.6 us
    all_gather x1, waiting for transfers between devices, local(): lax.all_gather(ladder_integrals, 'own', axis=0, tiled=True)  34.8 us
    dot_general x1, matrix products, local(): jnp.dot(flat, lax.all_gather(ladder_integrals, 'own', axis=0, tiled=True)...  25.1 us
    dot_general x1, matrix products, local(): jnp.einsum('ikac,kcm->iam', split, weights, precision=lax.Precision.HIGHE...  16.5 us
    all_gather x1, waiting for transfers between devices, cycle_piece(): pieces = lax.all_gather(piece, 'vir')  9.57 us
    mul x1, local copies, waits for them, and re-layouts, local(): screened = amplitudes * live[:, :, None]  8.2 us
    mul x1, other arithmetic, local(): screened = amplitudes * live[:, :, None]  5.97 us
  transfers between devices with their start and end apart: 3, of which 3 were waited for; matrix products, arithmetic and copies ran while one was open for 33% of the time, Pallas kernels for 0%

profile of v1, /device:TPU:1, one launch (start us, length us, event | category | flops | bytes accessed | tf_op | source)
XLA Modules:
  0.0 172.5 jit_solution(13416756823033637218)
XLA Ops:
  7.2 0.0 copy-start
  7.2 0.0 all-gather.6.cloned.1.call-start
  7.2 1.5 copy-done
  8.8 0.7 constant_dynamic-slice_fusion
  9.5 0.0 all-gather.6.cloned.1.call-update
  9.5 0.0 all-gather.4.cloned.1.call-start
  9.6 0.7 all-gather.4.cloned.1.call-update
  10.3 0.0 reduce-scatter.2.cloned.1.call-start
  10.3 0.7 convert_element_type.3
  11.0 0.1 copy.10
  11.1 6.0 %broadcast_multiply_fusion.1 = f32[96,16,1024]{2,1,0:T(8,128)} fusion(f32[96,16,1024]{2,1,0:T(8,128)} %param.4, f32[96,16]{1,0:T(8,128)S(1)} %copy.10), kind=kLoop, calls=%fused_computation.3 | loop fusion | flops 1572864 | bytes 12589056 | tf_op jit(solution)/shard_map/mul | solution.py:18
  17.1 8.2 %copy.11 = f32[96,16,1024]{0,2,1:T(8,128)} copy(f32[96,16,1024]{2,1,0:T(8,128)} %broadcast_multiply_fusion.1) | data formatting | bytes 12582912 | tf_op jit(solution)/shard_map/mul | solution.py:18
  25.3 9.6 %all-gather.6.cloned.1.call-done = f32[64,32,128]{2,1,0:T(8,128)} async-done(((f32[16,32,128]{2,1,0:T(8,128)}), f32[64,32,128]{2,1,0:T(8,128)}) %all-gather.6.cloned.1.call-update) | async-done | bytes 1048592 | tf_op jit(solution)/shard_map/all_gather | solution.py:12
  34.9 16.5 %convolution_bitcast_fusion = f32[96,32,128]{2,0,1:T(8,128)} fusion(f32[96,16,32,32]{0,3,2,1:T(8,128)} %bitcast.17, f32[4,16,32,128]{3,2,1,0:T(8,128)} %bitcast.18, s32[]{:T(128)S(6)} %select_n.21), kind=kOutput, calls=%fused_computation.4 | convolution fusion | flops 2415919104 | bytes 10223620 | tf_op jit(solution)/shard_map/ikac,kcm->iam/dot_general | solution.py:26
  51.3 0.0 reduce-scatter.2.cloned.1.call-update
  51.4 34.8 %all-gather.4.cloned.1.call-done = f32[1024,1024]{1,0:T(8,128)} async-done(((f32[32,1024]{1,0:T(8,128)}), f32[1024,1024]{1,0:T(8,128)}) %all-gather.4.cloned.1.call-update) | async-done | bytes 4194320 | tf_op jit(solution)/shard_map/all_gather | solution.py:38
  86.2 25.1 %broadcast_multiply_fusion = f32[96,16,1024]{2,1,0:T(8,128)} fusion(f32[96,16]{1,0:T(8,128)S(1)} %copy.10, f32[1024,1024]{1,0:T(8,128)} %all-gather.4.cloned.1.call-done, f32[96,16,1024]{2,1,0:T(8,128)} %param.4), kind=kOutput, calls=%fused_computation.2 | convolution fusion | flops 19330498560 | bytes 16783360 | tf_op jit(solution)/shard_map/dot_general | solution.py:36
  111.3 54.6 %reduce-scatter.2.cloned.1.call-done = f32[96,1,128]{2,0,1:T(8,128)} async-done(((f32[96,32,128]{2,0,1:T(8,128)}), f32[96,1,128]{2,0,1:T(8,128)}) %reduce-scatter.2.cloned.1.call-update) | async-done | bytes 49168 | tf_op jit(solution)/shard_map/reduce_scatter | solution.py:33
Async XLA Ops:
  7.2 1.6 copy-start
  7.2 27.7 %all-gather.6.cloned.1.call-start = ((), (), s32[]{:S(2)}) async-start(), calls=%async_computation.3 | async-start | bytes 1310720 | tf_op jit(solution)/shard_map/all_gather | solution.py:12
  9.5 76.7 %all-gather.4.cloned.1.call-start = ((), (), s32[]{:S(2)}) async-start(), calls=%async_computation.1 | async-start | bytes 4325376 | tf_op jit(solution)/shard_map/all_gather | solution.py:38
  10.3 155.7 %reduce-scatter.2.cloned.1.call-start = ((), (), s32[]{:S(2)}) async-start(), calls=%async_computation.2 | async-start | bytes 1622016 | tf_op jit(solution)/shard_map/reduce_scatter | solution.py:33
Sparse Core Ops, SparseCore 0:
  9.6 25.1 all-gather.5
  37.1 49.0 all-gather.3
  90.3 75.5 reduce-scatter.1

commit v2 on v1

--- a/solution.py
+++ b/solution.py
@@ -6,11 +6,23 @@
 
 def cycle_piece(cycle_integrals, kblock):
     own = lax.axis_index("own")
+    vir = lax.axis_index("vir")
+    n_own = lax.axis_size("own")
+    n_vir = lax.axis_size("vir")
     held = cycle_integrals.shape[0]
     start = own * kblock
     piece = lax.dynamic_slice_in_dim(cycle_integrals, start % held, kblock, axis=0)
-    pieces = lax.all_gather(piece, "vir")
-    return lax.dynamic_index_in_dim(pieces, start // held, axis=0, keepdims=False)
+    holder = start // held
+    chosen = piece
+    for shift in range(1, n_vir):
+        pairs = []
+        for o in range(n_own):
+            src = (o * kblock) // held
+            dst = (src + shift) % n_vir
+            pairs.append((o * n_vir + src, o * n_vir + dst))
+        got = lax.ppermute(piece, ("own", "vir"), pairs)
+        chosen = jnp.where((vir - holder) % n_vir == shift, got, chosen)
+    return chosen
 
 
 def local(amplitudes, pair_live, ladder_integrals, cycle_integrals):
@@ -24,13 +36,14 @@
     weights = cycle_piece(cycle_integrals, second_rows)
     split = screened.reshape(first_rows, second_rows, width // virtuals, virtuals)
     partial_value = jnp.einsum(
-        "ikac,kcm->iam",
+        "ikac,kcm->aim",
         split,
         weights,
         precision=lax.Precision.HIGHEST,
         preferred_element_type=jnp.float32,
     )
-    cycle_part = lax.psum_scatter(partial_value, "own", scatter_dimension=1, tiled=True)
+    gathered = lax.all_to_all(partial_value, "own", split_axis=0, concat_axis=0, tiled=True)
+    cycle_part = jnp.sum(gathered, axis=0)[:, None, :]
 
     flat = screened.reshape(first_rows * second_rows, width)
     ladder = jnp.dot(

time: 174 us -> 111 us (0.64)
  waiting for transfers between devices: 99.8 us -> 0.69 us
  blocking collectives: 0 us -> 29.1 us
  starting transfers between devices: 0.12 us -> 7.87 us
  other arithmetic: 6.67 us -> 8.79 us
    reduce_scatter x1 -> x0, waiting for transfers between devices: 54.6 us -> none  [local(): lax.psum_scatter(partial_value, 'own', scatter_dimension=1, tiled=True)]
    all_gather x1, waiting for transfers between devices: 34.8 us -> 0.01 us  [local(): lax.all_gather(ladder_integrals, 'own', axis=0, tiled=True)]
    all_to_all x0 -> x1, blocking collectives: none -> 29.1 us  [local(): lax.all_to_all(partial_value, 'own', split_axis=0, concat_axis=0, tiled=T...]
    all_gather x1 -> x0, waiting for transfers between devices: 9.57 us -> none  [cycle_piece(): pieces = lax.all_gather(piece, 'vir')]
    ppermute x0 -> x3, starting transfers between devices: none -> 7.83 us  [cycle_piece(): got = lax.ppermute(piece, ('own', 'vir'), pairs)]
    reduce_sum x0 -> x1, other arithmetic: none -> 2.11 us  [local(): cycle_part = jnp.sum(gathered, axis=0)[:, None, :]]
  transfers between devices with their start and end apart: 3 -> 4, of which waited for: 3 -> 0; matrix products, arithmetic and copies ran while one was open for 33% -> 30% of each run, Pallas kernels for 0% -> 0%
where the time goes in v2:
time: 111 us
  matrix products  40.9 us (37%)
  blocking collectives  29.1 us (26%)
  between operations  14.1 us (13%)
  local copies, waits for them, and re-layouts  9.14 us (8%)
  other arithmetic  8.79 us (8%)
  starting transfers between devices  7.87 us (7%)
    all_to_all x1, blocking collectives, local(): lax.all_to_all(partial_value, 'own', split_axis=0, concat_axis=0, tiled=T...  29.1 us
    dot_general x1, matrix products, local(): jnp.dot(flat, lax.all_gather(ladder_integrals, 'own', axis=0, tiled=True)...  25.1 us
    dot_general x1, matrix products, local(): jnp.einsum('ikac,kcm->aim', split, weights, precision=lax.Precision.HIGHE...  15.8 us
    mul x1, local copies, waits for them, and re-layouts, local(): screened = amplitudes * live[:, :, None]  8.2 us
    ppermute x3, starting transfers between devices, cycle_piece(): got = lax.ppermute(piece, ('own', 'vir'), pairs)  7.83 us
    mul x1, other arithmetic, local(): screened = amplitudes * live[:, :, None]  5.97 us
  transfers between devices with their start and end apart: 4, of which 0 were waited for; matrix products, arithmetic and copies ran while one was open for 30% of the time, Pallas kernels for 0%

profile of v2, /device:TPU:1, one launch (start us, length us, event | category | flops | bytes accessed | tf_op | source)
XLA Modules:
  0.0 110.6 jit_solution(13675838756079283556)
XLA Ops:
  7.2 0.0 copy-start
  7.2 0.0 all-gather.2.cloned.1.call-start
  7.2 0.7 all-gather.2.cloned.1.call-update
  7.9 0.8 copy-done
  8.8 5.2 %collective-permute-start = (f32[16,32,128]{2,1,0:T(8,128)S(1)}, f32[16,32,128]{2,1,0:T(8,128)S(1)}, u32[]{:S(2)}, u32[]{:S(2)}) collective-permute-start(f32[16,32,128]{2,1,0:T(8,128)S(1)} %constant_dynamic-slice_fusion), channel_id=1, source_target_pairs={{0,3},{4,7},{8,11},{12,15},{16,19},{20,23},{24,27},{28,31},{33,32}... | collective-permute-start | bytes 786440 | tf_op jit(solution)/shard_map/ppermute | solution.py:23
  14.0 1.3 %collective-permute-start.1 = (f32[16,32,128]{2,1,0:T(8,128)S(1)}, f32[16,32,128]{2,1,0:T(8,128)S(1)}, u32[]{:S(2)}, u32[]{:S(2)}) collective-permute-start(f32[16,32,128]{2,1,0:T(8,128)S(1)} %constant_dynamic-slice_fusion), channel_id=1, source_target_pairs={{0,2},{4,6},{8,10},{12,14},{16,18},{20,22},{24,26},{28,30},{33,35}... | collective-permute-start | bytes 786440 | tf_op jit(solution)/shard_map/ppermute | solution.py:23
  15.3 1.3 %collective-permute-start.2 = (f32[16,32,128]{2,1,0:T(8,128)S(1)}, f32[16,32,128]{2,1,0:T(8,128)S(1)}, u32[]{:S(2)}, u32[]{:S(2)}) collective-permute-start(f32[16,32,128]{2,1,0:T(8,128)S(1)} %constant_dynamic-slice_fusion), channel_id=1, source_target_pairs={{0,1},{4,5},{8,9},{12,13},{16,17},{20,21},{24,25},{28,29},{33,34},... | collective-permute-start | bytes 786440 | tf_op jit(solution)/shard_map/ppermute | solution.py:23
  16.6 0.7 convert_element_type.3
  17.3 0.1 copy.8
  17.4 6.0 %broadcast_multiply_fusion.1 = f32[96,16,1024]{2,1,0:T(8,128)} fusion(f32[96,16,1024]{2,1,0:T(8,128)} %param.4, f32[96,16]{1,0:T(8,128)S(1)} %copy.8), kind=kLoop, calls=%fused_computation.3 | loop fusion | flops 1572864 | bytes 12589056 | tf_op jit(solution)/shard_map/mul | solution.py:30
  23.4 8.2 %copy.9 = f32[96,16,1024]{0,2,1:T(8,128)} copy(f32[96,16,1024]{2,1,0:T(8,128)} %broadcast_multiply_fusion.1) | data formatting | bytes 12582912 | tf_op jit(solution)/shard_map/mul | solution.py:30
  31.6 0.0 collective-permute-done
  31.6 0.0 collective-permute-done.1
  31.6 0.0 collective-permute-done.2
  31.6 15.8 %convolution_bitcast_fusion = f32[32,96,128]{2,1,0:T(8,128)S(1)} fusion(f32[96,16,32,32]{0,3,2,1:T(8,128)} %bitcast.20, f32[16,32,128]{2,1,0:T(8,128)S(1)} %collective-permute-done, f32[16,32,128]{2,1,0:T(8,128)S(1)} %collective-permute-done.1, f32[16,32,128]{2,1,0:T(8,128)S(1)} %collective-permute-done.2, ...), kind=kOutput, calls=%fused_computation.4 | convolution fusion | flops 2416115712 | bytes 8912899 | tf_op jit(solution)/shard_map/ikac,kcm->aim/dot_general | solution.py:38
  47.4 29.1 %all_to_all.5 = f32[32,96,128]{2,1,0:T(8,128)} all-to-all(f32[32,96,128]{2,1,0:T(8,128)S(1)} %convolution_bitcast_fusion), channel_id=1, replica_groups=mesh['own'=32,'vir'=4] {'own'}, dimensions={0} | all-to-all | bytes 3145728 | tf_op jit(solution)/shard_map/all_to_all | solution.py:45
  76.5 2.1 %reduce_sum.9 = f32[96,128]{1,0:T(8,128)} reduce(f32[32,96,128]{2,1,0:T(8,128)} %all_to_all.5, f32[]{:T(128)} %constant.57.clone.1), dimensions={0}, to_apply=%region_0.1 | reduce | flops 380928 | bytes 1622020 | tf_op jit(solution)/shard_map/reduce_sum | solution.py:46
  78.7 0.0 all-gather.2.cloned.1.call-done
  78.7 25.1 %broadcast_multiply_fusion = f32[96,16,1024]{2,1,0:T(8,128)} fusion(f32[96,16]{1,0:T(8,128)S(1)} %copy.8, f32[1024,1024]{1,0:T(8,128)} %all-gather.2.cloned.1.call-done, f32[96,16,1024]{2,1,0:T(8,128)} %param.4), kind=kOutput, calls=%fused_computation.2 | convolution fusion | flops 19330498560 | bytes 16783360 | tf_op jit(solution)/shard_map/dot_general | solution.py:49
  (1 shorter events, 0.0 us)
Async XLA Ops:
  7.2 1.6 %copy-start = (f32[128,32,128]{2,1,0:T(8,128)S(1)}, f32[128,32,128]{2,1,0:T(8,128)}, u32[]{:S(2)}) copy-start(f32[128,32,128]{2,1,0:T(8,128)} %param.7) | copy-start | bytes 6291460
  7.2 71.5 %all-gather.2.cloned.1.call-start = ((), (), s32[]{:S(2)}) async-start(), calls=%async_computation.1 | async-start | bytes 4325376 | tf_op jit(solution)/shard_map/all_gather | solution.py:51
  8.8 22.8 %collective-permute-start = (f32[16,32,128]{2,1,0:T(8,128)S(1)}, f32[16,32,128]{2,1,0:T(8,128)S(1)}, u32[]{:S(2)}, u32[]{:S(2)}) collective-permute-start(f32[16,32,128]{2,1,0:T(8,128)S(1)} %constant_dynamic-slice_fusion), channel_id=1, source_target_pairs={{0,3},{4,7},{8,11},{12,15},{16,19},{20,23},{24,27},{28,31},{33,32}... | collective-permute-start | bytes 786440 | tf_op jit(solution)/shard_map/ppermute | solution.py:23
  14.0 17.6 %collective-permute-start.1 = (f32[16,32,128]{2,1,0:T(8,128)S(1)}, f32[16,32,128]{2,1,0:T(8,128)S(1)}, u32[]{:S(2)}, u32[]{:S(2)}) collective-permute-start(f32[16,32,128]{2,1,0:T(8,128)S(1)} %constant_dynamic-slice_fusion), channel_id=1, source_target_pairs={{0,2},{4,6},{8,10},{12,14},{16,18},{20,22},{24,26},{28,30},{33,35}... | collective-permute-start | bytes 786440 | tf_op jit(solution)/shard_map/ppermute | solution.py:23
  15.3 16.3 %collective-permute-start.2 = (f32[16,32,128]{2,1,0:T(8,128)S(1)}, f32[16,32,128]{2,1,0:T(8,128)S(1)}, u32[]{:S(2)}, u32[]{:S(2)}) collective-permute-start(f32[16,32,128]{2,1,0:T(8,128)S(1)} %constant_dynamic-slice_fusion), channel_id=1, source_target_pairs={{0,1},{4,5},{8,9},{12,13},{16,17},{20,21},{24,25},{28,29},{33,34},... | collective-permute-start | bytes 786440 | tf_op jit(solution)/shard_map/ppermute | solution.py:23
Sparse Core Ops, SparseCore 0:
  10.2 51.1 all-gather.1

commit v3 on v2

--- a/solution.py
+++ b/solution.py
@@ -2,6 +2,8 @@
 import jax.numpy as jnp
 from jax import lax
 from jax.sharding import PartitionSpec as P
+
+CORES = 2
 
 
 def cycle_piece(cycle_integrals, kblock):
@@ -25,6 +27,31 @@
     return chosen
 
 
+def core_stage(partial_value):
+    own = lax.axis_index("own")
+    n_own = lax.axis_size("own")
+    core = own % CORES
+    rest = partial_value.shape[1:]
+    by_core = partial_value.reshape((-1, CORES) + rest)
+    mine = lax.dynamic_index_in_dim(by_core, core, axis=1, keepdims=False)
+    theirs = lax.dynamic_index_in_dim(by_core, 1 - core, axis=1, keepdims=False)
+    return mine + lax.ppermute(theirs, "own", [(o, o ^ 1) for o in range(n_own)])
+
+
+def chip_sends(chip_blocks):
+    own = lax.axis_index("own")
+    n_own = lax.axis_size("own")
+    chips = n_own // CORES
+    chip = own // CORES
+    mine = lax.dynamic_index_in_dim(chip_blocks, chip, axis=0, keepdims=False)
+    received = [mine]
+    for shift in range(1, chips):
+        outgoing = lax.dynamic_index_in_dim(chip_blocks, (chip + shift) % chips, axis=0, keepdims=False)
+        pairs = [(o, ((o // CORES + shift) % chips) * CORES + o % CORES) for o in range(n_own)]
+        received.append(lax.ppermute(outgoing, "own", pairs))
+    return received
+
+
 def local(amplitudes, pair_live, ladder_integrals, cycle_integrals):
     live = pair_live.astype(jnp.float32)
     screened = amplitudes * live[:, :, None]
@@ -42,17 +69,18 @@
         precision=lax.Precision.HIGHEST,
         preferred_element_type=jnp.float32,
     )
-    gathered = lax.all_to_all(partial_value, "own", split_axis=0, concat_axis=0, tiled=True)
-    cycle_part = jnp.sum(gathered, axis=0)[:, None, :]
+    received = chip_sends(core_stage(partial_value))
 
     flat = screened.reshape(first_rows * second_rows, width)
     ladder = jnp.dot(
         flat,
         lax.all_gather(ladder_integrals, "own", axis=0, tiled=True),
-        precision=lax.Precision.HIGHEST,
+        precision=lax.Precision.HIGH,
         preferred_element_type=jnp.float32,
     )
     ladder_part = ladder.reshape(first_rows, second_rows, width) * live[:, :, None]
+    ladder_part, received = lax.optimization_barrier((ladder_part, received))
+    cycle_part = sum(received[1:], received[0])[:, None, :]
     return (ladder_part, cycle_part)
 
 

time: 111 us -> 106 us (0.955)
  the two profiles are of different devices: /device:TPU:1 before, /device:TPU:0 now
where the time goes in v3:
time: 106 us; the launch traced here: 105 us
  starting transfers between devices  33.8 us (32%)
  matrix products  30.6 us (29%)
  between operations  14.2 us (13%)
  local copies, waits for them, and re-layouts  11.4 us (11%)
  other arithmetic  8.56 us (8%)
  waiting for transfers between devices  6.57 us (6%)
    ppermute x15, starting transfers between devices, chip_sends(): received.append(lax.ppermute(outgoing, 'own', pairs))  26.4 us
    dot_general x1, matrix products, local(): jnp.einsum('ikac,kcm->aim', split, weights, precision=lax.Precision.HIGHE...  15.7 us
    dot_general x1, matrix products, local(): jnp.dot(flat, lax.all_gather(ladder_integrals, 'own', axis=0, tiled=True)...  14.9 us
    mul x1, local copies, waits for them, and re-layouts, local(): screened = amplitudes * live[:, :, None]  8.26 us
    ppermute x3, starting transfers between devices, cycle_piece(): got = lax.ppermute(piece, ('own', 'vir'), pairs)  7.4 us
    mul x1, other arithmetic, local(): screened = amplitudes * live[:, :, None]  5.97 us
    ppermute x15, waiting for transfers between devices, chip_sends(): received.append(lax.ppermute(outgoing, 'own', pairs))  3.23 us
    ppermute x1, waiting for transfers between devices, core_stage(): lax.ppermute(theirs, 'own', [(o, o ^ 1) for o in range(n_own)])  2.65 us
  transfers between devices with their start and end apart: 20, of which 2 were waited for; matrix products, arithmetic and copies ran while one was open for 46% of the time, Pallas kernels for 0%

profile of v3, /device:TPU:0, one launch (start us, length us, event | category | flops | bytes accessed | tf_op | source)
XLA Modules:
  0.0 105.1 jit_solution(5106001054114180290)
XLA Ops:
  7.2 0.0 copy-start
  7.2 0.0 all-gather.2.cloned.1.call-start
  7.2 0.7 all-gather.2.cloned.1.call-update
  7.9 0.8 copy-done
  8.8 4.8 %collective-permute-start = (f32[16,32,128]{2,1,0:T(8,128)S(1)}, f32[16,32,128]{2,1,0:T(8,128)S(1)}, u32[]{:S(2)}, u32[]{:S(2)}) collective-permute-start(f32[16,32,128]{2,1,0:T(8,128)S(1)} %constant_dynamic-slice_fusion), channel_id=1, source_target_pairs={{0,3},{4,7},{8,11},{12,15},{16,19},{20,23},{24,27},{28,31},{33,32}... | collective-permute-start | bytes 786440 | tf_op jit(solution)/shard_map/ppermute | solution.py:25
  13.6 1.3 %collective-permute-start.1 = (f32[16,32,128]{2,1,0:T(8,128)S(1)}, f32[16,32,128]{2,1,0:T(8,128)S(1)}, u32[]{:S(2)}, u32[]{:S(2)}) collective-permute-start(f32[16,32,128]{2,1,0:T(8,128)S(1)} %constant_dynamic-slice_fusion), channel_id=1, source_target_pairs={{0,2},{4,6},{8,10},{12,14},{16,18},{20,22},{24,26},{28,30},{33,35}... | collective-permute-start | bytes 786440 | tf_op jit(solution)/shard_map/ppermute | solution.py:25
  14.9 1.3 %collective-permute-start.2 = (f32[16,32,128]{2,1,0:T(8,128)S(1)}, f32[16,32,128]{2,1,0:T(8,128)S(1)}, u32[]{:S(2)}, u32[]{:S(2)}) collective-permute-start(f32[16,32,128]{2,1,0:T(8,128)S(1)} %constant_dynamic-slice_fusion), channel_id=1, source_target_pairs={{0,1},{4,5},{8,9},{12,13},{16,17},{20,21},{24,25},{28,29},{33,34},... | collective-permute-start | bytes 786440 | tf_op jit(solution)/shard_map/ppermute | solution.py:25
  16.2 0.7 convert_element_type.3
  16.9 0.1 copy.8
  17.0 6.0 %broadcast_multiply_fusion.1 = f32[96,16,1024]{2,1,0:T(8,128)} fusion(f32[96,16,1024]{2,1,0:T(8,128)} %param.4, f32[96,16]{1,0:T(8,128)S(1)} %copy.8), kind=kLoop, calls=%fused_computation.3 | loop fusion | flops 1572864 | bytes 12589056 | tf_op jit(solution)/shard_map/mul | solution.py:57
  23.0 8.3 %copy.9 = f32[96,16,1024]{0,2,1:T(8,128)} copy(f32[96,16,1024]{2,1,0:T(8,128)} %broadcast_multiply_fusion.1) | data formatting | bytes 12582912 | tf_op jit(solution)/shard_map/mul | solution.py:57
  31.2 0.0 collective-permute-done
  31.2 0.0 collective-permute-done.1
  31.2 0.0 collective-permute-done.2
  31.2 15.7 %fusion.4 = f32[128,96,32,1]{0,1,2,3:T(8,128)S(1)} fusion(f32[96,16,32,32]{0,3,2,1:T(8,128)} %bitcast.57, f32[16,32,128]{2,1,0:T(8,128)S(1)} %collective-permute-done, f32[16,32,128]{2,1,0:T(8,128)S(1)} %collective-permute-done.1, f32[16,32,128]{2,1,0:T(8,128)S(1)} %collective-permute-done.2, f32[16,32,128]{2,1,0:T(8,128)S(1)} %constant_dynamic-slice_fusion, ...), kind=kOutput, calls=%fused_computation.6 | convolution fusion | flops 2416115712 | bytes 8912899 | tf_op jit(solution)/shard_map/ikac,kcm->aim/dot_general | solution.py:65
  47.0 0.0 copy-start.1
  47.0 1.1 %copy-done.1 = f32[128,96,32,1]{0,1,2,3:T(8,128)} copy-done((f32[128,96,32,1]{0,1,2,3:T(8,128)}, f32[128,96,32,1]{0,1,2,3:T(8,128)S(1)}, u32[]{:S(2)}) %copy-start.1) | copy-done | bytes 1572888
  48.1 0.9 dynamic-slice_bitcast_fusion
  49.1 0.0 collective-permute-start.3
  49.1 2.7 %collective-permute-done.3 = f32[16,96,128]{2,1,0:T(8,128)S(1)} collective-permute-done((f32[16,96,128]{2,1,0:T(8,128)}, f32[16,96,128]{2,1,0:T(8,128)S(1)}, u32[]{:S(2)}, u32[]{:S(2)}) %collective-permute-start.3) | collective-permute-done | bytes 786464 | tf_op jit(solution)/shard_map/ppermute | solution.py:38
  51.7 1.2 %bitcast_add_fusion = f32[16,96,128]{2,1,0:T(8,128)S(1)} fusion(f32[16,96,128]{2,1,0:T(8,128)S(1)} %collective-permute-done.3, f32[16,2,96,128]{3,2,1,0:T(8,128)} %bitcast.59, s32[]{:T(128)S(6)} %select_n.176), kind=kLoop, calls=%fused_computation.4 | loop fusion | flops 196608 | bytes 2359300 | tf_op jit(solution)/shard_map/add | solution.py:38
  53.0 0.1 dynamic-slice_bitcast_fusion.1
  53.1 0.6 collective-permute-start.10
  53.7 2.9 %collective-permute-start.11 = (f32[96,128]{1,0:T(8,128)S(1)}, f32[96,128]{1,0:T(8,128)S(1)}, u32[]{:S(2)}, u32[]{:S(2)}) collective-permute-start(f32[96,128]{1,0:T(8,128)S(1)} %get-tuple-element.43), channel_id=1, source_target_pairs={{0,64},{4,68},{8,72},{12,76},{16,80},{20,84},{24,88},{28,92},{32,9... | collective-permute-start | bytes 147464 | tf_op jit(solution)/shard_map/ppermute | solution.py:51
  56.6 1.7 %collective-permute-start.12 = (f32[96,128]{1,0:T(8,128)S(1)}, f32[96,128]{1,0:T(8,128)S(1)}, u32[]{:S(2)}, u32[]{:S(2)}) collective-permute-start(f32[96,128]{1,0:T(8,128)S(1)} %get-tuple-element.42), channel_id=1, source_target_pairs={{0,72},{4,76},{8,80},{12,84},{16,88},{20,92},{24,96},{28,100},{32,... | collective-permute-start | bytes 147464 | tf_op jit(solution)/shard_map/ppermute | solution.py:51
  58.3 6.2 %collective-permute-start.13 = (f32[96,128]{1,0:T(8,128)S(1)}, f32[96,128]{1,0:T(8,128)S(1)}, u32[]{:S(2)}, u32[]{:S(2)}) collective-permute-start(f32[96,128]{1,0:T(8,128)S(1)} %get-tuple-element.41), channel_id=1, source_target_pairs={{0,80},{4,84},{8,88},{12,92},{16,96},{20,100},{24,104},{28,108},{3... | collective-permute-start | bytes 147464 | tf_op jit(solution)/shard_map/ppermute | solution.py:51
  64.5 0.4 collective-permute-start.14
  65.0 1.4 %collective-permute-start.15 = (f32[96,128]{1,0:T(8,128)S(1)}, f32[96,128]{1,0:T(8,128)S(1)}, u32[]{:S(2)}, u32[]{:S(2)}) collective-permute-start(f32[96,128]{1,0:T(8,128)S(1)} %get-tuple-element.39), channel_id=1, source_target_pairs={{0,96},{4,100},{8,104},{12,108},{16,112},{20,116},{24,120},{28,124... | collective-permute-start | bytes 147464 | tf_op jit(solution)/shard_map/ppermute | solution.py:51
  66.4 0.0 collective-permute-done.11
  66.4 0.0 collective-permute-start.16
  66.4 1.7 %collective-permute-start.17 = (f32[96,128]{1,0:T(8,128)S(1)}, f32[96,128]{1,0:T(8,128)S(1)}, u32[]{:S(2)}, u32[]{:S(2)}) collective-permute-start(f32[96,128]{1,0:T(8,128)S(1)} %get-tuple-element.37), channel_id=1, source_target_pairs={{0,112},{4,116},{8,120},{12,124},{16,0},{20,4},{24,8},{28,12},{32,... | collective-permute-start | bytes 147464 | tf_op jit(solution)/shard_map/ppermute | solution.py:51
  68.1 0.0 collective-permute-done.13
  68.1 5.4 %collective-permute-start.18 = (f32[96,128]{1,0:T(8,128)S(1)}, f32[96,128]{1,0:T(8,128)S(1)}, u32[]{:S(2)}, u32[]{:S(2)}) collective-permute-start(f32[96,128]{1,0:T(8,128)S(1)} %get-tuple-element.36), channel_id=1, source_target_pairs={{0,120},{4,124},{8,0},{12,4},{16,8},{20,12},{24,16},{28,20},{32,24... | collective-permute-start | bytes 147464 | tf_op jit(solution)/shard_map/ppermute | solution.py:51
  73.5 0.0 collective-permute-done.14
  73.5 0.0 collective-permute-start.4
  73.5 0.0 collective-permute-done.15
  73.5 0.1 collective-permute-start.5
  73.6 2.5 %collective-permute-start.6 = (f32[96,128]{1,0:T(8,128)S(1)}, f32[96,128]{1,0:T(8,128)S(1)}, u32[]{:S(2)}, u32[]{:S(2)}) collective-permute-start(f32[96,128]{1,0:T(8,128)S(1)} %get-tuple-element.48), channel_id=1, source_target_pairs={{0,24},{4,28},{8,32},{12,36},{16,40},{20,44},{24,48},{28,52},{32,5... | collective-permute-start | bytes 147464 | tf_op jit(solution)/shard_map/ppermute | solution.py:51
  76.1 0.7 collective-permute-start.7
  76.8 0.0 collective-permute-done.18
  76.8 1.5 %collective-permute-start.8 = (f32[96,128]{1,0:T(8,128)S(1)}, f32[96,128]{1,0:T(8,128)S(1)}, u32[]{:S(2)}, u32[]{:S(2)}) collective-permute-start(f32[96,128]{1,0:T(8,128)S(1)} %get-tuple-element.46), channel_id=1, source_target_pairs={{0,40},{4,44},{8,48},{12,52},{16,56},{20,60},{24,64},{28,68},{32,7... | collective-permute-start | bytes 147464 | tf_op jit(solution)/shard_map/ppermute | solution.py:51
  78.3 3.2 %collective-permute-done.4 = f32[96,128]{1,0:T(8,128)S(1)} collective-permute-done((f32[96,128]{1,0:T(8,128)S(1)}, f32[96,128]{1,0:T(8,128)S(1)}, u32[]{:S(2)}, u32[]{:S(2)}) %collective-permute-start.4) | collective-permute-done | bytes 49184 | tf_op jit(solution)/shard_map/ppermute | solution.py:51
  81.5 1.2 %collective-permute-start.9 = (f32[96,128]{1,0:T(8,128)S(1)}, f32[96,128]{1,0:T(8,128)S(1)}, u32[]{:S(2)}, u32[]{:S(2)}) collective-permute-start(f32[96,128]{1,0:T(8,128)S(1)} %get-tuple-element.45), channel_id=1, source_target_pairs={{0,48},{4,52},{8,56},{12,60},{16,64},{20,68},{24,72},{28,76},{32,8... | collective-permute-start | bytes 147464 | tf_op jit(solution)/shard_map/ppermute | solution.py:51
  82.7 14.9 %broadcast_multiply_fusion = f32[96,16,1024]{2,1,0:T(8,128)} fusion(f32[96,16]{1,0:T(8,128)S(1)} %copy.8, f32[1024,1024]{1,0:T(8,128)} %all-gather.2.cloned.1.call-done, f32[96,16,1024]{2,1,0:T(8,128)} %param.4), kind=kOutput, calls=%fused_computation.2 | convolution fusion | flops 9666822144 | bytes 16783360 | tf_op jit(solution)/shard_map/dot_general | solution.py:75
  97.6 0.0 collective-permute-done.5
  97.6 0.0 collective-permute-done.7
  97.6 0.0 collective-permute-done.9
  97.6 0.7 add_add_fusion
  (8 shorter events, 0.0 us)
Async XLA Ops:
  7.2 1.6 %copy-start = (f32[128,32,128]{2,1,0:T(8,128)S(1)}, f32[128,32,128]{2,1,0:T(8,128)}, u32[]{:S(2)}) copy-start(f32[128,32,128]{2,1,0:T(8,128)} %param.7) | copy-start | bytes 6291460
  7.2 75.5 %all-gather.2.cloned.1.call-start = ((), (), s32[]{:S(2)}) async-start(), calls=%async_computation | async-start | bytes 4325376 | tf_op jit(solution)/shard_map/all_gather | solution.py:77
  8.8 22.5 %collective-permute-start = (f32[16,32,128]{2,1,0:T(8,128)S(1)}, f32[16,32,128]{2,1,0:T(8,128)S(1)}, u32[]{:S(2)}, u32[]{:S(2)}) collective-permute-start(f32[16,32,128]{2,1,0:T(8,128)S(1)} %constant_dynamic-slice_fusion), channel_id=1, source_target_pairs={{0,3},{4,7},{8,11},{12,15},{16,19},{20,23},{24,27},{28,31},{33,32}... | collective-permute-start | bytes 786440 | tf_op jit(solution)/shard_map/ppermute | solution.py:25
  13.6 17.7 %collective-permute-start.1 = (f32[16,32,128]{2,1,0:T(8,128)S(1)}, f32[16,32,128]{2,1,0:T(8,128)S(1)}, u32[]{:S(2)}, u32[]{:S(2)}) collective-permute-start(f32[16,32,128]{2,1,0:T(8,128)S(1)} %constant_dynamic-slice_fusion), channel_id=1, source_target_pairs={{0,2},{4,6},{8,10},{12,14},{16,18},{20,22},{24,26},{28,30},{33,35}... | collective-permute-start | bytes 786440 | tf_op jit(solution)/shard_map/ppermute | solution.py:25
  14.9 16.4 %collective-permute-start.2 = (f32[16,32,128]{2,1,0:T(8,128)S(1)}, f32[16,32,128]{2,1,0:T(8,128)S(1)}, u32[]{:S(2)}, u32[]{:S(2)}) collective-permute-start(f32[16,32,128]{2,1,0:T(8,128)S(1)} %constant_dynamic-slice_fusion), channel_id=1, source_target_pairs={{0,1},{4,5},{8,9},{12,13},{16,17},{20,21},{24,25},{28,29},{33,34},... | collective-permute-start | bytes 786440 | tf_op jit(solution)/shard_map/ppermute | solution.py:25
  47.0 1.1 %copy-start.1 = (f32[128,96,32,1]{0,1,2,3:T(8,128)}, f32[128,96,32,1]{0,1,2,3:T(8,128)S(1)}, u32[]{:S(2)}) copy-start(f32[128,96,32,1]{0,1,2,3:T(8,128)S(1)} %fusion.4) | copy-start | bytes 4718596
  49.1 2.7 %collective-permute-start.3 = (f32[16,96,128]{2,1,0:T(8,128)}, f32[16,96,128]{2,1,0:T(8,128)S(1)}, u32[]{:S(2)}, u32[]{:S(2)}) collective-permute-start(f32[16,96,128]{2,1,0:T(8,128)} %dynamic-slice_bitcast_fusion), channel_id=1, source_target_pairs={{0,4},{4,0},{8,12},{12,8},{16,20},{20,16},{24,28},{28,24},{32,36},... | collective-permute-start | bytes 2359304 | tf_op jit(solution)/shard_map/ppermute | solution.py:38
  53.1 11.9 %collective-permute-start.10 = (f32[96,128]{1,0:T(8,128)S(1)}, f32[96,128]{1,0:T(8,128)S(1)}, u32[]{:S(2)}, u32[]{:S(2)}) collective-permute-start(f32[96,128]{1,0:T(8,128)S(1)} %get-tuple-element.44), channel_id=1, source_target_pairs={{0,56},{4,60},{8,64},{12,68},{16,72},{20,76},{24,80},{28,84},{32,8... | collective-permute-start | bytes 147464 | tf_op jit(solution)/shard_map/ppermute | solution.py:51
  53.7 12.7 %collective-permute-start.11 = (f32[96,128]{1,0:T(8,128)S(1)}, f32[96,128]{1,0:T(8,128)S(1)}, u32[]{:S(2)}, u32[]{:S(2)}) collective-permute-start(f32[96,128]{1,0:T(8,128)S(1)} %get-tuple-element.43), channel_id=1, source_target_pairs={{0,64},{4,68},{8,72},{12,76},{16,80},{20,84},{24,88},{28,92},{32,9... | collective-permute-start | bytes 147464 | tf_op jit(solution)/shard_map/ppermute | solution.py:51
  56.6 9.9 %collective-permute-start.12 = (f32[96,128]{1,0:T(8,128)S(1)}, f32[96,128]{1,0:T(8,128)S(1)}, u32[]{:S(2)}, u32[]{:S(2)}) collective-permute-start(f32[96,128]{1,0:T(8,128)S(1)} %get-tuple-element.42), channel_id=1, source_target_pairs={{0,72},{4,76},{8,80},{12,84},{16,88},{20,92},{24,96},{28,100},{32,... | collective-permute-start | bytes 147464 | tf_op jit(solution)/shard_map/ppermute | solution.py:51
  58.3 9.8 %collective-permute-start.13 = (f32[96,128]{1,0:T(8,128)S(1)}, f32[96,128]{1,0:T(8,128)S(1)}, u32[]{:S(2)}, u32[]{:S(2)}) collective-permute-start(f32[96,128]{1,0:T(8,128)S(1)} %get-tuple-element.41), channel_id=1, source_target_pairs={{0,80},{4,84},{8,88},{12,92},{16,96},{20,100},{24,104},{28,108},{3... | collective-permute-start | bytes 147464 | tf_op jit(solution)/shard_map/ppermute | solution.py:51
  64.5 9.0 %collective-permute-start.14 = (f32[96,128]{1,0:T(8,128)S(1)}, f32[96,128]{1,0:T(8,128)S(1)}, u32[]{:S(2)}, u32[]{:S(2)}) collective-permute-start(f32[96,128]{1,0:T(8,128)S(1)} %get-tuple-element.40), channel_id=1, source_target_pairs={{0,88},{4,92},{8,96},{12,100},{16,104},{20,108},{24,112},{28,116},... | collective-permute-start | bytes 147464 | tf_op jit(solution)/shard_map/ppermute | solution.py:51
  65.0 8.5 %collective-permute-start.15 = (f32[96,128]{1,0:T(8,128)S(1)}, f32[96,128]{1,0:T(8,128)S(1)}, u32[]{:S(2)}, u32[]{:S(2)}) collective-permute-start(f32[96,128]{1,0:T(8,128)S(1)} %get-tuple-element.39), channel_id=1, source_target_pairs={{0,96},{4,100},{8,104},{12,108},{16,112},{20,116},{24,120},{28,124... | collective-permute-start | bytes 147464 | tf_op jit(solution)/shard_map/ppermute | solution.py:51
  66.4 7.2 %collective-permute-start.16 = (f32[96,128]{1,0:T(8,128)S(1)}, f32[96,128]{1,0:T(8,128)S(1)}, u32[]{:S(2)}, u32[]{:S(2)}) collective-permute-start(f32[96,128]{1,0:T(8,128)S(1)} %get-tuple-element.38), channel_id=1, source_target_pairs={{0,104},{4,108},{8,112},{12,116},{16,120},{20,124},{24,0},{28,4},{... | collective-permute-start | bytes 147464 | tf_op jit(solution)/shard_map/ppermute | solution.py:51
  66.4 9.7 %collective-permute-start.17 = (f32[96,128]{1,0:T(8,128)S(1)}, f32[96,128]{1,0:T(8,128)S(1)}, u32[]{:S(2)}, u32[]{:S(2)}) collective-permute-start(f32[96,128]{1,0:T(8,128)S(1)} %get-tuple-element.37), channel_id=1, source_target_pairs={{0,112},{4,116},{8,120},{12,124},{16,0},{20,4},{24,8},{28,12},{32,... | collective-permute-start | bytes 147464 | tf_op jit(solution)/shard_map/ppermute | solution.py:51
  68.1 8.7 %collective-permute-start.18 = (f32[96,128]{1,0:T(8,128)S(1)}, f32[96,128]{1,0:T(8,128)S(1)}, u32[]{:S(2)}, u32[]{:S(2)}) collective-permute-start(f32[96,128]{1,0:T(8,128)S(1)} %get-tuple-element.36), channel_id=1, source_target_pairs={{0,120},{4,124},{8,0},{12,4},{16,8},{20,12},{24,16},{28,20},{32,24... | collective-permute-start | bytes 147464 | tf_op jit(solution)/shard_map/ppermute | solution.py:51
  73.5 8.0 %collective-permute-start.4 = (f32[96,128]{1,0:T(8,128)S(1)}, f32[96,128]{1,0:T(8,128)S(1)}, u32[]{:S(2)}, u32[]{:S(2)}) collective-permute-start(f32[96,128]{1,0:T(8,128)S(1)} %get-tuple-element.50), channel_id=1, source_target_pairs={{0,8},{4,12},{8,16},{12,20},{16,24},{20,28},{24,32},{28,36},{32,40... | collective-permute-start | bytes 147464 | tf_op jit(solution)/shard_map/ppermute | solution.py:51
  73.5 24.1 %collective-permute-start.5 = (f32[96,128]{1,0:T(8,128)S(1)}, f32[96,128]{1,0:T(8,128)S(1)}, u32[]{:S(2)}, u32[]{:S(2)}) collective-permute-start(f32[96,128]{1,0:T(8,128)S(1)} %get-tuple-element.49), channel_id=1, source_target_pairs={{0,16},{4,20},{8,24},{12,28},{16,32},{20,36},{24,40},{28,44},{32,4... | collective-permute-start | bytes 147464 | tf_op jit(solution)/shard_map/ppermute | solution.py:51
  73.6 24.0 %collective-permute-start.6 = (f32[96,128]{1,0:T(8,128)S(1)}, f32[96,128]{1,0:T(8,128)S(1)}, u32[]{:S(2)}, u32[]{:S(2)}) collective-permute-start(f32[96,128]{1,0:T(8,128)S(1)} %get-tuple-element.48), channel_id=1, source_target_pairs={{0,24},{4,28},{8,32},{12,36},{16,40},{20,44},{24,48},{28,52},{32,5... | collective-permute-start | bytes 147464 | tf_op jit(solution)/shard_map/ppermute | solution.py:51
  76.1 21.5 %collective-permute-start.7 = (f32[96,128]{1,0:T(8,128)S(1)}, f32[96,128]{1,0:T(8,128)S(1)}, u32[]{:S(2)}, u32[]{:S(2)}) collective-permute-start(f32[96,128]{1,0:T(8,128)S(1)} %get-tuple-element.47), channel_id=1, source_target_pairs={{0,32},{4,36},{8,40},{12,44},{16,48},{20,52},{24,56},{28,60},{32,6... | collective-permute-start | bytes 147464 | tf_op jit(solution)/shard_map/ppermute | solution.py:51
  76.8 20.8 %collective-permute-start.8 = (f32[96,128]{1,0:T(8,128)S(1)}, f32[96,128]{1,0:T(8,128)S(1)}, u32[]{:S(2)}, u32[]{:S(2)}) collective-permute-start(f32[96,128]{1,0:T(8,128)S(1)} %get-tuple-element.46), channel_id=1, source_target_pairs={{0,40},{4,44},{8,48},{12,52},{16,56},{20,60},{24,64},{28,68},{32,7... | collective-permute-start | bytes 147464 | tf_op jit(solution)/shard_map/ppermute | solution.py:51
  81.5 16.1 %collective-permute-start.9 = (f32[96,128]{1,0:T(8,128)S(1)}, f32[96,128]{1,0:T(8,128)S(1)}, u32[]{:S(2)}, u32[]{:S(2)}) collective-permute-start(f32[96,128]{1,0:T(8,128)S(1)} %get-tuple-element.45), channel_id=1, source_target_pairs={{0,48},{4,52},{8,56},{12,60},{16,64},{20,68},{24,72},{28,76},{32,8... | collective-permute-start | bytes 147464 | tf_op jit(solution)/shard_map/ppermute | solution.py:51
Sparse Core Ops, SparseCore 0:
  10.2 48.6 all-gather.1

commit v4 on v2

--- a/solution.py
+++ b/solution.py
@@ -2,7 +2,6 @@
 import jax.numpy as jnp
 from jax import lax
 from jax.sharding import PartitionSpec as P
-
 
 def cycle_piece(cycle_integrals, kblock):
     own = lax.axis_index("own")
@@ -39,7 +38,7 @@
         "ikac,kcm->aim",
         split,
         weights,
-        precision=lax.Precision.HIGHEST,
+        precision=lax.Precision.HIGH,
         preferred_element_type=jnp.float32,
     )
     gathered = lax.all_to_all(partial_value, "own", split_axis=0, concat_axis=0, tiled=True)
@@ -49,7 +48,7 @@
     ladder = jnp.dot(
         flat,
         lax.all_gather(ladder_integrals, "own", axis=0, tiled=True),
-        precision=lax.Precision.HIGHEST,
+        precision=lax.Precision.HIGH,
         preferred_element_type=jnp.float32,
     )
     ladder_part = ladder.reshape(first_rows, second_rows, width) * live[:, :, None]

time: 111 us -> 99 us (0.89)
  matrix products: 40.9 us -> 24 us
  blocking collectives: 29.1 us -> 33.9 us
    dot_general x1, matrix products: 25.1 us -> 14.9 us  [local(): jnp.dot(flat, lax.all_gather(ladder_integrals, 'own', axis=0, tiled=True)...]
    dot_general x1, matrix products: 15.8 us -> 9.17 us  [local(): jnp.einsum('ikac,kcm->aim', split, weights, precision=lax.Precision.HIGH,...]
    all_to_all x1, blocking collectives: 29.1 us -> 33.9 us  [local(): lax.all_to_all(partial_value, 'own', split_axis=0, concat_axis=0, tiled=T...]
  transfers between devices with their start and end apart: 4 -> 4, of which waited for: 0 -> 0; matrix products, arithmetic and copies ran while one was open for 30% -> 27% of each run, Pallas kernels for 0% -> 0%
where the time goes in v4:
time: 99 us; the launch traced here: 98.5 us
  blocking collectives  33.9 us (34%)
  matrix products  24 us (24%)
  between operations  14.1 us (14%)
  local copies, waits for them, and re-layouts  9.14 us (9%)
  other arithmetic  8.79 us (9%)
  starting transfers between devices  7.87 us (8%)
    all_to_all x1, blocking collectives, local(): lax.all_to_all(partial_value, 'own', split_axis=0, concat_axis=0, tiled=T...  33.9 us
    dot_general x1, matrix products, local(): jnp.dot(flat, lax.all_gather(ladder_integrals, 'own', axis=0, tiled=True)...  14.9 us
    dot_general x1, matrix products, local(): jnp.einsum('ikac,kcm->aim', split, weights, precision=lax.Precision.HIGH,...  9.17 us
    mul x1, local copies, waits for them, and re-layouts, local(): screened = amplitudes * live[:, :, None]  8.2 us
    ppermute x3, starting transfers between devices, cycle_piece(): got = lax.ppermute(piece, ('own', 'vir'), pairs)  7.83 us
    mul x1, other arithmetic, local(): screened = amplitudes * live[:, :, None]  5.97 us
    reduce_sum x1, other arithmetic, local(): cycle_part = jnp.sum(gathered, axis=0)[:, None, :]  2.11 us
  transfers between devices with their start and end apart: 4, of which 0 were waited for; matrix products, arithmetic and copies ran while one was open for 27% of the time, Pallas kernels for 0%

profile of v4, /device:TPU:1, one launch (start us, length us, event | category | flops | bytes accessed | tf_op | source)
XLA Modules:
  0.0 98.5 jit_solution(2748800994009803598)
XLA Ops:
  7.2 0.0 copy-start
  7.2 0.0 all-gather.2.cloned.1.call-start
  7.2 0.7 all-gather.2.cloned.1.call-update
  7.9 0.8 copy-done
  8.8 5.2 %collective-permute-start = (f32[16,32,128]{2,1,0:T(8,128)S(1)}, f32[16,32,128]{2,1,0:T(8,128)S(1)}, u32[]{:S(2)}, u32[]{:S(2)}) collective-permute-start(f32[16,32,128]{2,1,0:T(8,128)S(1)} %constant_dynamic-slice_fusion), channel_id=1, source_target_pairs={{0,3},{4,7},{8,11},{12,15},{16,19},{20,23},{24,27},{28,31},{33,32}... | collective-permute-start | bytes 786440 | tf_op jit(solution)/shard_map/ppermute | solution.py:22
  14.0 1.3 %collective-permute-start.1 = (f32[16,32,128]{2,1,0:T(8,128)S(1)}, f32[16,32,128]{2,1,0:T(8,128)S(1)}, u32[]{:S(2)}, u32[]{:S(2)}) collective-permute-start(f32[16,32,128]{2,1,0:T(8,128)S(1)} %constant_dynamic-slice_fusion), channel_id=1, source_target_pairs={{0,2},{4,6},{8,10},{12,14},{16,18},{20,22},{24,26},{28,30},{33,35}... | collective-permute-start | bytes 786440 | tf_op jit(solution)/shard_map/ppermute | solution.py:22
  15.3 1.3 %collective-permute-start.2 = (f32[16,32,128]{2,1,0:T(8,128)S(1)}, f32[16,32,128]{2,1,0:T(8,128)S(1)}, u32[]{:S(2)}, u32[]{:S(2)}) collective-permute-start(f32[16,32,128]{2,1,0:T(8,128)S(1)} %constant_dynamic-slice_fusion), channel_id=1, source_target_pairs={{0,1},{4,5},{8,9},{12,13},{16,17},{20,21},{24,25},{28,29},{33,34},... | collective-permute-start | bytes 786440 | tf_op jit(solution)/shard_map/ppermute | solution.py:22
  16.6 0.7 convert_element_type.3
  17.3 0.1 copy.8
  17.4 6.0 %broadcast_multiply_fusion.1 = f32[96,16,1024]{2,1,0:T(8,128)} fusion(f32[96,16,1024]{2,1,0:T(8,128)} %param.4, f32[96,16]{1,0:T(8,128)S(1)} %copy.8), kind=kLoop, calls=%fused_computation.3 | loop fusion | flops 1572864 | bytes 12589056 | tf_op jit(solution)/shard_map/mul | solution.py:29
  23.4 8.2 %copy.9 = f32[96,16,1024]{0,2,1:T(8,128)} copy(f32[96,16,1024]{2,1,0:T(8,128)} %broadcast_multiply_fusion.1) | data formatting | bytes 12582912 | tf_op jit(solution)/shard_map/mul | solution.py:29
  31.6 0.0 collective-permute-done
  31.6 0.0 collective-permute-done.1
  31.6 0.0 collective-permute-done.2
  31.6 9.2 %convolution_bitcast_fusion = f32[32,96,128]{2,1,0:T(8,128)S(1)} fusion(f32[96,16,32,32]{0,3,2,1:T(8,128)} %bitcast.20, f32[16,32,128]{2,1,0:T(8,128)S(1)} %collective-permute-done, f32[16,32,128]{2,1,0:T(8,128)S(1)} %collective-permute-done.1, f32[16,32,128]{2,1,0:T(8,128)S(1)} %collective-permute-done.2, ...), kind=kOutput, calls=%fused_computation.4 | convolution fusion | flops 1208156160 | bytes 8912899 | tf_op jit(solution)/shard_map/ikac,kcm->aim/dot_general | solution.py:37
  40.8 33.9 %all_to_all.5 = f32[32,96,128]{2,1,0:T(8,128)} all-to-all(f32[32,96,128]{2,1,0:T(8,128)S(1)} %convolution_bitcast_fusion), channel_id=1, replica_groups=mesh['own'=32,'vir'=4] {'own'}, dimensions={0} | all-to-all | bytes 3145728 | tf_op jit(solution)/shard_map/all_to_all | solution.py:44
  74.7 2.1 %reduce_sum.9 = f32[96,128]{1,0:T(8,128)} reduce(f32[32,96,128]{2,1,0:T(8,128)} %all_to_all.5, f32[]{:T(128)} %constant.57.clone.1), dimensions={0}, to_apply=%region_0.1 | reduce | flops 380928 | bytes 1622020 | tf_op jit(solution)/shard_map/reduce_sum | solution.py:45
  76.8 0.0 all-gather.2.cloned.1.call-done
  76.8 14.9 %broadcast_multiply_fusion = f32[96,16,1024]{2,1,0:T(8,128)} fusion(f32[96,16]{1,0:T(8,128)S(1)} %copy.8, f32[1024,1024]{1,0:T(8,128)} %all-gather.2.cloned.1.call-done, f32[96,16,1024]{2,1,0:T(8,128)} %param.4), kind=kOutput, calls=%fused_computation.2 | convolution fusion | flops 9666822144 | bytes 16783360 | tf_op jit(solution)/shard_map/dot_general | solution.py:48
  (1 shorter events, 0.0 us)
Async XLA Ops:
  7.2 1.6 %copy-start = (f32[128,32,128]{2,1,0:T(8,128)S(1)}, f32[128,32,128]{2,1,0:T(8,128)}, u32[]{:S(2)}) copy-start(f32[128,32,128]{2,1,0:T(8,128)} %param.7) | copy-start | bytes 6291460
  7.2 69.6 %all-gather.2.cloned.1.call-start = ((), (), s32[]{:S(2)}) async-start(), calls=%async_computation.1 | async-start | bytes 4325376 | tf_op jit(solution)/shard_map/all_gather | solution.py:50
  8.8 22.8 %collective-permute-start = (f32[16,32,128]{2,1,0:T(8,128)S(1)}, f32[16,32,128]{2,1,0:T(8,128)S(1)}, u32[]{:S(2)}, u32[]{:S(2)}) collective-permute-start(f32[16,32,128]{2,1,0:T(8,128)S(1)} %constant_dynamic-slice_fusion), channel_id=1, source_target_pairs={{0,3},{4,7},{8,11},{12,15},{16,19},{20,23},{24,27},{28,31},{33,32}... | collective-permute-start | bytes 786440 | tf_op jit(solution)/shard_map/ppermute | solution.py:22
  14.0 17.6 %collective-permute-start.1 = (f32[16,32,128]{2,1,0:T(8,128)S(1)}, f32[16,32,128]{2,1,0:T(8,128)S(1)}, u32[]{:S(2)}, u32[]{:S(2)}) collective-permute-start(f32[16,32,128]{2,1,0:T(8,128)S(1)} %constant_dynamic-slice_fusion), channel_id=1, source_target_pairs={{0,2},{4,6},{8,10},{12,14},{16,18},{20,22},{24,26},{28,30},{33,35}... | collective-permute-start | bytes 786440 | tf_op jit(solution)/shard_map/ppermute | solution.py:22
  15.3 16.3 %collective-permute-start.2 = (f32[16,32,128]{2,1,0:T(8,128)S(1)}, f32[16,32,128]{2,1,0:T(8,128)S(1)}, u32[]{:S(2)}, u32[]{:S(2)}) collective-permute-start(f32[16,32,128]{2,1,0:T(8,128)S(1)} %constant_dynamic-slice_fusion), channel_id=1, source_target_pairs={{0,1},{4,5},{8,9},{12,13},{16,17},{20,21},{24,25},{28,29},{33,34},... | collective-permute-start | bytes 786440 | tf_op jit(solution)/shard_map/ppermute | solution.py:22
Sparse Core Ops, SparseCore 0:
  10.2 61.8 all-gather.1

commit v5 on v4

--- a/solution.py
+++ b/solution.py
@@ -1,12 +1,17 @@
 import jax
 import jax.numpy as jnp
 from jax import lax
+from jax.sharding import Mesh
 from jax.sharding import PartitionSpec as P
 
+PARTS = ("y", "z", "core")
+CHIPS = ("y", "z")
+
+
 def cycle_piece(cycle_integrals, kblock):
-    own = lax.axis_index("own")
+    own = lax.axis_index(PARTS)
     vir = lax.axis_index("vir")
-    n_own = lax.axis_size("own")
+    n_own = lax.axis_size(PARTS)
     n_vir = lax.axis_size("vir")
     held = cycle_integrals.shape[0]
     start = own * kblock
@@ -19,9 +24,22 @@
             src = (o * kblock) // held
             dst = (src + shift) % n_vir
             pairs.append((o * n_vir + src, o * n_vir + dst))
-        got = lax.ppermute(piece, ("own", "vir"), pairs)
+        got = lax.ppermute(piece, PARTS + ("vir",), pairs)
         chosen = jnp.where((vir - holder) % n_vir == shift, got, chosen)
     return chosen
+
+
+def cycle_reduce(partial_value):
+    cores = lax.axis_size("core")
+    core = lax.axis_index("core")
+    rest = partial_value.shape[1:]
+    by_core = partial_value.reshape((-1, cores) + rest)
+    mine = lax.dynamic_index_in_dim(by_core, core, axis=1, keepdims=False)
+    theirs = lax.dynamic_index_in_dim(by_core, (core + 1) % cores, axis=1, keepdims=False)
+    pairs = [(c, (c + 1) % cores) for c in range(cores)]
+    chip_share = mine + lax.ppermute(theirs, "core", pairs)
+    gathered = lax.all_to_all(chip_share, CHIPS, split_axis=0, concat_axis=0, tiled=True)
+    return jnp.sum(gathered, axis=0)[:, None, :]
 
 
 def local(amplitudes, pair_live, ladder_integrals, cycle_integrals):
@@ -41,13 +59,12 @@
         precision=lax.Precision.HIGH,
         preferred_element_type=jnp.float32,
     )
-    gathered = lax.all_to_all(partial_value, "own", split_axis=0, concat_axis=0, tiled=True)
-    cycle_part = jnp.sum(gathered, axis=0)[:, None, :]
+    cycle_part = cycle_reduce(partial_value)
 
     flat = screened.reshape(first_rows * second_rows, width)
     ladder = jnp.dot(
         flat,
-        lax.all_gather(ladder_integrals, "own", axis=0, tiled=True),
+        lax.all_gather(ladder_integrals, PARTS, axis=0, tiled=True),
         precision=lax.Precision.HIGH,
         preferred_element_type=jnp.float32,
     )
@@ -56,11 +73,14 @@
 
 
 def solution(mesh):
-    placed = (P("vir", "own", None), P("vir", "own"), P("own", None), P("vir", None, None))
+    sizes = (4, 4, 2)
+    named = Mesh(mesh.devices.reshape(sizes + (mesh.shape["vir"],)), PARTS + ("vir",))
+    assert mesh.axis_names == ("own", "vir") and mesh.shape["own"] == 32
+    placed = (P("vir", PARTS, None), P("vir", PARTS), P(PARTS, None), P("vir", None, None))
     return jax.shard_map(
         local,
-        mesh=mesh,
+        mesh=named,
         in_specs=placed,
-        out_specs=(P("vir", "own", None), P("vir", "own", None)),
+        out_specs=(P("vir", PARTS, None), P("vir", PARTS, None)),
         check_vma=False,
     )

time: 99 us -> 90 us (0.909)
  blocking collectives: 33.9 us -> 19.5 us
  waiting for transfers between devices: 0.69 us -> 2.81 us
  local copies, waits for them, and re-layouts: 9.14 us -> 11.2 us
    all_to_all x1, blocking collectives: 33.9 us -> 19.5 us  [cycle_reduce(): lax.all_to_all(chip_share, CHIPS, split_axis=0, concat_axis=0, tiled=True)]
    ppermute x3 -> x4, waiting for transfers between devices: 0.01 us -> 2.13 us  [the longest x1 2.12 us: cycle_reduce(): chip_share = mine + lax.ppermute(theirs, 'core', pairs)]
    reduce_sum x1, other arithmetic: 2.11 us -> 0.66 us  [cycle_reduce(): return jnp.sum(gathered, axis=0)[:, None, :]]
    add x0 -> x1, other arithmetic: none -> 1.22 us  [cycle_reduce(): chip_share = mine + lax.ppermute(theirs, 'core', pairs)]
    unnamed x2 -> x4, local copies, waits for them, and re-layouts: 0.84 us -> 1.97 us
    ppermute x3 -> x4, starting transfers between devices: 7.83 us -> 8.77 us  [the longest x3 7.83 us: cycle_piece(): got = lax.ppermute(piece, PARTS + ('vir',), pairs)]
  transfers between devices with their start and end apart: 4 -> 5, of which waited for: 0 -> 1; matrix products, arithmetic and copies ran while one was open for 27% -> 30% of each run, Pallas kernels for 0% -> 0%
where the time goes in v5:
time: 90 us; the launch traced here: 89.1 us
  matrix products  24 us (27%)
  blocking collectives  19.5 us (22%)
  between operations  14.1 us (16%)
  local copies, waits for them, and re-layouts  11.2 us (12%)
  starting transfers between devices  8.8 us (10%)
  other arithmetic  8.56 us (10%)
  waiting for transfers between devices  2.81 us (3%)
    all_to_all x1, blocking collectives, cycle_reduce(): lax.all_to_all(chip_share, CHIPS, split_axis=0, concat_axis=0, tiled=True)  19.5 us
    dot_general x1, matrix products, local(): jnp.dot(flat, lax.all_gather(ladder_integrals, PARTS, axis=0, tiled=True)...  14.9 us
    dot_general x1, matrix products, local(): jnp.einsum('ikac,kcm->aim', split, weights, precision=lax.Precision.HIGH,...  9.17 us
    mul x1, local copies, waits for them, and re-layouts, local(): screened = amplitudes * live[:, :, None]  8.21 us
    ppermute x3, starting transfers between devices, cycle_piece(): got = lax.ppermute(piece, PARTS + ('vir',), pairs)  7.83 us
    mul x1, other arithmetic, local(): screened = amplitudes * live[:, :, None]  5.97 us
    ppermute x1, waiting for transfers between devices, cycle_reduce(): chip_share = mine + lax.ppermute(theirs, 'core', pairs)  2.12 us
    unnamed x4, local copies, waits for them, and re-layouts  1.97 us
  transfers between devices with their start and end apart: 5, of which 1 were waited for; matrix products, arithmetic and copies ran while one was open for 30% of the time, Pallas kernels for 0%

profile of v5, /device:TPU:1, one launch (start us, length us, event | category | flops | bytes accessed | tf_op | source)
XLA Modules:
  0.0 89.1 jit_solution(3734948557187343962)
XLA Ops:
  7.2 0.0 copy-start
  7.2 0.0 all-gather.2.cloned.1.call-start
  7.2 0.7 all-gather.2.cloned.1.call-update
  7.9 0.8 copy-done
  8.8 5.2 %collective-permute-start = (f32[16,32,128]{2,1,0:T(8,128)S(1)}, f32[16,32,128]{2,1,0:T(8,128)S(1)}, u32[]{:S(2)}, u32[]{:S(2)}) collective-permute-start(f32[16,32,128]{2,1,0:T(8,128)S(1)} %constant_dynamic-slice_fusion), channel_id=1, source_target_pairs={{0,3},{4,7},{8,11},{12,15},{16,19},{20,23},{24,27},{28,31},{33,32}... | collective-permute-start | bytes 786440 | tf_op jit(solution)/shard_map/ppermute | solution.py:27
  14.0 1.3 %collective-permute-start.1 = (f32[16,32,128]{2,1,0:T(8,128)S(1)}, f32[16,32,128]{2,1,0:T(8,128)S(1)}, u32[]{:S(2)}, u32[]{:S(2)}) collective-permute-start(f32[16,32,128]{2,1,0:T(8,128)S(1)} %constant_dynamic-slice_fusion), channel_id=1, source_target_pairs={{0,2},{4,6},{8,10},{12,14},{16,18},{20,22},{24,26},{28,30},{33,35}... | collective-permute-start | bytes 786440 | tf_op jit(solution)/shard_map/ppermute | solution.py:27
  15.3 1.3 %collective-permute-start.2 = (f32[16,32,128]{2,1,0:T(8,128)S(1)}, f32[16,32,128]{2,1,0:T(8,128)S(1)}, u32[]{:S(2)}, u32[]{:S(2)}) collective-permute-start(f32[16,32,128]{2,1,0:T(8,128)S(1)} %constant_dynamic-slice_fusion), channel_id=1, source_target_pairs={{0,1},{4,5},{8,9},{12,13},{16,17},{20,21},{24,25},{28,29},{33,34},... | collective-permute-start | bytes 786440 | tf_op jit(solution)/shard_map/ppermute | solution.py:27
  16.6 0.7 convert_element_type.3
  17.3 0.1 copy.8
  17.4 6.0 %broadcast_multiply_fusion.1 = f32[96,16,1024]{2,1,0:T(8,128)} fusion(f32[96,16,1024]{2,1,0:T(8,128)} %param.4, f32[96,16]{1,0:T(8,128)S(1)} %copy.8), kind=kLoop, calls=%fused_computation.3 | loop fusion | flops 1572864 | bytes 12589056 | tf_op jit(solution)/shard_map/mul | solution.py:47
  23.4 8.2 %copy.9 = f32[96,16,1024]{0,2,1:T(8,128)} copy(f32[96,16,1024]{2,1,0:T(8,128)} %broadcast_multiply_fusion.1) | data formatting | bytes 12582912 | tf_op jit(solution)/shard_map/mul | solution.py:47
  31.6 0.0 collective-permute-done
  31.6 0.0 collective-permute-done.1
  31.6 0.0 collective-permute-done.2
  31.6 9.2 %fusion.4 = f32[128,96,32,1]{0,1,2,3:T(8,128)S(1)} fusion(f32[96,16,32,32]{0,3,2,1:T(8,128)} %bitcast.25, f32[16,32,128]{2,1,0:T(8,128)S(1)} %collective-permute-done, f32[16,32,128]{2,1,0:T(8,128)S(1)} %collective-permute-done.1, f32[16,32,128]{2,1,0:T(8,128)S(1)} %collective-permute-done.2, f32[16,32,128]{2,1,0:T(8,128)S(1)} %constant_dynamic-slice_fusion, ...), kind=kOutput, calls=%fused_computation.6 | convolution fusion | flops 1208156160 | bytes 8912899 | tf_op jit(solution)/shard_map/ikac,kcm->aim/dot_general | solution.py:55
  40.8 0.0 copy-start.1
  40.8 1.1 %copy-done.1 = f32[128,96,32,1]{0,1,2,3:T(8,128)} copy-done((f32[128,96,32,1]{0,1,2,3:T(8,128)}, f32[128,96,32,1]{0,1,2,3:T(8,128)S(1)}, u32[]{:S(2)}) %copy-start.1) | copy-done | bytes 1572888
  41.9 1.0 %dynamic-slice_bitcast_fusion = f32[16,96,128]{2,1,0:T(8,128)} fusion(f32[16,2,96,128]{3,2,1,0:T(8,128)S(1)} %bitcast.26, s32[]{:T(128)S(6)} %select_n.65), kind=kLoop, calls=%fused_computation.5 | loop fusion | bytes 1572868 | tf_op jit(solution)/shard_map/jit(dynamic_index_in_dim)/squeeze | solution.py:38
  42.9 0.9 %collective-permute-start.3 = (f32[16,96,128]{2,1,0:T(8,128)}, f32[16,96,128]{2,1,0:T(8,128)S(1)}, u32[]{:S(2)}, u32[]{:S(2)}) collective-permute-start(f32[16,96,128]{2,1,0:T(8,128)} %dynamic-slice_bitcast_fusion), channel_id=1, source_target_pairs={{0,4},{4,0},{1,5},{5,1},{2,6},{6,2},{3,7},{7,3},{8,12},{12,8},{9,1... | collective-permute-start | bytes 2359304 | tf_op jit(solution)/shard_map/ppermute | solution.py:40
  43.8 2.1 %collective-permute-done.3 = f32[16,96,128]{2,1,0:T(8,128)S(1)} collective-permute-done((f32[16,96,128]{2,1,0:T(8,128)}, f32[16,96,128]{2,1,0:T(8,128)S(1)}, u32[]{:S(2)}, u32[]{:S(2)}) %collective-permute-start.3) | collective-permute-done | bytes 786464 | tf_op jit(solution)/shard_map/ppermute | solution.py:40
  46.0 1.2 %bitcast_add_fusion = f32[16,96,128]{2,1,0:T(8,128)S(1)} fusion(f32[16,96,128]{2,1,0:T(8,128)S(1)} %collective-permute-done.3, f32[16,2,96,128]{3,2,1,0:T(8,128)} %bitcast.27, s32[]{:T(128)S(6)} %select_n.63), kind=kLoop, calls=%fused_computation.4 | loop fusion | flops 196608 | bytes 2359300 | tf_op jit(solution)/shard_map/add | solution.py:40
  47.2 19.5 %all_to_all.5 = f32[16,96,128]{2,1,0:T(8,128)S(1)} all-to-all(f32[16,96,128]{2,1,0:T(8,128)S(1)} %bitcast_add_fusion), channel_id=1, replica_groups=mesh['y'=4,'z'=4,'core'=2,'vir'=4] {'y','z'}, dimensions={0} | all-to-all | bytes 1572864 | tf_op jit(solution)/shard_map/all_to_all | solution.py:41
  66.7 0.7 reduce_sum.9
  67.3 0.0 all-gather.2.cloned.1.call-done
  67.4 14.9 %broadcast_multiply_fusion = f32[96,16,1024]{2,1,0:T(8,128)} fusion(f32[96,16]{1,0:T(8,128)S(1)} %copy.8, f32[1024,1024]{1,0:T(8,128)} %all-gather.2.cloned.1.call-done, f32[96,16,1024]{2,1,0:T(8,128)} %param.4), kind=kOutput, calls=%fused_computation.2 | convolution fusion | flops 9666822144 | bytes 16783360 | tf_op jit(solution)/shard_map/dot_general | solution.py:65
  (1 shorter events, 0.0 us)
Async XLA Ops:
  7.2 1.6 %copy-start = (f32[128,32,128]{2,1,0:T(8,128)S(1)}, f32[128,32,128]{2,1,0:T(8,128)}, u32[]{:S(2)}) copy-start(f32[128,32,128]{2,1,0:T(8,128)} %param.7) | copy-start | bytes 6291460
  7.2 60.2 %all-gather.2.cloned.1.call-start = ((), (), s32[]{:S(2)}) async-start(), calls=%async_computation.1 | async-start | bytes 4325376 | tf_op jit(solution)/shard_map/all_gather | solution.py:67
  8.8 22.8 %collective-permute-start = (f32[16,32,128]{2,1,0:T(8,128)S(1)}, f32[16,32,128]{2,1,0:T(8,128)S(1)}, u32[]{:S(2)}, u32[]{:S(2)}) collective-permute-start(f32[16,32,128]{2,1,0:T(8,128)S(1)} %constant_dynamic-slice_fusion), channel_id=1, source_target_pairs={{0,3},{4,7},{8,11},{12,15},{16,19},{20,23},{24,27},{28,31},{33,32}... | collective-permute-start | bytes 786440 | tf_op jit(solution)/shard_map/ppermute | solution.py:27
  14.0 17.6 %collective-permute-start.1 = (f32[16,32,128]{2,1,0:T(8,128)S(1)}, f32[16,32,128]{2,1,0:T(8,128)S(1)}, u32[]{:S(2)}, u32[]{:S(2)}) collective-permute-start(f32[16,32,128]{2,1,0:T(8,128)S(1)} %constant_dynamic-slice_fusion), channel_id=1, source_target_pairs={{0,2},{4,6},{8,10},{12,14},{16,18},{20,22},{24,26},{28,30},{33,35}... | collective-permute-start | bytes 786440 | tf_op jit(solution)/shard_map/ppermute | solution.py:27
  15.3 16.3 %collective-permute-start.2 = (f32[16,32,128]{2,1,0:T(8,128)S(1)}, f32[16,32,128]{2,1,0:T(8,128)S(1)}, u32[]{:S(2)}, u32[]{:S(2)}) collective-permute-start(f32[16,32,128]{2,1,0:T(8,128)S(1)} %constant_dynamic-slice_fusion), channel_id=1, source_target_pairs={{0,1},{4,5},{8,9},{12,13},{16,17},{20,21},{24,25},{28,29},{33,34},... | collective-permute-start | bytes 786440 | tf_op jit(solution)/shard_map/ppermute | solution.py:27
  40.8 1.1 %copy-start.1 = (f32[128,96,32,1]{0,1,2,3:T(8,128)}, f32[128,96,32,1]{0,1,2,3:T(8,128)S(1)}, u32[]{:S(2)}) copy-start(f32[128,96,32,1]{0,1,2,3:T(8,128)S(1)} %fusion.4) | copy-start | bytes 4718596
  42.9 3.1 %collective-permute-start.3 = (f32[16,96,128]{2,1,0:T(8,128)}, f32[16,96,128]{2,1,0:T(8,128)S(1)}, u32[]{:S(2)}, u32[]{:S(2)}) collective-permute-start(f32[16,96,128]{2,1,0:T(8,128)} %dynamic-slice_bitcast_fusion), channel_id=1, source_target_pairs={{0,4},{4,0},{1,5},{5,1},{2,6},{6,2},{3,7},{7,3},{8,12},{12,8},{9,1... | collective-permute-start | bytes 2359304 | tf_op jit(solution)/shard_map/ppermute | solution.py:40
Sparse Core Ops, SparseCore 0:
  10.2 52.6 all-gather.1

commit v6 on v5

--- a/solution.py
+++ b/solution.py
@@ -1,6 +1,8 @@
 import jax
 import jax.numpy as jnp
 from jax import lax
+from jax.experimental import pallas as pl
+from jax.experimental.pallas import tpu as pltpu
 from jax.sharding import Mesh
 from jax.sharding import PartitionSpec as P
 
@@ -42,6 +44,24 @@
     return jnp.sum(gathered, axis=0)[:, None, :]
 
 
+def screen_kernel(live_ref, amp_ref, out_ref):
+    n_a, _, rows = out_ref.shape
+    nc = amp_ref.shape[2] // n_a
+    for k in range(amp_ref.shape[1]):
+        flipped = (amp_ref[:, k, :] * live_ref[:, k:k + 1]).T
+        out_ref[:, k * nc:(k + 1) * nc, :] = flipped.reshape(n_a, nc, rows)
+
+
+def screened_by_a(amplitudes, live, virtuals):
+    rows, kblock, width = amplitudes.shape
+    return pl.pallas_call(
+        screen_kernel,
+        out_shape=jax.ShapeDtypeStruct((width // virtuals, kblock * virtuals, rows), jnp.float32),
+        in_specs=[pl.BlockSpec(memory_space=pltpu.VMEM), pl.BlockSpec(memory_space=pltpu.VMEM)],
+        out_specs=pl.BlockSpec(memory_space=pltpu.VMEM),
+    )(live, amplitudes)
+
+
 def local(amplitudes, pair_live, ladder_integrals, cycle_integrals):
     live = pair_live.astype(jnp.float32)
     screened = amplitudes * live[:, :, None]
@@ -51,9 +71,9 @@
     virtuals = cycle_integrals.shape[1]
 
     weights = cycle_piece(cycle_integrals, second_rows)
-    split = screened.reshape(first_rows, second_rows, width // virtuals, virtuals)
+    split = screened_by_a(amplitudes, live, virtuals).reshape(width // virtuals, second_rows, virtuals, first_rows)
     partial_value = jnp.einsum(
-        "ikac,kcm->aim",
+        "akci,kcm->aim",
         split,
         weights,
         precision=lax.Precision.HIGH,

time: 90 us -> 89 us (0.989)
  Pallas kernels: 0 us -> 9.65 us
  local copies, waits for them, and re-layouts: 11.2 us -> 3.72 us
  other arithmetic: 8.56 us -> 2.51 us
  blocking collectives: 19.5 us -> 22.2 us
    pallas_call x0 -> x1, Pallas kernels: none -> 9.65 us  [screened_by_a(): pl.pallas_call(screen_kernel, out_shape=jax.ShapeDtypeStruct((width // vi...]
    mul x1 -> x0, local copies, waits for them, and re-layouts: 8.21 us -> none  [local(): screened = amplitudes * live[:, :, None]]
    mul x1 -> x0, other arithmetic: 5.97 us -> none  [local(): screened = amplitudes * live[:, :, None]]
    all_to_all x1, blocking collectives: 19.5 us -> 22.2 us  [cycle_reduce(): lax.all_to_all(chip_share, CHIPS, split_axis=0, concat_axis=0, tiled=True)]
    unnamed x4 -> x7, local copies, waits for them, and re-layouts: 1.97 us -> 2.76 us
  transfers between devices with their start and end apart: 5 -> 5, of which waited for: 1 -> 2; matrix products, arithmetic and copies ran while one was open for 30% -> 15% of each run, Pallas kernels for 0% -> 11%
where the time goes in v6:
time: 89 us; the launch traced here: 88.6 us
  matrix products  24 us (27%)
  blocking collectives  22.2 us (25%)
  between operations  14.2 us (16%)
  Pallas kernels  9.65 us (11%)
  starting transfers between devices  8.83 us (10%)
  local copies, waits for them, and re-layouts  3.72 us (4%)
  waiting for transfers between devices  3.57 us (4%)
  other arithmetic  2.51 us (3%)
    all_to_all x1, blocking collectives, cycle_reduce(): lax.all_to_all(chip_share, CHIPS, split_axis=0, concat_axis=0, tiled=True)  22.2 us
    dot_general x1, matrix products, local(): jnp.dot(flat, lax.all_gather(ladder_integrals, PARTS, axis=0, tiled=True)...  14.9 us
    pallas_call x1, Pallas kernels, screened_by_a(): pl.pallas_call(screen_kernel, out_shape=jax.ShapeDtypeStruct((width // vi...  9.65 us
    dot_general x1, matrix products, local(): jnp.einsum('akci,kcm->aim', split, weights, precision=lax.Precision.HIGH,...  9.15 us
    ppermute x3, starting transfers between devices, cycle_piece(): got = lax.ppermute(piece, PARTS + ('vir',), pairs)  7.83 us
    unnamed x7, local copies, waits for them, and re-layouts  2.76 us
    ppermute x1, waiting for transfers between devices, cycle_reduce(): chip_share = mine + lax.ppermute(theirs, 'core', pairs)  2.12 us
  transfers between devices with their start and end apart: 5, of which 2 were waited for; matrix products, arithmetic and copies ran while one was open for 15% of the time, Pallas kernels for 11%

profile of v6, /device:TPU:1, one launch (start us, length us, event | category | flops | bytes accessed | tf_op | source)
XLA Modules:
  0.0 88.6 jit_solution(13650504857931820511)
XLA Ops:
  7.2 0.0 copy-start
  7.2 0.0 all-gather.2.cloned.1.call-start
  7.2 0.7 all-gather.2.cloned.1.call-update
  7.9 0.8 copy-done
  8.8 5.2 %collective-permute-start = (f32[16,32,128]{2,1,0:T(8,128)S(1)}, f32[16,32,128]{2,1,0:T(8,128)S(1)}, u32[]{:S(2)}, u32[]{:S(2)}) collective-permute-start(f32[16,32,128]{2,1,0:T(8,128)S(1)} %constant_dynamic-slice_fusion), channel_id=1, source_target_pairs={{0,3},{4,7},{8,11},{12,15},{16,19},{20,23},{24,27},{28,31},{33,32}... | collective-permute-start | bytes 786440 | tf_op jit(solution)/shard_map/ppermute | solution.py:29
  14.0 1.3 %collective-permute-start.1 = (f32[16,32,128]{2,1,0:T(8,128)S(1)}, f32[16,32,128]{2,1,0:T(8,128)S(1)}, u32[]{:S(2)}, u32[]{:S(2)}) collective-permute-start(f32[16,32,128]{2,1,0:T(8,128)S(1)} %constant_dynamic-slice_fusion), channel_id=1, source_target_pairs={{0,2},{4,6},{8,10},{12,14},{16,18},{20,22},{24,26},{28,30},{33,35}... | collective-permute-start | bytes 786440 | tf_op jit(solution)/shard_map/ppermute | solution.py:29
  15.3 1.3 %collective-permute-start.2 = (f32[16,32,128]{2,1,0:T(8,128)S(1)}, f32[16,32,128]{2,1,0:T(8,128)S(1)}, u32[]{:S(2)}, u32[]{:S(2)}) collective-permute-start(f32[16,32,128]{2,1,0:T(8,128)S(1)} %constant_dynamic-slice_fusion), channel_id=1, source_target_pairs={{0,1},{4,5},{8,9},{12,13},{16,17},{20,21},{24,25},{28,29},{33,34},... | collective-permute-start | bytes 786440 | tf_op jit(solution)/shard_map/ppermute | solution.py:29
  16.7 0.8 copy.6
  17.5 0.6 convert_element_type.3.live_ref
  18.1 9.6 %shard_map.59 = f32[32,512,96]{2,1,0:T(8,128)} custom-call(f32[96,16]{1,0:T(8,128)} %convert_element_type.3.live_ref, f32[96,16,1024]{2,1,0:T(8,128)} %amp_ref.1), custom_call_target="tpu_custom_call" | custom-call | tf_op jit(solution)/shard_map/pallas_call | solution.py:57
  27.7 0.0 collective-permute-done
  27.8 0.0 collective-permute-done.1
  27.8 0.0 collective-permute-done.2
  27.8 0.0 copy-start.2
  27.8 9.2 %convolution_bitcast_fusion = f32[16,2,96,128]{3,2,1,0:T(8,128)S(1)} fusion(f32[16,2,96,32,16]{2,3,4,1,0:T(8,128)} %bitcast.24, f32[16,32,128]{2,1,0:T(8,128)S(1)} %collective-permute-done, f32[16,32,128]{2,1,0:T(8,128)S(1)} %collective-permute-done.1, f32[16,32,128]{2,1,0:T(8,128)S(1)} %collective-permute-done.2, ...), kind=kOutput, calls=%fused_computation.5 | convolution fusion | flops 1208156160 | bytes 8912899 | tf_op jit(solution)/shard_map/akci,kcm->aim/dot_general | solution.py:75
  36.9 0.0 copy-start.1
  36.9 1.1 %copy-done.1 = f32[16,2,96,128]{3,2,1,0:T(8,128)} copy-done((f32[16,2,96,128]{3,2,1,0:T(8,128)}, f32[16,2,96,128]{3,2,1,0:T(8,128)S(1)}, u32[]{:S(2)}) %copy-start.1) | copy-done | bytes 1572888
  38.1 0.9 %dynamic-slice_bitcast_fusion = f32[16,96,128]{2,1,0:T(8,128)} fusion(f32[16,2,96,128]{3,2,1,0:T(8,128)S(1)} %convolution_bitcast_fusion, s32[]{:T(128)S(6)} %select_n.65), kind=kLoop, calls=%fused_computation.7 | loop fusion | bytes 1572868 | tf_op jit(solution)/shard_map/jit(dynamic_index_in_dim)/squeeze | solution.py:40
  39.0 1.0 %collective-permute-start.3 = (f32[16,96,128]{2,1,0:T(8,128)}, f32[16,96,128]{2,1,0:T(8,128)S(1)}, u32[]{:S(2)}, u32[]{:S(2)}) collective-permute-start(f32[16,96,128]{2,1,0:T(8,128)} %dynamic-slice_bitcast_fusion), channel_id=1, source_target_pairs={{0,4},{4,0},{1,5},{5,1},{2,6},{6,2},{3,7},{7,3},{8,12},{12,8},{9,1... | collective-permute-start | bytes 2359304 | tf_op jit(solution)/shard_map/ppermute | solution.py:42
  40.0 2.1 %collective-permute-done.3 = f32[16,96,128]{2,1,0:T(8,128)S(1)} collective-permute-done((f32[16,96,128]{2,1,0:T(8,128)}, f32[16,96,128]{2,1,0:T(8,128)S(1)}, u32[]{:S(2)}, u32[]{:S(2)}) %collective-permute-start.3) | collective-permute-done | bytes 786464 | tf_op jit(solution)/shard_map/ppermute | solution.py:42
  42.1 1.2 %bitcast_add_fusion = f32[16,96,128]{2,1,0:T(8,128)S(1)} fusion(f32[16,96,128]{2,1,0:T(8,128)S(1)} %collective-permute-done.3, f32[16,2,96,128]{3,2,1,0:T(8,128)} %copy-done.1, s32[]{:T(128)S(6)} %select_n.63), kind=kLoop, calls=%fused_computation.6 | loop fusion | flops 196608 | bytes 2359300 | tf_op jit(solution)/shard_map/add | solution.py:42
  43.3 22.2 %all_to_all.5 = f32[16,96,128]{2,1,0:T(8,128)S(1)} all-to-all(f32[16,96,128]{2,1,0:T(8,128)S(1)} %bitcast_add_fusion), channel_id=1, replica_groups=mesh['y'=4,'z'=4,'core'=2,'vir'=4] {'y','z'}, dimensions={0} | all-to-all | bytes 1572864 | tf_op jit(solution)/shard_map/all_to_all | solution.py:43
  65.5 0.7 reduce_sum.9
  66.2 0.8 all-gather.2.cloned.1.call-done
  66.9 0.0 copy-done.2
  66.9 14.9 %fusion.3 = f32[96,16,1024]{2,1,0:T(8,128)} fusion(f32[1024,1024]{1,0:T(8,128)} %all-gather.2.cloned.1.call-done, f32[96,16,1024]{2,1,0:T(8,128)} %amp_ref.1, f32[96,16]{1,0:T(8,128)S(1)} %copy-done.2), kind=kOutput, calls=%fused_computation.3 | convolution fusion | flops 9666822144 | bytes 16783360 | tf_op jit(solution)/shard_map/dot_general | solution.py:85
  (1 shorter events, 0.0 us)
Async XLA Ops:
  7.2 1.6 %copy-start = (f32[128,32,128]{2,1,0:T(8,128)S(1)}, f32[128,32,128]{2,1,0:T(8,128)}, u32[]{:S(2)}) copy-start(f32[128,32,128]{2,1,0:T(8,128)} %param.7) | copy-start | bytes 6291460
  7.2 59.8 %all-gather.2.cloned.1.call-start = ((), (), s32[]{:S(2)}) async-start(), calls=%async_computation.1 | async-start | bytes 4325376 | tf_op jit(solution)/shard_map/all_gather | solution.py:87
  8.8 19.0 %collective-permute-start = (f32[16,32,128]{2,1,0:T(8,128)S(1)}, f32[16,32,128]{2,1,0:T(8,128)S(1)}, u32[]{:S(2)}, u32[]{:S(2)}) collective-permute-start(f32[16,32,128]{2,1,0:T(8,128)S(1)} %constant_dynamic-slice_fusion), channel_id=1, source_target_pairs={{0,3},{4,7},{8,11},{12,15},{16,19},{20,23},{24,27},{28,31},{33,32}... | collective-permute-start | bytes 786440 | tf_op jit(solution)/shard_map/ppermute | solution.py:29
  14.0 13.7 %collective-permute-start.1 = (f32[16,32,128]{2,1,0:T(8,128)S(1)}, f32[16,32,128]{2,1,0:T(8,128)S(1)}, u32[]{:S(2)}, u32[]{:S(2)}) collective-permute-start(f32[16,32,128]{2,1,0:T(8,128)S(1)} %constant_dynamic-slice_fusion), channel_id=1, source_target_pairs={{0,2},{4,6},{8,10},{12,14},{16,18},{20,22},{24,26},{28,30},{33,35}... | collective-permute-start | bytes 786440 | tf_op jit(solution)/shard_map/ppermute | solution.py:29
  15.3 12.4 %collective-permute-start.2 = (f32[16,32,128]{2,1,0:T(8,128)S(1)}, f32[16,32,128]{2,1,0:T(8,128)S(1)}, u32[]{:S(2)}, u32[]{:S(2)}) collective-permute-start(f32[16,32,128]{2,1,0:T(8,128)S(1)} %constant_dynamic-slice_fusion), channel_id=1, source_target_pairs={{0,1},{4,5},{8,9},{12,13},{16,17},{20,21},{24,25},{28,29},{33,34},... | collective-permute-start | bytes 786440 | tf_op jit(solution)/shard_map/ppermute | solution.py:29
  27.8 39.2 %copy-start.2 = (f32[96,16]{1,0:T(8,128)S(1)}, f32[96,16]{1,0:T(8,128)}, u32[]{:S(2)}) copy-start(f32[96,16]{1,0:T(8,128)} %convert_element_type.3.live_ref) | copy-start | bytes 18436
  36.9 1.1 %copy-start.1 = (f32[16,2,96,128]{3,2,1,0:T(8,128)}, f32[16,2,96,128]{3,2,1,0:T(8,128)S(1)}, u32[]{:S(2)}) copy-start(f32[16,2,96,128]{3,2,1,0:T(8,128)S(1)} %convolution_bitcast_fusion) | copy-start | bytes 4718596
  39.0 3.1 %collective-permute-start.3 = (f32[16,96,128]{2,1,0:T(8,128)}, f32[16,96,128]{2,1,0:T(8,128)S(1)}, u32[]{:S(2)}, u32[]{:S(2)}) collective-permute-start(f32[16,96,128]{2,1,0:T(8,128)} %dynamic-slice_bitcast_fusion), channel_id=1, source_target_pairs={{0,4},{4,0},{1,5},{5,1},{2,6},{6,2},{3,7},{7,3},{8,12},{12,8},{9,1... | collective-permute-start | bytes 2359304 | tf_op jit(solution)/shard_map/ppermute | solution.py:42
Sparse Core Ops, SparseCore 0:
  10.2 56.6 all-gather.1

commit v7 on v6

--- a/solution.py
+++ b/solution.py
@@ -54,11 +54,17 @@
 
 def screened_by_a(amplitudes, live, virtuals):
     rows, kblock, width = amplitudes.shape
+    lanes = 128
+    per_step = lanes // virtuals
     return pl.pallas_call(
         screen_kernel,
+        grid=(width // lanes,),
         out_shape=jax.ShapeDtypeStruct((width // virtuals, kblock * virtuals, rows), jnp.float32),
-        in_specs=[pl.BlockSpec(memory_space=pltpu.VMEM), pl.BlockSpec(memory_space=pltpu.VMEM)],
-        out_specs=pl.BlockSpec(memory_space=pltpu.VMEM),
+        in_specs=[
+            pl.BlockSpec((rows, kblock), lambda s: (0, 0)),
+            pl.BlockSpec((rows, kblock, lanes), lambda s: (0, 0, s)),
+        ],
+        out_specs=pl.BlockSpec((per_step, kblock * virtuals, rows), lambda s: (s, 0, 0)),
     )(live, amplitudes)
 
 

time: 89 us -> 89.3 us (level)
  transfers between devices with their start and end apart: 5 -> 5, of which waited for: 2 -> 2; matrix products, arithmetic and copies ran while one was open for 15% -> 15% of each run, Pallas kernels for 11% -> 12%
where the time goes in v7:
time: 89.3 us; the launch traced here: 88.8 us
  matrix products  24 us (27%)
  blocking collectives  21.5 us (24%)
  between operations  14.2 us (16%)
  Pallas kernels  10.3 us (12%)
  starting transfers between devices  8.82 us (10%)
  local copies, waits for them, and re-layouts  3.72 us (4%)
  waiting for transfers between devices  3.69 us (4%)
  other arithmetic  2.64 us (3%)
    all_to_all x1, blocking collectives, cycle_reduce(): lax.all_to_all(chip_share, CHIPS, split_axis=0, concat_axis=0, tiled=True)  21.5 us
    dot_general x1, matrix products, local(): jnp.dot(flat, lax.all_gather(ladder_integrals, PARTS, axis=0, tiled=True)...  14.9 us
    pallas_call x1, Pallas kernels, screened_by_a(): pl.pallas_call(screen_kernel, grid=(width // lanes,), out_shape=jax.Shape...  10.3 us
    dot_general x1, matrix products, local(): jnp.einsum('akci,kcm->aim', split, weights, precision=lax.Precision.HIGH,...  9.12 us
    ppermute x3, starting transfers between devices, cycle_piece(): got = lax.ppermute(piece, PARTS + ('vir',), pairs)  7.83 us
    unnamed x7, local copies, waits for them, and re-layouts  2.76 us
    ppermute x1, waiting for transfers between devices, cycle_reduce(): chip_share = mine + lax.ppermute(theirs, 'core', pairs)  2.12 us
  transfers between devices with their start and end apart: 5, of which 2 were waited for; matrix products, arithmetic and copies ran while one was open for 15% of the time, Pallas kernels for 12%

profile of v7, /device:TPU:1, one launch (start us, length us, event | category | flops | bytes accessed | tf_op | source)
XLA Modules:
  0.0 88.8 jit_solution(17110428678785624149)
XLA Ops:
  7.2 0.0 copy-start
  7.2 0.0 all-gather.2.cloned.1.call-start
  7.2 0.7 all-gather.2.cloned.1.call-update
  7.9 0.8 copy-done
  8.8 5.2 %collective-permute-start = (f32[16,32,128]{2,1,0:T(8,128)S(1)}, f32[16,32,128]{2,1,0:T(8,128)S(1)}, u32[]{:S(2)}, u32[]{:S(2)}) collective-permute-start(f32[16,32,128]{2,1,0:T(8,128)S(1)} %constant_dynamic-slice_fusion), channel_id=1, source_target_pairs={{0,3},{4,7},{8,11},{12,15},{16,19},{20,23},{24,27},{28,31},{33,32}... | collective-permute-start | bytes 786440 | tf_op jit(solution)/shard_map/ppermute | solution.py:29
  14.0 1.3 %collective-permute-start.1 = (f32[16,32,128]{2,1,0:T(8,128)S(1)}, f32[16,32,128]{2,1,0:T(8,128)S(1)}, u32[]{:S(2)}, u32[]{:S(2)}) collective-permute-start(f32[16,32,128]{2,1,0:T(8,128)S(1)} %constant_dynamic-slice_fusion), channel_id=1, source_target_pairs={{0,2},{4,6},{8,10},{12,14},{16,18},{20,22},{24,26},{28,30},{33,35}... | collective-permute-start | bytes 786440 | tf_op jit(solution)/shard_map/ppermute | solution.py:29
  15.3 1.3 %collective-permute-start.2 = (f32[16,32,128]{2,1,0:T(8,128)S(1)}, f32[16,32,128]{2,1,0:T(8,128)S(1)}, u32[]{:S(2)}, u32[]{:S(2)}) collective-permute-start(f32[16,32,128]{2,1,0:T(8,128)S(1)} %constant_dynamic-slice_fusion), channel_id=1, source_target_pairs={{0,1},{4,5},{8,9},{12,13},{16,17},{20,21},{24,25},{28,29},{33,34},... | collective-permute-start | bytes 786440 | tf_op jit(solution)/shard_map/ppermute | solution.py:29
  16.7 0.8 copy.6
  17.5 0.6 convert_element_type.3.live_ref
  18.1 10.3 %shard_map.59 = f32[32,512,96]{2,1,0:T(8,128)} custom-call(f32[96,16]{1,0:T(8,128)} %convert_element_type.3.live_ref, f32[96,16,1024]{2,1,0:T(8,128)} %amp_ref.1), custom_call_target="tpu_custom_call" | custom-call | tf_op jit(solution)/shard_map/pallas_call | solution.py:59
  28.4 0.0 collective-permute-done
  28.4 0.0 collective-permute-done.1
  28.4 0.0 collective-permute-done.2
  28.5 0.0 copy-start.2
  28.5 9.1 %convolution_bitcast_fusion = f32[16,2,96,128]{3,2,1,0:T(8,128)S(1)} fusion(f32[16,2,96,32,16]{2,3,4,1,0:T(8,128)} %bitcast.24, f32[16,32,128]{2,1,0:T(8,128)S(1)} %collective-permute-done, f32[16,32,128]{2,1,0:T(8,128)S(1)} %collective-permute-done.1, f32[16,32,128]{2,1,0:T(8,128)S(1)} %collective-permute-done.2, ...), kind=kOutput, calls=%fused_computation.5 | convolution fusion | flops 1208156160 | bytes 8912899 | tf_op jit(solution)/shard_map/akci,kcm->aim/dot_general | solution.py:81
  37.6 0.0 copy-start.1
  37.6 1.1 %copy-done.1 = f32[16,2,96,128]{3,2,1,0:T(8,128)} copy-done((f32[16,2,96,128]{3,2,1,0:T(8,128)}, f32[16,2,96,128]{3,2,1,0:T(8,128)S(1)}, u32[]{:S(2)}) %copy-start.1) | copy-done | bytes 1572888
  38.7 0.9 %dynamic-slice_bitcast_fusion = f32[16,96,128]{2,1,0:T(8,128)} fusion(f32[16,2,96,128]{3,2,1,0:T(8,128)S(1)} %convolution_bitcast_fusion, s32[]{:T(128)S(6)} %select_n.65), kind=kLoop, calls=%fused_computation.7 | loop fusion | bytes 1572868 | tf_op jit(solution)/shard_map/jit(dynamic_index_in_dim)/squeeze | solution.py:40
  39.7 1.0 %collective-permute-start.3 = (f32[16,96,128]{2,1,0:T(8,128)}, f32[16,96,128]{2,1,0:T(8,128)S(1)}, u32[]{:S(2)}, u32[]{:S(2)}) collective-permute-start(f32[16,96,128]{2,1,0:T(8,128)} %dynamic-slice_bitcast_fusion), channel_id=1, source_target_pairs={{0,4},{4,0},{1,5},{5,1},{2,6},{6,2},{3,7},{7,3},{8,12},{12,8},{9,1... | collective-permute-start | bytes 2359304 | tf_op jit(solution)/shard_map/ppermute | solution.py:42
  40.6 2.1 %collective-permute-done.3 = f32[16,96,128]{2,1,0:T(8,128)S(1)} collective-permute-done((f32[16,96,128]{2,1,0:T(8,128)}, f32[16,96,128]{2,1,0:T(8,128)S(1)}, u32[]{:S(2)}, u32[]{:S(2)}) %collective-permute-start.3) | collective-permute-done | bytes 786464 | tf_op jit(solution)/shard_map/ppermute | solution.py:42
  42.8 1.4 %bitcast_add_fusion = f32[16,96,128]{2,1,0:T(8,128)S(1)} fusion(f32[16,96,128]{2,1,0:T(8,128)S(1)} %collective-permute-done.3, f32[16,2,96,128]{3,2,1,0:T(8,128)} %copy-done.1, s32[]{:T(128)S(6)} %select_n.63), kind=kLoop, calls=%fused_computation.6 | loop fusion | flops 196608 | bytes 2359300 | tf_op jit(solution)/shard_map/add | solution.py:42
  44.1 21.5 %all_to_all.5 = f32[16,96,128]{2,1,0:T(8,128)S(1)} all-to-all(f32[16,96,128]{2,1,0:T(8,128)S(1)} %bitcast_add_fusion), channel_id=1, replica_groups=mesh['y'=4,'z'=4,'core'=2,'vir'=4] {'y','z'}, dimensions={0} | all-to-all | bytes 1572864 | tf_op jit(solution)/shard_map/all_to_all | solution.py:43
  65.6 0.7 reduce_sum.9
  66.2 0.9 all-gather.2.cloned.1.call-done
  67.1 0.0 copy-done.2
  67.1 14.9 %fusion.3 = f32[96,16,1024]{2,1,0:T(8,128)} fusion(f32[1024,1024]{1,0:T(8,128)} %all-gather.2.cloned.1.call-done, f32[96,16,1024]{2,1,0:T(8,128)} %amp_ref.1, f32[96,16]{1,0:T(8,128)S(1)} %copy-done.2), kind=kOutput, calls=%fused_computation.3 | convolution fusion | flops 9666822144 | bytes 16783360 | tf_op jit(solution)/shard_map/dot_general | solution.py:91
  (1 shorter events, 0.0 us)
Async XLA Ops:
  7.2 1.6 %copy-start = (f32[128,32,128]{2,1,0:T(8,128)S(1)}, f32[128,32,128]{2,1,0:T(8,128)}, u32[]{:S(2)}) copy-start(f32[128,32,128]{2,1,0:T(8,128)} %param.7) | copy-start | bytes 6291460
  7.2 59.9 %all-gather.2.cloned.1.call-start = ((), (), s32[]{:S(2)}) async-start(), calls=%async_computation.1 | async-start | bytes 4325376 | tf_op jit(solution)/shard_map/all_gather | solution.py:93
  8.8 19.7 %collective-permute-start = (f32[16,32,128]{2,1,0:T(8,128)S(1)}, f32[16,32,128]{2,1,0:T(8,128)S(1)}, u32[]{:S(2)}, u32[]{:S(2)}) collective-permute-start(f32[16,32,128]{2,1,0:T(8,128)S(1)} %constant_dynamic-slice_fusion), channel_id=1, source_target_pairs={{0,3},{4,7},{8,11},{12,15},{16,19},{20,23},{24,27},{28,31},{33,32}... | collective-permute-start | bytes 786440 | tf_op jit(solution)/shard_map/ppermute | solution.py:29
  14.0 14.4 %collective-permute-start.1 = (f32[16,32,128]{2,1,0:T(8,128)S(1)}, f32[16,32,128]{2,1,0:T(8,128)S(1)}, u32[]{:S(2)}, u32[]{:S(2)}) collective-permute-start(f32[16,32,128]{2,1,0:T(8,128)S(1)} %constant_dynamic-slice_fusion), channel_id=1, source_target_pairs={{0,2},{4,6},{8,10},{12,14},{16,18},{20,22},{24,26},{28,30},{33,35}... | collective-permute-start | bytes 786440 | tf_op jit(solution)/shard_map/ppermute | solution.py:29
  15.3 13.1 %collective-permute-start.2 = (f32[16,32,128]{2,1,0:T(8,128)S(1)}, f32[16,32,128]{2,1,0:T(8,128)S(1)}, u32[]{:S(2)}, u32[]{:S(2)}) collective-permute-start(f32[16,32,128]{2,1,0:T(8,128)S(1)} %constant_dynamic-slice_fusion), channel_id=1, source_target_pairs={{0,1},{4,5},{8,9},{12,13},{16,17},{20,21},{24,25},{28,29},{33,34},... | collective-permute-start | bytes 786440 | tf_op jit(solution)/shard_map/ppermute | solution.py:29
  28.5 38.7 %copy-start.2 = (f32[96,16]{1,0:T(8,128)S(1)}, f32[96,16]{1,0:T(8,128)}, u32[]{:S(2)}) copy-start(f32[96,16]{1,0:T(8,128)} %convert_element_type.3.live_ref) | copy-start | bytes 18436
  37.6 1.1 %copy-start.1 = (f32[16,2,96,128]{3,2,1,0:T(8,128)}, f32[16,2,96,128]{3,2,1,0:T(8,128)S(1)}, u32[]{:S(2)}) copy-start(f32[16,2,96,128]{3,2,1,0:T(8,128)S(1)} %convolution_bitcast_fusion) | copy-start | bytes 4718596
  39.7 3.1 %collective-permute-start.3 = (f32[16,96,128]{2,1,0:T(8,128)}, f32[16,96,128]{2,1,0:T(8,128)S(1)}, u32[]{:S(2)}, u32[]{:S(2)}) collective-permute-start(f32[16,96,128]{2,1,0:T(8,128)} %dynamic-slice_bitcast_fusion), channel_id=1, source_target_pairs={{0,4},{4,0},{1,5},{5,1},{2,6},{6,2},{3,7},{7,3},{8,12},{12,8},{9,1... | collective-permute-start | bytes 2359304 | tf_op jit(solution)/shard_map/ppermute | solution.py:42
Sparse Core Ops, SparseCore 0:
  10.2 56.8 all-gather.1

commit v8 on v7

--- a/solution.py
+++ b/solution.py
@@ -7,7 +7,6 @@
 from jax.sharding import PartitionSpec as P
 
 PARTS = ("y", "z", "core")
-CHIPS = ("y", "z")
 
 
 def cycle_piece(cycle_integrals, kblock):
@@ -40,15 +39,17 @@
     theirs = lax.dynamic_index_in_dim(by_core, (core + 1) % cores, axis=1, keepdims=False)
     pairs = [(c, (c + 1) % cores) for c in range(cores)]
     chip_share = mine + lax.ppermute(theirs, "core", pairs)
-    gathered = lax.all_to_all(chip_share, CHIPS, split_axis=0, concat_axis=0, tiled=True)
-    return jnp.sum(gathered, axis=0)[:, None, :]
+    n_y = lax.axis_size("y")
+    by_y = chip_share.reshape((n_y, -1) + rest)
+    rows_y = jnp.sum(lax.all_to_all(by_y, "y", split_axis=0, concat_axis=0, tiled=False), axis=0)
+    return lax.all_to_all(rows_y, "z", split_axis=0, concat_axis=0, tiled=False)
 
 
 def screen_kernel(live_ref, amp_ref, out_ref):
     n_a, _, rows = out_ref.shape
     nc = amp_ref.shape[2] // n_a
     for k in range(amp_ref.shape[1]):
-        flipped = (amp_ref[:, k, :] * live_ref[:, k:k + 1]).T
+        flipped = (amp_ref[:, k, :] * live_ref[:, k:k + 1].astype(jnp.float32)).T
         out_ref[:, k * nc:(k + 1) * nc, :] = flipped.reshape(n_a, nc, rows)
 
 
@@ -77,7 +78,7 @@
     virtuals = cycle_integrals.shape[1]
 
     weights = cycle_piece(cycle_integrals, second_rows)
-    split = screened_by_a(amplitudes, live, virtuals).reshape(width // virtuals, second_rows, virtuals, first_rows)
+    split = screened_by_a(amplitudes, pair_live, virtuals).reshape(width // virtuals, second_rows, virtuals, first_rows)
     partial_value = jnp.einsum(
         "akci,kcm->aim",
         split,
@@ -95,7 +96,8 @@
         preferred_element_type=jnp.float32,
     )
     ladder_part = ladder.reshape(first_rows, second_rows, width) * live[:, :, None]
-    return (ladder_part, cycle_part)
+    ladder_part, cycle_part = lax.optimization_barrier((ladder_part, cycle_part))
+    return (ladder_part, jnp.sum(cycle_part, axis=0)[:, None, :])
 
 
 def solution(mesh):

time: 89.3 us -> 93.1 us (1.043)
  blocking collectives: 21.5 us -> 0 us
  waiting for transfers between devices: 3.69 us -> 20.1 us
  starting transfers between devices: 8.82 us -> 15.7 us
  other arithmetic: 2.64 us -> 3.65 us
    all_to_all x1 -> x0, blocking collectives: 21.5 us -> none  [cycle_reduce(): lax.all_to_all(chip_share, CHIPS, split_axis=0, concat_axis=0, tiled=True)]
    all_to_all x0 -> x2, waiting for transfers between devices: none -> 17.3 us  [the longest x1 17.3 us: cycle_reduce(): lax.all_to_all(by_y, 'y', split_axis=0, concat_axis=0, tiled=False)]
    all_to_all x0 -> x2, starting transfers between devices: none -> 6.86 us  [the longest x1 3.49 us: cycle_reduce(): lax.all_to_all(by_y, 'y', split_axis=0, concat_axis=0, tiled=False)]
    add x1, other arithmetic: 1.35 us -> 2.31 us  [cycle_reduce(): chip_share = mine + lax.ppermute(theirs, 'core', pairs)]
  transfers between devices with their start and end apart: 5 -> 7, of which waited for: 2 -> 2; matrix products, arithmetic and copies ran while one was open for 15% -> 32% of each run, Pallas kernels for 12% -> 11%
where the time goes in v8:
time: 93.1 us; the launch traced here: 92.5 us
  matrix products  24 us (26%)
  waiting for transfers between devices  20.1 us (22%)
  starting transfers between devices  15.7 us (17%)
  between operations  14.2 us (15%)
  Pallas kernels  10.3 us (11%)
  local copies, waits for them, and re-layouts  4.44 us (5%)
  other arithmetic  3.65 us (4%)
    all_to_all x1, waiting for transfers between devices, cycle_reduce(): lax.all_to_all(by_y, 'y', split_axis=0, concat_axis=0, tiled=False)  17.3 us
    dot_general x1, matrix products, local(): jnp.dot(flat, lax.all_gather(ladder_integrals, PARTS, axis=0, tiled=True)...  14.9 us
    pallas_call x1, Pallas kernels, screened_by_a(): pl.pallas_call(screen_kernel, grid=(width // lanes,), out_shape=jax.Shape...  10.3 us
    dot_general x1, matrix products, local(): jnp.einsum('akci,kcm->aim', split, weights, precision=lax.Precision.HIGH,...  9.15 us
    ppermute x3, starting transfers between devices, cycle_piece(): got = lax.ppermute(piece, PARTS + ('vir',), pairs)  7.83 us
    all_to_all x1, starting transfers between devices, cycle_reduce(): lax.all_to_all(by_y, 'y', split_axis=0, concat_axis=0, tiled=False)  3.49 us
    unnamed x7, local copies, waits for them, and re-layouts  3.38 us
    all_to_all x1, starting transfers between devices, cycle_reduce(): return lax.all_to_all(rows_y, 'z', split_axis=0, concat_axis=0, tiled=False)  3.36 us
  transfers between devices with their start and end apart: 7, of which 2 were waited for; matrix products, arithmetic and copies ran while one was open for 32% of the time, Pallas kernels for 11%

profile of v8, /device:TPU:1, one launch (start us, length us, event | category | flops | bytes accessed | tf_op | source)
XLA Modules:
  0.0 92.5 jit_solution(17171354430162669917)
XLA Ops:
  7.2 0.0 copy-start
  7.2 0.0 all-gather.2.cloned.1.call-start
  7.2 0.7 all-gather.2.cloned.1.call-update
  7.9 0.8 copy-done
  8.8 5.2 %collective-permute-start = (f32[16,32,128]{2,1,0:T(8,128)S(1)}, f32[16,32,128]{2,1,0:T(8,128)S(1)}, u32[]{:S(2)}, u32[]{:S(2)}) collective-permute-start(f32[16,32,128]{2,1,0:T(8,128)S(1)} %constant_dynamic-slice_fusion), channel_id=1, source_target_pairs={{0,3},{4,7},{8,11},{12,15},{16,19},{20,23},{24,27},{28,31},{33,32}... | collective-permute-start | bytes 786440 | tf_op jit(solution)/shard_map/ppermute | solution.py:28
  14.0 1.3 %collective-permute-start.1 = (f32[16,32,128]{2,1,0:T(8,128)S(1)}, f32[16,32,128]{2,1,0:T(8,128)S(1)}, u32[]{:S(2)}, u32[]{:S(2)}) collective-permute-start(f32[16,32,128]{2,1,0:T(8,128)S(1)} %constant_dynamic-slice_fusion), channel_id=1, source_target_pairs={{0,2},{4,6},{8,10},{12,14},{16,18},{20,22},{24,26},{28,30},{33,35}... | collective-permute-start | bytes 786440 | tf_op jit(solution)/shard_map/ppermute | solution.py:28
  15.3 1.3 %collective-permute-start.2 = (f32[16,32,128]{2,1,0:T(8,128)S(1)}, f32[16,32,128]{2,1,0:T(8,128)S(1)}, u32[]{:S(2)}, u32[]{:S(2)}) collective-permute-start(f32[16,32,128]{2,1,0:T(8,128)S(1)} %constant_dynamic-slice_fusion), channel_id=1, source_target_pairs={{0,1},{4,5},{8,9},{12,13},{16,17},{20,21},{24,25},{28,29},{33,34},... | collective-permute-start | bytes 786440 | tf_op jit(solution)/shard_map/ppermute | solution.py:28
  16.7 1.4 %copy.7.live_ref = s32[96,16]{1,0:T(8,128)} copy(s32[96,16]{0,1:T(8,128)} %param.5) | data formatting | bytes 12288 | tf_op args[1]
  18.1 10.3 %shard_map.59 = f32[32,512,96]{2,1,0:T(8,128)} custom-call(s32[96,16]{1,0:T(8,128)} %copy.7.live_ref, f32[96,16,1024]{2,1,0:T(8,128)} %amp_ref.1), custom_call_target="tpu_custom_call" | custom-call | tf_op jit(solution)/shard_map/pallas_call | solution.py:60
  28.4 0.0 collective-permute-done
  28.4 0.0 collective-permute-done.1
  28.4 0.0 collective-permute-done.2
  28.5 0.0 copy-start.2
  28.5 9.1 %convolution_bitcast_fusion = f32[16,2,96,128]{3,2,1,0:T(8,128)S(1)} fusion(f32[16,2,96,32,16]{2,3,4,1,0:T(8,128)} %bitcast.25, f32[16,32,128]{2,1,0:T(8,128)S(1)} %collective-permute-done, f32[16,32,128]{2,1,0:T(8,128)S(1)} %collective-permute-done.1, f32[16,32,128]{2,1,0:T(8,128)S(1)} %collective-permute-done.2, ...), kind=kOutput, calls=%fused_computation.5 | convolution fusion | flops 1208156160 | bytes 8912899 | tf_op jit(solution)/shard_map/akci,kcm->aim/dot_general | solution.py:82
  37.6 0.0 copy-start.1
  37.6 1.1 %copy-done.1 = f32[16,2,96,128]{3,2,1,0:T(8,128)} copy-done((f32[16,2,96,128]{3,2,1,0:T(8,128)}, f32[16,2,96,128]{3,2,1,0:T(8,128)S(1)}, u32[]{:S(2)}) %copy-start.1) | copy-done | bytes 1572888
  38.8 0.9 %dynamic-slice_bitcast_fusion = f32[16,96,128]{2,1,0:T(8,128)} fusion(f32[16,2,96,128]{3,2,1,0:T(8,128)S(1)} %convolution_bitcast_fusion, s32[]{:T(128)S(6)} %select_n.65), kind=kLoop, calls=%fused_computation.7 | loop fusion | bytes 1572868 | tf_op jit(solution)/shard_map/jit(dynamic_index_in_dim)/squeeze | solution.py:39
  39.7 1.0 %collective-permute-start.3 = (f32[16,96,128]{2,1,0:T(8,128)}, f32[16,96,128]{2,1,0:T(8,128)S(1)}, u32[]{:S(2)}, u32[]{:S(2)}) collective-permute-start(f32[16,96,128]{2,1,0:T(8,128)} %dynamic-slice_bitcast_fusion), channel_id=1, source_target_pairs={{0,4},{4,0},{1,5},{5,1},{2,6},{6,2},{3,7},{7,3},{8,12},{12,8},{9,1... | collective-permute-start | bytes 2359304 | tf_op jit(solution)/shard_map/ppermute | solution.py:41
  40.7 2.1 %collective-permute-done.3 = f32[16,96,128]{2,1,0:T(8,128)S(1)} collective-permute-done((f32[16,96,128]{2,1,0:T(8,128)}, f32[16,96,128]{2,1,0:T(8,128)S(1)}, u32[]{:S(2)}, u32[]{:S(2)}) %collective-permute-start.3) | collective-permute-done | bytes 786464 | tf_op jit(solution)/shard_map/ppermute | solution.py:41
  42.8 2.3 %bitcast_add_fusion = f32[16,96,128]{2,1,0:T(8,128)} fusion(f32[16,96,128]{2,1,0:T(8,128)S(1)} %collective-permute-done.3, f32[16,2,96,128]{3,2,1,0:T(8,128)} %copy-done.1, s32[]{:T(128)S(6)} %select_n.63), kind=kLoop, calls=%fused_computation.6 | loop fusion | flops 196608 | bytes 2359300 | tf_op jit(solution)/shard_map/add | solution.py:41
  45.1 3.5 %all-to-all-start = ((f32[4,4,96,128]{3,2,1,0:T(8,128)}), f32[4,4,96,128]{3,2,1,0:T(8,128)S(1)}, u32[]{:S(2)}, u32[]{:S(2)}) async-start(f32[4,4,96,128]{3,2,1,0:T(8,128)} %bitcast.10), calls=%async_computation | async-start | bytes 1572864 | tf_op jit(solution)/shard_map/all_to_all | solution.py:44
  48.6 0.0 copy-done.2
  48.6 0.1 copy.6
  48.7 17.3 %all-to-all-done = f32[4,4,96,128]{3,2,1,0:T(8,128)S(1)} async-done(((f32[4,4,96,128]{3,2,1,0:T(8,128)}), f32[4,4,96,128]{3,2,1,0:T(8,128)S(1)}, u32[]{:S(2)}, u32[]{:S(2)}) %all-to-all-start) | async-done | bytes 786464 | tf_op jit(solution)/shard_map/all_to_all | solution.py:44
  66.0 0.7 reduce_sum.18
  66.7 3.4 %all-to-all-start.1 = ((f32[4,96,128]{2,1,0:T(8,128)}), f32[4,96,128]{2,1,0:T(8,128)S(1)}, u32[]{:S(2)}, u32[]{:S(2)}) async-start(f32[4,96,128]{2,1,0:T(8,128)} %reduce_sum.18), calls=%async_computation.1 | async-start | bytes 393216 | tf_op jit(solution)/shard_map/all_to_all | solution.py:45
  70.1 0.0 all-gather.2.cloned.1.call-done
  70.1 14.9 %fusion.3 = f32[96,16,1024]{2,1,0:T(8,128)} fusion(f32[1024,1024]{1,0:T(8,128)} %all-gather.2.cloned.1.call-done, f32[96,16,1024]{2,1,0:T(8,128)} %amp_ref.1, f32[96,16]{1,0:T(8,128)S(1)} %copy.6), kind=kOutput, calls=%fused_computation.3 | convolution fusion | flops 9666822144 | bytes 16783360 | tf_op jit(solution)/shard_map/dot_general | solution.py:92
  85.0 0.0 all-to-all-done.1
  85.0 0.6 reduce_sum.19
  (2 shorter events, 0.0 us)
Async XLA Ops:
  7.2 1.6 %copy-start = (f32[128,32,128]{2,1,0:T(8,128)S(1)}, f32[128,32,128]{2,1,0:T(8,128)}, u32[]{:S(2)}) copy-start(f32[128,32,128]{2,1,0:T(8,128)} %param.7) | copy-start | bytes 6291460
  7.2 62.9 %all-gather.2.cloned.1.call-start = ((), (), s32[]{:S(2)}) async-start(), calls=%async_computation.2 | async-start | bytes 4325376 | tf_op jit(solution)/shard_map/all_gather | solution.py:94
  8.8 19.7 %collective-permute-start = (f32[16,32,128]{2,1,0:T(8,128)S(1)}, f32[16,32,128]{2,1,0:T(8,128)S(1)}, u32[]{:S(2)}, u32[]{:S(2)}) collective-permute-start(f32[16,32,128]{2,1,0:T(8,128)S(1)} %constant_dynamic-slice_fusion), channel_id=1, source_target_pairs={{0,3},{4,7},{8,11},{12,15},{16,19},{20,23},{24,27},{28,31},{33,32}... | collective-permute-start | bytes 786440 | tf_op jit(solution)/shard_map/ppermute | solution.py:28
  14.0 14.4 %collective-permute-start.1 = (f32[16,32,128]{2,1,0:T(8,128)S(1)}, f32[16,32,128]{2,1,0:T(8,128)S(1)}, u32[]{:S(2)}, u32[]{:S(2)}) collective-permute-start(f32[16,32,128]{2,1,0:T(8,128)S(1)} %constant_dynamic-slice_fusion), channel_id=1, source_target_pairs={{0,2},{4,6},{8,10},{12,14},{16,18},{20,22},{24,26},{28,30},{33,35}... | collective-permute-start | bytes 786440 | tf_op jit(solution)/shard_map/ppermute | solution.py:28
  15.3 13.1 %collective-permute-start.2 = (f32[16,32,128]{2,1,0:T(8,128)S(1)}, f32[16,32,128]{2,1,0:T(8,128)S(1)}, u32[]{:S(2)}, u32[]{:S(2)}) collective-permute-start(f32[16,32,128]{2,1,0:T(8,128)S(1)} %constant_dynamic-slice_fusion), channel_id=1, source_target_pairs={{0,1},{4,5},{8,9},{12,13},{16,17},{20,21},{24,25},{28,29},{33,34},... | collective-permute-start | bytes 786440 | tf_op jit(solution)/shard_map/ppermute | solution.py:28
  28.5 20.2 %copy-start.2 = (s32[96,16]{0,1:T(8,128)S(1)}, s32[96,16]{0,1:T(8,128)}, u32[]{:S(2)}) copy-start(s32[96,16]{0,1:T(8,128)} %param.5) | copy-start | bytes 18436
  37.6 1.1 %copy-start.1 = (f32[16,2,96,128]{3,2,1,0:T(8,128)}, f32[16,2,96,128]{3,2,1,0:T(8,128)S(1)}, u32[]{:S(2)}) copy-start(f32[16,2,96,128]{3,2,1,0:T(8,128)S(1)} %convolution_bitcast_fusion) | copy-start | bytes 4718596
  39.7 3.1 %collective-permute-start.3 = (f32[16,96,128]{2,1,0:T(8,128)}, f32[16,96,128]{2,1,0:T(8,128)S(1)}, u32[]{:S(2)}, u32[]{:S(2)}) collective-permute-start(f32[16,96,128]{2,1,0:T(8,128)} %dynamic-slice_bitcast_fusion), channel_id=1, source_target_pairs={{0,4},{4,0},{1,5},{5,1},{2,6},{6,2},{3,7},{7,3},{8,12},{12,8},{9,1... | collective-permute-start | bytes 2359304 | tf_op jit(solution)/shard_map/ppermute | solution.py:41
  45.1 20.9 %all-to-all-start = ((f32[4,4,96,128]{3,2,1,0:T(8,128)}), f32[4,4,96,128]{3,2,1,0:T(8,128)S(1)}, u32[]{:S(2)}, u32[]{:S(2)}) async-start(f32[4,4,96,128]{3,2,1,0:T(8,128)} %bitcast.10), calls=%async_computation | async-start | bytes 1572864 | tf_op jit(solution)/shard_map/all_to_all | solution.py:44
  66.7 18.3 %all-to-all-start.1 = ((f32[4,96,128]{2,1,0:T(8,128)}), f32[4,96,128]{2,1,0:T(8,128)S(1)}, u32[]{:S(2)}, u32[]{:S(2)}) async-start(f32[4,96,128]{2,1,0:T(8,128)} %reduce_sum.18), calls=%async_computation.1 | async-start | bytes 393216 | tf_op jit(solution)/shard_map/all_to_all | solution.py:45
Sparse Core Ops, SparseCore 0:
  10.2 53.7 all-gather.1

commit v9 on v7

--- a/solution.py
+++ b/solution.py
@@ -40,8 +40,7 @@
     theirs = lax.dynamic_index_in_dim(by_core, (core + 1) % cores, axis=1, keepdims=False)
     pairs = [(c, (c + 1) % cores) for c in range(cores)]
     chip_share = mine + lax.ppermute(theirs, "core", pairs)
-    gathered = lax.all_to_all(chip_share, CHIPS, split_axis=0, concat_axis=0, tiled=True)
-    return jnp.sum(gathered, axis=0)[:, None, :]
+    return lax.all_to_all(chip_share, CHIPS, split_axis=0, concat_axis=0, tiled=True)
 
 
 def screen_kernel(live_ref, amp_ref, out_ref):
@@ -95,7 +94,8 @@
         preferred_element_type=jnp.float32,
     )
     ladder_part = ladder.reshape(first_rows, second_rows, width) * live[:, :, None]
-    return (ladder_part, cycle_part)
+    ladder_part, cycle_part = lax.optimization_barrier((ladder_part, cycle_part))
+    return (ladder_part, jnp.sum(cycle_part, axis=0)[:, None, :])
 
 
 def solution(mesh):

time: 89.3 us -> 88.2 us (0.988)
  blocking collectives: 21.5 us -> 0 us
  waiting for transfers between devices: 3.69 us -> 17.9 us
  starting transfers between devices: 8.82 us -> 13.9 us
  other arithmetic: 2.64 us -> 3.54 us
    all_to_all x1 -> x0, blocking collectives: 21.5 us -> none  [cycle_reduce(): lax.all_to_all(chip_share, CHIPS, split_axis=0, concat_axis=0, tiled=True)]
    all_gather x1, waiting for transfers between devices: 0.88 us -> 15.1 us  [local(): lax.all_gather(ladder_integrals, PARTS, axis=0, tiled=True)]
    all_to_all x0 -> x1, starting transfers between devices: none -> 5.04 us  [cycle_reduce(): lax.all_to_all(chip_share, CHIPS, split_axis=0, concat_axis=0, tiled=True)]
    add x1, other arithmetic: 1.35 us -> 2.25 us  [cycle_reduce(): chip_share = mine + lax.ppermute(theirs, 'core', pairs)]
  transfers between devices with their start and end apart: 5 -> 6, of which waited for: 2 -> 2; matrix products, arithmetic and copies ran while one was open for 15% -> 33% of each run, Pallas kernels for 12% -> 12%
where the time goes in v9:
time: 88.2 us; the launch traced here: 87.5 us
  matrix products  24 us (27%)
  waiting for transfers between devices  17.9 us (20%)
  between operations  14.2 us (16%)
  starting transfers between devices  13.9 us (16%)
  Pallas kernels  10.3 us (12%)
  local copies, waits for them, and re-layouts  3.72 us (4%)
  other arithmetic  3.54 us (4%)
    all_gather x1, waiting for transfers between devices, local(): lax.all_gather(ladder_integrals, PARTS, axis=0, tiled=True)  15.1 us
    dot_general x1, matrix products, local(): jnp.dot(flat, lax.all_gather(ladder_integrals, PARTS, axis=0, tiled=True)...  14.9 us
    pallas_call x1, Pallas kernels, screened_by_a(): pl.pallas_call(screen_kernel, grid=(width // lanes,), out_shape=jax.Shape...  10.3 us
    dot_general x1, matrix products, local(): jnp.einsum('akci,kcm->aim', split, weights, precision=lax.Precision.HIGH,...  9.12 us
    ppermute x3, starting transfers between devices, cycle_piece(): got = lax.ppermute(piece, PARTS + ('vir',), pairs)  7.83 us
    all_to_all x1, starting transfers between devices, cycle_reduce(): lax.all_to_all(chip_share, CHIPS, split_axis=0, concat_axis=0, tiled=True)  5.04 us
    unnamed x7, local copies, waits for them, and re-layouts  2.76 us
    add x1, other arithmetic, cycle_reduce(): chip_share = mine + lax.ppermute(theirs, 'core', pairs)  2.25 us
  transfers between devices with their start and end apart: 6, of which 2 were waited for; matrix products, arithmetic and copies ran while one was open for 33% of the time, Pallas kernels for 12%

profile of v9, /device:TPU:1, one launch (start us, length us, event | category | flops | bytes accessed | tf_op | source)
XLA Modules:
  0.0 87.5 jit_solution(3273358609960381808)
XLA Ops:
  7.2 0.0 copy-start
  7.2 0.0 all-gather.2.cloned.1.call-start
  7.2 0.7 all-gather.2.cloned.1.call-update
  7.9 0.8 copy-done
  8.8 5.2 %collective-permute-start = (f32[16,32,128]{2,1,0:T(8,128)S(1)}, f32[16,32,128]{2,1,0:T(8,128)S(1)}, u32[]{:S(2)}, u32[]{:S(2)}) collective-permute-start(f32[16,32,128]{2,1,0:T(8,128)S(1)} %constant_dynamic-slice_fusion), channel_id=1, source_target_pairs={{0,3},{4,7},{8,11},{12,15},{16,19},{20,23},{24,27},{28,31},{33,32}... | collective-permute-start | bytes 786440 | tf_op jit(solution)/shard_map/ppermute | solution.py:29
  14.0 1.3 %collective-permute-start.1 = (f32[16,32,128]{2,1,0:T(8,128)S(1)}, f32[16,32,128]{2,1,0:T(8,128)S(1)}, u32[]{:S(2)}, u32[]{:S(2)}) collective-permute-start(f32[16,32,128]{2,1,0:T(8,128)S(1)} %constant_dynamic-slice_fusion), channel_id=1, source_target_pairs={{0,2},{4,6},{8,10},{12,14},{16,18},{20,22},{24,26},{28,30},{33,35}... | collective-permute-start | bytes 786440 | tf_op jit(solution)/shard_map/ppermute | solution.py:29
  15.3 1.3 %collective-permute-start.2 = (f32[16,32,128]{2,1,0:T(8,128)S(1)}, f32[16,32,128]{2,1,0:T(8,128)S(1)}, u32[]{:S(2)}, u32[]{:S(2)}) collective-permute-start(f32[16,32,128]{2,1,0:T(8,128)S(1)} %constant_dynamic-slice_fusion), channel_id=1, source_target_pairs={{0,1},{4,5},{8,9},{12,13},{16,17},{20,21},{24,25},{28,29},{33,34},... | collective-permute-start | bytes 786440 | tf_op jit(solution)/shard_map/ppermute | solution.py:29
  16.7 0.8 copy.6
  17.5 0.6 convert_element_type.3.live_ref
  18.1 10.3 %shard_map.59 = f32[32,512,96]{2,1,0:T(8,128)} custom-call(f32[96,16]{1,0:T(8,128)} %convert_element_type.3.live_ref, f32[96,16,1024]{2,1,0:T(8,128)} %amp_ref.1), custom_call_target="tpu_custom_call" | custom-call | tf_op jit(solution)/shard_map/pallas_call | solution.py:58
  28.4 0.0 collective-permute-done
  28.4 0.0 collective-permute-done.1
  28.5 0.0 collective-permute-done.2
  28.5 0.0 copy-start.2
  28.5 9.1 %convolution_bitcast_fusion = f32[16,2,96,128]{3,2,1,0:T(8,128)S(1)} fusion(f32[16,2,96,32,16]{2,3,4,1,0:T(8,128)} %bitcast.24, f32[16,32,128]{2,1,0:T(8,128)S(1)} %collective-permute-done, f32[16,32,128]{2,1,0:T(8,128)S(1)} %collective-permute-done.1, f32[16,32,128]{2,1,0:T(8,128)S(1)} %collective-permute-done.2, ...), kind=kOutput, calls=%fused_computation.5 | convolution fusion | flops 1208156160 | bytes 8912899 | tf_op jit(solution)/shard_map/akci,kcm->aim/dot_general | solution.py:80
  37.6 0.0 copy-start.1
  37.6 1.1 %copy-done.1 = f32[16,2,96,128]{3,2,1,0:T(8,128)} copy-done((f32[16,2,96,128]{3,2,1,0:T(8,128)}, f32[16,2,96,128]{3,2,1,0:T(8,128)S(1)}, u32[]{:S(2)}) %copy-start.1) | copy-done | bytes 1572888
  38.8 0.9 %dynamic-slice_bitcast_fusion = f32[16,96,128]{2,1,0:T(8,128)} fusion(f32[16,2,96,128]{3,2,1,0:T(8,128)S(1)} %convolution_bitcast_fusion, s32[]{:T(128)S(6)} %select_n.65), kind=kLoop, calls=%fused_computation.7 | loop fusion | bytes 1572868 | tf_op jit(solution)/shard_map/jit(dynamic_index_in_dim)/squeeze | solution.py:40
  39.7 1.0 %collective-permute-start.3 = (f32[16,96,128]{2,1,0:T(8,128)}, f32[16,96,128]{2,1,0:T(8,128)S(1)}, u32[]{:S(2)}, u32[]{:S(2)}) collective-permute-start(f32[16,96,128]{2,1,0:T(8,128)} %dynamic-slice_bitcast_fusion), channel_id=1, source_target_pairs={{0,4},{4,0},{1,5},{5,1},{2,6},{6,2},{3,7},{7,3},{8,12},{12,8},{9,1... | collective-permute-start | bytes 2359304 | tf_op jit(solution)/shard_map/ppermute | solution.py:42
  40.7 2.1 %collective-permute-done.3 = f32[16,96,128]{2,1,0:T(8,128)S(1)} collective-permute-done((f32[16,96,128]{2,1,0:T(8,128)}, f32[16,96,128]{2,1,0:T(8,128)S(1)}, u32[]{:S(2)}, u32[]{:S(2)}) %collective-permute-start.3) | collective-permute-done | bytes 786464 | tf_op jit(solution)/shard_map/ppermute | solution.py:42
  42.8 2.3 %bitcast_add_fusion = f32[16,96,128]{2,1,0:T(8,128)} fusion(f32[16,96,128]{2,1,0:T(8,128)S(1)} %collective-permute-done.3, f32[16,2,96,128]{3,2,1,0:T(8,128)} %copy-done.1, s32[]{:T(128)S(6)} %select_n.63), kind=kLoop, calls=%fused_computation.6 | loop fusion | flops 196608 | bytes 2359300 | tf_op jit(solution)/shard_map/add | solution.py:42
  45.0 5.0 %all-to-all-start = ((f32[16,96,128]{2,1,0:T(8,128)}), f32[16,96,128]{2,1,0:T(8,128)S(1)}, u32[]{:S(2)}, u32[]{:S(2)}) async-start(f32[16,96,128]{2,1,0:T(8,128)} %bitcast_add_fusion), calls=%async_computation | async-start | bytes 1572864 | tf_op jit(solution)/shard_map/all_to_all | solution.py:43
  50.1 15.1 %all-gather.2.cloned.1.call-done = f32[1024,1024]{1,0:T(8,128)} async-done(((f32[32,1024]{1,0:T(8,128)}), f32[1024,1024]{1,0:T(8,128)}) %all-gather.2.cloned.1.call-update) | async-done | bytes 4194320 | tf_op jit(solution)/shard_map/all_gather | solution.py:92
  65.2 0.0 copy-done.2
  65.2 14.9 %fusion.3 = f32[96,16,1024]{2,1,0:T(8,128)} fusion(f32[1024,1024]{1,0:T(8,128)} %all-gather.2.cloned.1.call-done, f32[96,16,1024]{2,1,0:T(8,128)} %amp_ref.1, f32[96,16]{1,0:T(8,128)S(1)} %copy-done.2), kind=kOutput, calls=%fused_computation.3 | convolution fusion | flops 9666822144 | bytes 16783360 | tf_op jit(solution)/shard_map/dot_general | solution.py:90
  80.0 0.0 all-to-all-done
  80.0 0.7 reduce_sum.9
  (1 shorter events, 0.0 us)
Async XLA Ops:
  7.2 1.6 %copy-start = (f32[128,32,128]{2,1,0:T(8,128)S(1)}, f32[128,32,128]{2,1,0:T(8,128)}, u32[]{:S(2)}) copy-start(f32[128,32,128]{2,1,0:T(8,128)} %param.7) | copy-start | bytes 6291460
  7.2 58.0 %all-gather.2.cloned.1.call-start = ((), (), s32[]{:S(2)}) async-start(), calls=%async_computation.1 | async-start | bytes 4325376 | tf_op jit(solution)/shard_map/all_gather | solution.py:92
  8.8 19.7 %collective-permute-start = (f32[16,32,128]{2,1,0:T(8,128)S(1)}, f32[16,32,128]{2,1,0:T(8,128)S(1)}, u32[]{:S(2)}, u32[]{:S(2)}) collective-permute-start(f32[16,32,128]{2,1,0:T(8,128)S(1)} %constant_dynamic-slice_fusion), channel_id=1, source_target_pairs={{0,3},{4,7},{8,11},{12,15},{16,19},{20,23},{24,27},{28,31},{33,32}... | collective-permute-start | bytes 786440 | tf_op jit(solution)/shard_map/ppermute | solution.py:29
  14.0 14.4 %collective-permute-start.1 = (f32[16,32,128]{2,1,0:T(8,128)S(1)}, f32[16,32,128]{2,1,0:T(8,128)S(1)}, u32[]{:S(2)}, u32[]{:S(2)}) collective-permute-start(f32[16,32,128]{2,1,0:T(8,128)S(1)} %constant_dynamic-slice_fusion), channel_id=1, source_target_pairs={{0,2},{4,6},{8,10},{12,14},{16,18},{20,22},{24,26},{28,30},{33,35}... | collective-permute-start | bytes 786440 | tf_op jit(solution)/shard_map/ppermute | solution.py:29
  15.3 13.1 %collective-permute-start.2 = (f32[16,32,128]{2,1,0:T(8,128)S(1)}, f32[16,32,128]{2,1,0:T(8,128)S(1)}, u32[]{:S(2)}, u32[]{:S(2)}) collective-permute-start(f32[16,32,128]{2,1,0:T(8,128)S(1)} %constant_dynamic-slice_fusion), channel_id=1, source_target_pairs={{0,1},{4,5},{8,9},{12,13},{16,17},{20,21},{24,25},{28,29},{33,34},... | collective-permute-start | bytes 786440 | tf_op jit(solution)/shard_map/ppermute | solution.py:29
  28.5 36.7 %copy-start.2 = (f32[96,16]{1,0:T(8,128)S(1)}, f32[96,16]{1,0:T(8,128)}, u32[]{:S(2)}) copy-start(f32[96,16]{1,0:T(8,128)} %convert_element_type.3.live_ref) | copy-start | bytes 18436
  37.6 1.1 %copy-start.1 = (f32[16,2,96,128]{3,2,1,0:T(8,128)}, f32[16,2,96,128]{3,2,1,0:T(8,128)S(1)}, u32[]{:S(2)}) copy-start(f32[16,2,96,128]{3,2,1,0:T(8,128)S(1)} %convolution_bitcast_fusion) | copy-start | bytes 4718596
  39.7 3.1 %collective-permute-start.3 = (f32[16,96,128]{2,1,0:T(8,128)}, f32[16,96,128]{2,1,0:T(8,128)S(1)}, u32[]{:S(2)}, u32[]{:S(2)}) collective-permute-start(f32[16,96,128]{2,1,0:T(8,128)} %dynamic-slice_bitcast_fusion), channel_id=1, source_target_pairs={{0,4},{4,0},{1,5},{5,1},{2,6},{6,2},{3,7},{7,3},{8,12},{12,8},{9,1... | collective-permute-start | bytes 2359304 | tf_op jit(solution)/shard_map/ppermute | solution.py:42
  45.0 35.0 %all-to-all-start = ((f32[16,96,128]{2,1,0:T(8,128)}), f32[16,96,128]{2,1,0:T(8,128)S(1)}, u32[]{:S(2)}, u32[]{:S(2)}) async-start(f32[16,96,128]{2,1,0:T(8,128)} %bitcast_add_fusion), calls=%async_computation | async-start | bytes 1572864 | tf_op jit(solution)/shard_map/all_to_all | solution.py:43
Sparse Core Ops, SparseCore 0:
  10.2 54.8 all-gather.1

commit v10 on v9

--- a/solution.py
+++ b/solution.py
@@ -67,6 +67,25 @@
     )(live, amplitudes)
 
 
+def gathered_integrals(ladder_integrals):
+    cores = lax.axis_size("core")
+    core = lax.axis_index("core")
+    chips = lax.axis_size(CHIPS)
+    chip = lax.axis_index(CHIPS)
+    sibling = lax.ppermute(ladder_integrals, "core", [(c, (c + 1) % cores) for c in range(cores)])
+    pair = jnp.where(core == 0, jnp.concatenate([ladder_integrals, sibling], 0), jnp.concatenate([sibling, ladder_integrals], 0))
+    half = pair.shape[1] // cores
+    mine = lax.dynamic_slice_in_dim(pair, core * half, half, axis=1)
+    blocks = [mine]
+    for shift in range(1, chips):
+        blocks.append(lax.ppermute(mine, CHIPS, [(q, (q + shift) % chips) for q in range(chips)]))
+    by_shift = jnp.stack(blocks, 0)
+    by_chip = jnp.take(by_shift, (chip - jnp.arange(chips)) % chips, axis=0)
+    column = by_chip.reshape(-1, half)
+    other = lax.ppermute(column, "core", [(c, (c + 1) % cores) for c in range(cores)])
+    return jnp.where(core == 0, jnp.concatenate([column, other], 1), jnp.concatenate([other, column], 1))
+
+
 def local(amplitudes, pair_live, ladder_integrals, cycle_integrals):
     live = pair_live.astype(jnp.float32)
     screened = amplitudes * live[:, :, None]
@@ -89,7 +108,7 @@
     flat = screened.reshape(first_rows * second_rows, width)
     ladder = jnp.dot(
         flat,
-        lax.all_gather(ladder_integrals, PARTS, axis=0, tiled=True),
+        gathered_integrals(ladder_integrals),
         precision=lax.Precision.HIGH,
         preferred_element_type=jnp.float32,
     )

time: 88.2 us -> 117 us (1.33)
  starting transfers between devices: 13.9 us -> 48.6 us
  between operations: 14.2 us -> 0.84 us
  local copies, waits for them, and re-layouts: 3.72 us -> 15.9 us
  waiting for transfers between devices: 17.9 us -> 7.07 us
  other arithmetic: 3.54 us -> 8.25 us
  matrix products: 24 us -> 25.4 us
    ppermute x0 -> x17, starting transfers between devices: none -> 36.3 us  [the longest x15 25.2 us: gathered_integrals(): lax.ppermute(mine, CHIPS, [(q, (q + shift) % chips) for q in range(chips)])]
    all_gather x1 -> x0, waiting for transfers between devices: 15.1 us -> none  [local(): lax.all_gather(ladder_integrals, PARTS, axis=0, tiled=True)]
    unnamed x7 -> x23, local copies, waits for them, and re-layouts: 2.76 us -> 10.5 us
    ppermute x0 -> x17, waiting for transfers between devices: none -> 4.84 us  [the longest x15 3.66 us: gathered_integrals(): lax.ppermute(mine, CHIPS, [(q, (q + shift) % chips) for q in range(chips)])]
    gather x0 -> x1, local copies, waits for them, and re-layouts: none -> 3.6 us  [gathered_integrals(): by_chip = jnp.take(by_shift, (chip - jnp.arange(chips)) % chips, axis=0)]
    select_n x0 -> x2, other arithmetic: none -> 3.24 us  [gathered_integrals(): by_chip = jnp.take(by_shift, (chip - jnp.arange(chips)) % chips, axis=0)]
    unnamed x0 -> x1, other arithmetic: none -> 1.6 us
    dot_general x1, matrix products: 14.9 us -> 16.2 us  [local(): jnp.dot(flat, gathered_integrals(ladder_integrals), precision=lax.Precisi...]
  transfers between devices with their start and end apart: 6 -> 22, of which waited for: 2 -> 6; matrix products, arithmetic and copies ran while one was open for 33% -> 33% of each run, Pallas kernels for 12% -> 9%
where the time goes in v10:
time: 117 us; the launch traced here: 116 us
  starting transfers between devices  48.6 us (42%)
  matrix products  25.4 us (22%)
  local copies, waits for them, and re-layouts  15.9 us (14%)
  Pallas kernels  10.4 us (9%)
  other arithmetic  8.25 us (7%)
  waiting for transfers between devices  7.07 us (6%)
    ppermute x15, starting transfers between devices, gathered_integrals(): lax.ppermute(mine, CHIPS, [(q, (q + shift) % chips) for q in range(chips)])  25.2 us
    dot_general x1, matrix products, local(): jnp.dot(flat, gathered_integrals(ladder_integrals), precision=lax.Precisi...  16.2 us
    unnamed x23, local copies, waits for them, and re-layouts  10.5 us
    pallas_call x1, Pallas kernels, screened_by_a(): pl.pallas_call(screen_kernel, grid=(width // lanes,), out_shape=jax.Shape...  10.4 us
    ppermute x1, starting transfers between devices, gathered_integrals(): lax.ppermute(column, 'core', [(c, (c + 1) % cores) for c in range(cores)])  9.72 us
    dot_general x1, matrix products, local(): jnp.einsum('akci,kcm->aim', split, weights, precision=lax.Precision.HIGH,...  9.14 us
    ppermute x3, starting transfers between devices, cycle_piece(): got = lax.ppermute(piece, PARTS + ('vir',), pairs)  7.01 us
    all_to_all x1, starting transfers between devices, cycle_reduce(): lax.all_to_all(chip_share, CHIPS, split_axis=0, concat_axis=0, tiled=True)  4.95 us
  transfers between devices with their start and end apart: 22, of which 6 were waited for; matrix products, arithmetic and copies ran while one was open for 33% of the time, Pallas kernels for 9%

profile of v10, /device:TPU:1, one launch (start us, length us, event | category | flops | bytes accessed | tf_op | source)
XLA Modules:
  0.0 116.4 jit_solution(6103777085018715605)
XLA Ops:
  0.6 1.5 %collective-permute-start = (f32[32,1024]{1,0:T(8,128)}, f32[32,1024]{1,0:T(8,128)S(1)}, u32[]{:S(2)}, u32[]{:S(2)}) collective-permute-start(f32[32,1024]{1,0:T(8,128)} %param.6), channel_id=1, source_target_pairs={{0,4},{4,0},{1,5},{5,1},{2,6},{6,2},{3,7},{7,3},{8,12},{12,8},{9,1... | collective-permute-start | bytes 393224 | tf_op jit(solution)/shard_map/ppermute | solution.py:75
  2.1 1.2 %collective-permute-done = f32[32,1024]{1,0:T(8,128)S(1)} collective-permute-done((f32[32,1024]{1,0:T(8,128)}, f32[32,1024]{1,0:T(8,128)S(1)}, u32[]{:S(2)}, u32[]{:S(2)}) %collective-permute-start) | collective-permute-done | bytes 131104 | tf_op jit(solution)/shard_map/ppermute | solution.py:75
  3.3 1.6 %bitcast_dynamic-update-slice_fusion.15 = (f32[16,64,512]{2,1,0:T(8,128)}, f32[64,512]{1,0:T(8,128)S(1)}) fusion(s32[]{:T(128)S(6)} %select_n.115, f32[32,1024]{1,0:T(8,128)} %param.6, f32[32,1024]{1,0:T(8,128)S(1)} %collective-permute-done, pred[]{:T(512)S(6)} %eq.21), kind=kLoop, calls=%fused_computation.43 | loop fusion | flops 98303 | bytes 524293
  4.9 1.7 %collective-permute-start.1 = (f32[64,512]{1,0:T(8,128)S(1)}, f32[64,512]{1,0:T(8,128)S(1)}, u32[]{:S(2)}, u32[]{:S(2)}) collective-permute-start(f32[64,512]{1,0:T(8,128)S(1)} %get-tuple-element.7), channel_id=1, source_target_pairs={{0,8},{8,16},{16,24},{24,32},{32,40},{40,48},{48,56},{56,64},{64,7... | collective-permute-start | bytes 393224 | tf_op jit(solution)/shard_map/ppermute | solution.py:81
  6.9 3.3 %collective-permute-start.2 = (f32[64,512]{1,0:T(8,128)S(1)}, f32[64,512]{1,0:T(8,128)S(1)}, u32[]{:S(2)}, u32[]{:S(2)}) collective-permute-start(f32[64,512]{1,0:T(8,128)S(1)} %get-tuple-element.7), channel_id=1, source_target_pairs={{0,16},{8,24},{16,32},{24,40},{32,48},{40,56},{48,64},{56,72},{64,... | collective-permute-start | bytes 393224 | tf_op jit(solution)/shard_map/ppermute | solution.py:81
  10.2 1.7 %collective-permute-start.3 = (f32[64,512]{1,0:T(8,128)S(1)}, f32[64,512]{1,0:T(8,128)S(1)}, u32[]{:S(2)}, u32[]{:S(2)}) collective-permute-start(f32[64,512]{1,0:T(8,128)S(1)} %get-tuple-element.7), channel_id=1, source_target_pairs={{0,24},{8,32},{16,40},{24,48},{32,56},{40,64},{48,72},{56,80},{64,... | collective-permute-start | bytes 393224 | tf_op jit(solution)/shard_map/ppermute | solution.py:81
  11.9 1.3 %collective-permute-start.4 = (f32[64,512]{1,0:T(8,128)S(1)}, f32[64,512]{1,0:T(8,128)S(1)}, u32[]{:S(2)}, u32[]{:S(2)}) collective-permute-start(f32[64,512]{1,0:T(8,128)S(1)} %get-tuple-element.7), channel_id=1, source_target_pairs={{0,32},{8,40},{16,48},{24,56},{32,64},{40,72},{48,80},{56,88},{64,... | collective-permute-start | bytes 393224 | tf_op jit(solution)/shard_map/ppermute | solution.py:81
  13.2 1.5 %collective-permute-start.5 = (f32[64,512]{1,0:T(8,128)S(1)}, f32[64,512]{1,0:T(8,128)S(1)}, u32[]{:S(2)}, u32[]{:S(2)}) collective-permute-start(f32[64,512]{1,0:T(8,128)S(1)} %get-tuple-element.7), channel_id=1, source_target_pairs={{0,40},{8,48},{16,56},{24,64},{32,72},{40,80},{48,88},{56,96},{64,... | collective-permute-start | bytes 393224 | tf_op jit(solution)/shard_map/ppermute | solution.py:81
  15.8 0.7 bitcast_dynamic-update-slice_fusion.14
  17.0 1.9 %collective-permute-start.7 = (f32[64,512]{1,0:T(8,128)S(1)}, f32[64,512]{1,0:T(8,128)S(1)}, u32[]{:S(2)}, u32[]{:S(2)}) collective-permute-start(f32[64,512]{1,0:T(8,128)S(1)} %get-tuple-element.7), channel_id=1, source_target_pairs={{0,56},{8,64},{16,72},{24,80},{32,88},{40,96},{48,104},{56,112},{6... | collective-permute-start | bytes 393224 | tf_op jit(solution)/shard_map/ppermute | solution.py:81
  18.8 0.7 bitcast_dynamic-update-slice_fusion.13
  19.5 2.2 %collective-permute-start.8 = (f32[64,512]{1,0:T(8,128)S(1)}, f32[64,512]{1,0:T(8,128)S(1)}, u32[]{:S(2)}, u32[]{:S(2)}) collective-permute-start(f32[64,512]{1,0:T(8,128)S(1)} %get-tuple-element.7), channel_id=1, source_target_pairs={{0,64},{8,72},{16,80},{24,88},{32,96},{40,104},{48,112},{56,120},{... | collective-permute-start | bytes 393224 | tf_op jit(solution)/shard_map/ppermute | solution.py:81
  21.7 0.7 bitcast_dynamic-update-slice_fusion.12
  22.4 1.2 %collective-permute-start.9 = (f32[64,512]{1,0:T(8,128)S(1)}, f32[64,512]{1,0:T(8,128)S(1)}, u32[]{:S(2)}, u32[]{:S(2)}) collective-permute-start(f32[64,512]{1,0:T(8,128)S(1)} %get-tuple-element.7), channel_id=1, source_target_pairs={{0,72},{8,80},{16,88},{24,96},{32,104},{40,112},{48,120},{56,0},{6... | collective-permute-start | bytes 393224 | tf_op jit(solution)/shard_map/ppermute | solution.py:81
  23.6 0.7 bitcast_dynamic-update-slice_fusion.11
  24.3 1.7 %collective-permute-done.5 = f32[64,512]{1,0:T(8,128)S(1)} collective-permute-done((f32[64,512]{1,0:T(8,128)S(1)}, f32[64,512]{1,0:T(8,128)S(1)}, u32[]{:S(2)}, u32[]{:S(2)}) %collective-permute-start.5) | collective-permute-done | bytes 131104 | tf_op jit(solution)/shard_map/ppermute | solution.py:81
  25.9 2.4 %collective-permute-start.10 = (f32[64,512]{1,0:T(8,128)S(1)}, f32[64,512]{1,0:T(8,128)S(1)}, u32[]{:S(2)}, u32[]{:S(2)}) collective-permute-start(f32[64,512]{1,0:T(8,128)S(1)} %get-tuple-element.7), channel_id=1, source_target_pairs={{0,80},{8,88},{16,96},{24,104},{32,112},{40,120},{48,0},{56,8},{64... | collective-permute-start | bytes 393224 | tf_op jit(solution)/shard_map/ppermute | solution.py:81
  28.3 0.7 bitcast_dynamic-update-slice_fusion.10
  28.9 2.4 %collective-permute-start.11 = (f32[64,512]{1,0:T(8,128)S(1)}, f32[64,512]{1,0:T(8,128)S(1)}, u32[]{:S(2)}, u32[]{:S(2)}) collective-permute-start(f32[64,512]{1,0:T(8,128)S(1)} %get-tuple-element.7), channel_id=1, source_target_pairs={{0,88},{8,96},{16,104},{24,112},{32,120},{40,0},{48,8},{56,16},{64... | collective-permute-start | bytes 393224 | tf_op jit(solution)/shard_map/ppermute | solution.py:81
  31.3 0.7 bitcast_dynamic-update-slice_fusion.9
  32.0 2.1 %collective-permute-start.12 = (f32[64,512]{1,0:T(8,128)S(1)}, f32[64,512]{1,0:T(8,128)S(1)}, u32[]{:S(2)}, u32[]{:S(2)}) collective-permute-start(f32[64,512]{1,0:T(8,128)S(1)} %get-tuple-element.7), channel_id=1, source_target_pairs={{0,96},{8,104},{16,112},{24,120},{32,0},{40,8},{48,16},{56,24},{64... | collective-permute-start | bytes 393224 | tf_op jit(solution)/shard_map/ppermute | solution.py:81
  34.1 0.7 bitcast_dynamic-update-slice_fusion.8
  34.7 0.7 bitcast_dynamic-update-slice_fusion.7
  35.4 1.2 %collective-permute-start.14 = (f32[64,512]{1,0:T(8,128)S(1)}, f32[64,512]{1,0:T(8,128)S(1)}, u32[]{:S(2)}, u32[]{:S(2)}) collective-permute-start(f32[64,512]{1,0:T(8,128)S(1)} %get-tuple-element.7), channel_id=1, source_target_pairs={{0,112},{8,120},{16,0},{24,8},{32,16},{40,24},{48,32},{56,40},{64,... | collective-permute-start | bytes 393224 | tf_op jit(solution)/shard_map/ppermute | solution.py:81
  36.6 0.7 bitcast_dynamic-update-slice_fusion.6
  37.3 1.6 %collective-permute-start.15 = (f32[64,512]{1,0:T(8,128)S(1)}, f32[64,512]{1,0:T(8,128)S(1)}, u32[]{:S(2)}, u32[]{:S(2)}) collective-permute-start(f32[64,512]{1,0:T(8,128)S(1)} %get-tuple-element.7), channel_id=1, source_target_pairs={{0,120},{8,0},{16,8},{24,16},{32,24},{40,32},{48,40},{56,48},{64,5... | collective-permute-start | bytes 393224 | tf_op jit(solution)/shard_map/ppermute | solution.py:81
  38.9 0.7 bitcast_dynamic-update-slice_fusion.5
  39.6 0.7 bitcast_dynamic-update-slice_fusion.4
  40.3 0.7 bitcast_dynamic-update-slice_fusion.3
  40.9 0.7 bitcast_dynamic-update-slice_fusion.2
  41.6 0.7 bitcast_dynamic-update-slice_fusion.1
  42.3 1.0 collective-permute-done.15
  43.2 0.7 bitcast_dynamic-update-slice_fusion
  43.9 3.6 %gather_fusion = f32[16,64,512]{2,1,0:T(8,128)} fusion(f32[16,64,512]{2,1,0:T(8,128)} %bitcast_dynamic-update-slice_fusion, s32[1024]{0:T(1024)S(1)} %pad_clamp_fusion), kind=kCustom, calls=%fused_computation | custom fusion | bytes 4194368 | tf_op jit(solution)/shard_map/jit(_take)/gather | solution.py:83
  47.5 3.2 %bitcast_select_fusion = f32[1024,512]{1,0:T(8,128)} fusion(f32[16,64,512]{2,1,0:T(8,128)} %gather_fusion, pred[1024]{0:T(1024)(128)(4,1)S(1)} %broadcast_in_dim.20), kind=kLoop, calls=%fused_computation.12 | loop fusion | flops 524288 | bytes 4195328 | tf_op jit(solution)/shard_map/jit(_take)/select_n | solution.py:83
  50.7 9.7 %collective-permute-start.16 = (f32[1024,512]{1,0:T(8,128)}, f32[1024,512]{1,0:T(8,128)}, u32[]{:S(2)}, u32[]{:S(2)}) collective-permute-start(f32[1024,512]{1,0:T(8,128)} %bitcast_select_fusion), channel_id=1, source_target_pairs={{0,4},{4,0},{1,5},{5,1},{2,6},{6,2},{3,7},{7,3},{8,12},{12,8},{9,1... | collective-permute-start | bytes 6291464 | tf_op jit(solution)/shard_map/ppermute | solution.py:85
  60.5 4.4 %collective-permute-start.17 = (f32[16,32,128]{2,1,0:T(8,128)S(1)}, f32[16,32,128]{2,1,0:T(8,128)S(1)}, u32[]{:S(2)}, u32[]{:S(2)}) collective-permute-start(f32[16,32,128]{2,1,0:T(8,128)S(1)} %constant_dynamic-slice_fusion), channel_id=1, source_target_pairs={{0,3},{4,7},{8,11},{12,15},{16,19},{20,23},{24,27},{28,31},{33,32}... | collective-permute-start | bytes 786440 | tf_op jit(solution)/shard_map/ppermute | solution.py:29
  64.9 1.3 %collective-permute-start.18 = (f32[16,32,128]{2,1,0:T(8,128)S(1)}, f32[16,32,128]{2,1,0:T(8,128)S(1)}, u32[]{:S(2)}, u32[]{:S(2)}) collective-permute-start(f32[16,32,128]{2,1,0:T(8,128)S(1)} %constant_dynamic-slice_fusion), channel_id=1, source_target_pairs={{0,2},{4,6},{8,10},{12,14},{16,18},{20,22},{24,26},{28,30},{33,35}... | collective-permute-start | bytes 786440 | tf_op jit(solution)/shard_map/ppermute | solution.py:29
  66.2 1.3 %collective-permute-start.19 = (f32[16,32,128]{2,1,0:T(8,128)S(1)}, f32[16,32,128]{2,1,0:T(8,128)S(1)}, u32[]{:S(2)}, u32[]{:S(2)}) collective-permute-start(f32[16,32,128]{2,1,0:T(8,128)S(1)} %constant_dynamic-slice_fusion), channel_id=1, source_target_pairs={{0,1},{4,5},{8,9},{12,13},{16,17},{20,21},{24,25},{28,29},{33,34},... | collective-permute-start | bytes 786440 | tf_op jit(solution)/shard_map/ppermute | solution.py:29
  68.3 10.4 %shard_map.59 = f32[32,512,96]{2,1,0:T(8,128)} custom-call(f32[96,16]{1,0:T(8,128)} %convert_element_type.3.live_ref, f32[96,16,1024]{2,1,0:T(8,128)} %amp_ref.1), custom_call_target="tpu_custom_call" | custom-call | tf_op jit(solution)/shard_map/pallas_call | solution.py:58
  78.7 9.1 %convolution_bitcast_fusion = f32[16,2,96,128]{3,2,1,0:T(8,128)S(1)} fusion(f32[16,2,96,32,16]{2,3,4,1,0:T(8,128)} %bitcast.60, f32[16,32,128]{2,1,0:T(8,128)S(1)} %collective-permute-done.17, f32[16,32,128]{2,1,0:T(8,128)S(1)} %collective-permute-done.18, f32[16,32,128]{2,1,0:T(8,128)S(1)} %collective-permute-done.19, ...), kind=kOutput, calls=%fused_computation.14 | convolution fusion | flops 1208156160 | bytes 8912899 | tf_op jit(solution)/shard_map/akci,kcm->aim/dot_general | solution.py:99
  87.9 1.1 copy-done.1
  89.0 0.9 dynamic-slice_bitcast_fusion
  90.2 2.2 %collective-permute-done.20 = f32[16,96,128]{2,1,0:T(8,128)S(1)} collective-permute-done((f32[16,96,128]{2,1,0:T(8,128)}, f32[16,96,128]{2,1,0:T(8,128)S(1)}, u32[]{:S(2)}, u32[]{:S(2)}) %collective-permute-start.20) | collective-permute-done | bytes 786464 | tf_op jit(solution)/shard_map/ppermute | solution.py:42
  92.4 2.1 %bitcast_add_fusion = f32[16,96,128]{2,1,0:T(8,128)} fusion(f32[16,96,128]{2,1,0:T(8,128)S(1)} %collective-permute-done.20, f32[16,2,96,128]{3,2,1,0:T(8,128)} %copy-done.1, s32[]{:T(128)S(6)} %select_n.130), kind=kLoop, calls=%fused_computation.15 | loop fusion | flops 196608 | bytes 2359300 | tf_op jit(solution)/shard_map/add | solution.py:42
  94.5 5.0 %all-to-all-start = ((f32[16,96,128]{2,1,0:T(8,128)}), f32[16,96,128]{2,1,0:T(8,128)S(1)}, u32[]{:S(2)}, u32[]{:S(2)}) async-start(f32[16,96,128]{2,1,0:T(8,128)} %bitcast_add_fusion), calls=%async_computation | async-start | bytes 1572864 | tf_op jit(solution)/shard_map/all_to_all | solution.py:43
  99.5 16.2 %fusion.9 = f32[96,16,1024]{2,1,0:T(8,128)} fusion(f32[1024,512]{1,0:T(8,128)} %collective-permute-done.16, f32[1024,512]{1,0:T(8,128)} %bitcast_select_fusion, f32[96,16,1024]{2,1,0:T(8,128)} %amp_ref.1, f32[96,16]{1,0:T(8,128)S(1)} %copy-done.2, pred[]{:T(512)S(6)} %eq.21), kind=kOutput, calls=%fused_computation.10 | convolution fusion | flops 9669967872 | bytes 16783360 | tf_op jit(solution)/shard_map/dot_general | solution.py:109
  115.7 0.7 reduce_sum.9
  (36 shorter events, 2.9 us)
Async XLA Ops:
  0.6 59.8 %copy-start = (f32[128,32,128]{2,1,0:T(8,128)S(1)}, f32[128,32,128]{2,1,0:T(8,128)}, u32[]{:S(2)}) copy-start(f32[128,32,128]{2,1,0:T(8,128)} %param.7) | copy-start | bytes 6291460
  0.6 2.7 %collective-permute-start = (f32[32,1024]{1,0:T(8,128)}, f32[32,1024]{1,0:T(8,128)S(1)}, u32[]{:S(2)}, u32[]{:S(2)}) collective-permute-start(f32[32,1024]{1,0:T(8,128)} %param.6), channel_id=1, source_target_pairs={{0,4},{4,0},{1,5},{5,1},{2,6},{6,2},{3,7},{7,3},{8,12},{12,8},{9,1... | collective-permute-start | bytes 393224 | tf_op jit(solution)/shard_map/ppermute | solution.py:75
  4.9 10.3 %collective-permute-start.1 = (f32[64,512]{1,0:T(8,128)S(1)}, f32[64,512]{1,0:T(8,128)S(1)}, u32[]{:S(2)}, u32[]{:S(2)}) collective-permute-start(f32[64,512]{1,0:T(8,128)S(1)} %get-tuple-element.7), channel_id=1, source_target_pairs={{0,8},{8,16},{16,24},{24,32},{32,40},{40,48},{48,56},{56,64},{64,7... | collective-permute-start | bytes 393224 | tf_op jit(solution)/shard_map/ppermute | solution.py:81
  6.9 10.1 %collective-permute-start.2 = (f32[64,512]{1,0:T(8,128)S(1)}, f32[64,512]{1,0:T(8,128)S(1)}, u32[]{:S(2)}, u32[]{:S(2)}) collective-permute-start(f32[64,512]{1,0:T(8,128)S(1)} %get-tuple-element.7), channel_id=1, source_target_pairs={{0,16},{8,24},{16,32},{24,40},{32,48},{40,56},{48,64},{56,72},{64,... | collective-permute-start | bytes 393224 | tf_op jit(solution)/shard_map/ppermute | solution.py:81
  10.2 9.3 %collective-permute-start.3 = (f32[64,512]{1,0:T(8,128)S(1)}, f32[64,512]{1,0:T(8,128)S(1)}, u32[]{:S(2)}, u32[]{:S(2)}) collective-permute-start(f32[64,512]{1,0:T(8,128)S(1)} %get-tuple-element.7), channel_id=1, source_target_pairs={{0,24},{8,32},{16,40},{24,48},{32,56},{40,64},{48,72},{56,80},{64,... | collective-permute-start | bytes 393224 | tf_op jit(solution)/shard_map/ppermute | solution.py:81
  11.9 10.4 %collective-permute-start.4 = (f32[64,512]{1,0:T(8,128)S(1)}, f32[64,512]{1,0:T(8,128)S(1)}, u32[]{:S(2)}, u32[]{:S(2)}) collective-permute-start(f32[64,512]{1,0:T(8,128)S(1)} %get-tuple-element.7), channel_id=1, source_target_pairs={{0,32},{8,40},{16,48},{24,56},{32,64},{40,72},{48,80},{56,88},{64,... | collective-permute-start | bytes 393224 | tf_op jit(solution)/shard_map/ppermute | solution.py:81
  13.2 12.7 %collective-permute-start.5 = (f32[64,512]{1,0:T(8,128)S(1)}, f32[64,512]{1,0:T(8,128)S(1)}, u32[]{:S(2)}, u32[]{:S(2)}) collective-permute-start(f32[64,512]{1,0:T(8,128)S(1)} %get-tuple-element.7), channel_id=1, source_target_pairs={{0,40},{8,48},{16,56},{24,64},{32,72},{40,80},{48,88},{56,96},{64,... | collective-permute-start | bytes 393224 | tf_op jit(solution)/shard_map/ppermute | solution.py:81
  15.2 13.7 %collective-permute-start.6 = (f32[64,512]{1,0:T(8,128)S(1)}, f32[64,512]{1,0:T(8,128)S(1)}, u32[]{:S(2)}, u32[]{:S(2)}) collective-permute-start(f32[64,512]{1,0:T(8,128)S(1)} %get-tuple-element.7), channel_id=1, source_target_pairs={{0,48},{8,56},{16,64},{24,72},{32,80},{40,88},{48,96},{56,104},{64... | collective-permute-start | bytes 393224 | tf_op jit(solution)/shard_map/ppermute | solution.py:81
  17.0 15.0 %collective-permute-start.7 = (f32[64,512]{1,0:T(8,128)S(1)}, f32[64,512]{1,0:T(8,128)S(1)}, u32[]{:S(2)}, u32[]{:S(2)}) collective-permute-start(f32[64,512]{1,0:T(8,128)S(1)} %get-tuple-element.7), channel_id=1, source_target_pairs={{0,56},{8,64},{16,72},{24,80},{32,88},{40,96},{48,104},{56,112},{6... | collective-permute-start | bytes 393224 | tf_op jit(solution)/shard_map/ppermute | solution.py:81
  19.5 15.2 %collective-permute-start.8 = (f32[64,512]{1,0:T(8,128)S(1)}, f32[64,512]{1,0:T(8,128)S(1)}, u32[]{:S(2)}, u32[]{:S(2)}) collective-permute-start(f32[64,512]{1,0:T(8,128)S(1)} %get-tuple-element.7), channel_id=1, source_target_pairs={{0,64},{8,72},{16,80},{24,88},{32,96},{40,104},{48,112},{56,120},{... | collective-permute-start | bytes 393224 | tf_op jit(solution)/shard_map/ppermute | solution.py:81
  22.4 13.0 %collective-permute-start.9 = (f32[64,512]{1,0:T(8,128)S(1)}, f32[64,512]{1,0:T(8,128)S(1)}, u32[]{:S(2)}, u32[]{:S(2)}) collective-permute-start(f32[64,512]{1,0:T(8,128)S(1)} %get-tuple-element.7), channel_id=1, source_target_pairs={{0,72},{8,80},{16,88},{24,96},{32,104},{40,112},{48,120},{56,0},{6... | collective-permute-start | bytes 393224 | tf_op jit(solution)/shard_map/ppermute | solution.py:81
  25.9 11.3 %collective-permute-start.10 = (f32[64,512]{1,0:T(8,128)S(1)}, f32[64,512]{1,0:T(8,128)S(1)}, u32[]{:S(2)}, u32[]{:S(2)}) collective-permute-start(f32[64,512]{1,0:T(8,128)S(1)} %get-tuple-element.7), channel_id=1, source_target_pairs={{0,80},{8,88},{16,96},{24,104},{32,112},{40,120},{48,0},{56,8},{64... | collective-permute-start | bytes 393224 | tf_op jit(solution)/shard_map/ppermute | solution.py:81
  28.9 10.6 %collective-permute-start.11 = (f32[64,512]{1,0:T(8,128)S(1)}, f32[64,512]{1,0:T(8,128)S(1)}, u32[]{:S(2)}, u32[]{:S(2)}) collective-permute-start(f32[64,512]{1,0:T(8,128)S(1)} %get-tuple-element.7), channel_id=1, source_target_pairs={{0,88},{8,96},{16,104},{24,112},{32,120},{40,0},{48,8},{56,16},{64... | collective-permute-start | bytes 393224 | tf_op jit(solution)/shard_map/ppermute | solution.py:81
  32.0 8.2 %collective-permute-start.12 = (f32[64,512]{1,0:T(8,128)S(1)}, f32[64,512]{1,0:T(8,128)S(1)}, u32[]{:S(2)}, u32[]{:S(2)}) collective-permute-start(f32[64,512]{1,0:T(8,128)S(1)} %get-tuple-element.7), channel_id=1, source_target_pairs={{0,96},{8,104},{16,112},{24,120},{32,0},{40,8},{48,16},{56,24},{64... | collective-permute-start | bytes 393224 | tf_op jit(solution)/shard_map/ppermute | solution.py:81
  34.7 6.2 %collective-permute-start.13 = (f32[64,512]{1,0:T(8,128)S(1)}, f32[64,512]{1,0:T(8,128)S(1)}, u32[]{:S(2)}, u32[]{:S(2)}) collective-permute-start(f32[64,512]{1,0:T(8,128)S(1)} %get-tuple-element.7), channel_id=1, source_target_pairs={{0,104},{8,112},{16,120},{24,0},{32,8},{40,16},{48,24},{56,32},{64... | collective-permute-start | bytes 393224 | tf_op jit(solution)/shard_map/ppermute | solution.py:81
  35.4 6.2 %collective-permute-start.14 = (f32[64,512]{1,0:T(8,128)S(1)}, f32[64,512]{1,0:T(8,128)S(1)}, u32[]{:S(2)}, u32[]{:S(2)}) collective-permute-start(f32[64,512]{1,0:T(8,128)S(1)} %get-tuple-element.7), channel_id=1, source_target_pairs={{0,112},{8,120},{16,0},{24,8},{32,16},{40,24},{48,32},{56,40},{64,... | collective-permute-start | bytes 393224 | tf_op jit(solution)/shard_map/ppermute | solution.py:81
  37.3 6.0 %collective-permute-start.15 = (f32[64,512]{1,0:T(8,128)S(1)}, f32[64,512]{1,0:T(8,128)S(1)}, u32[]{:S(2)}, u32[]{:S(2)}) collective-permute-start(f32[64,512]{1,0:T(8,128)S(1)} %get-tuple-element.7), channel_id=1, source_target_pairs={{0,120},{8,0},{16,8},{24,16},{32,24},{40,32},{48,40},{56,48},{64,5... | collective-permute-start | bytes 393224 | tf_op jit(solution)/shard_map/ppermute | solution.py:81
  47.5 20.1 %copy-start.3 = (s32[96,16]{0,1:T(8,128)S(1)}, s32[96,16]{0,1:T(8,128)}, u32[]{:S(2)}) copy-start(s32[96,16]{0,1:T(8,128)} %param.5) | copy-start | bytes 18436
  50.7 48.7 %collective-permute-start.16 = (f32[1024,512]{1,0:T(8,128)}, f32[1024,512]{1,0:T(8,128)}, u32[]{:S(2)}, u32[]{:S(2)}) collective-permute-start(f32[1024,512]{1,0:T(8,128)} %bitcast_select_fusion), channel_id=1, source_target_pairs={{0,4},{4,0},{1,5},{5,1},{2,6},{6,2},{3,7},{7,3},{8,12},{12,8},{9,1... | collective-permute-start | bytes 6291464 | tf_op jit(solution)/shard_map/ppermute | solution.py:85
  60.5 18.2 %collective-permute-start.17 = (f32[16,32,128]{2,1,0:T(8,128)S(1)}, f32[16,32,128]{2,1,0:T(8,128)S(1)}, u32[]{:S(2)}, u32[]{:S(2)}) collective-permute-start(f32[16,32,128]{2,1,0:T(8,128)S(1)} %constant_dynamic-slice_fusion), channel_id=1, source_target_pairs={{0,3},{4,7},{8,11},{12,15},{16,19},{20,23},{24,27},{28,31},{33,32}... | collective-permute-start | bytes 786440 | tf_op jit(solution)/shard_map/ppermute | solution.py:29
  64.9 13.8 %collective-permute-start.18 = (f32[16,32,128]{2,1,0:T(8,128)S(1)}, f32[16,32,128]{2,1,0:T(8,128)S(1)}, u32[]{:S(2)}, u32[]{:S(2)}) collective-permute-start(f32[16,32,128]{2,1,0:T(8,128)S(1)} %constant_dynamic-slice_fusion), channel_id=1, source_target_pairs={{0,2},{4,6},{8,10},{12,14},{16,18},{20,22},{24,26},{28,30},{33,35}... | collective-permute-start | bytes 786440 | tf_op jit(solution)/shard_map/ppermute | solution.py:29
  66.2 12.5 %collective-permute-start.19 = (f32[16,32,128]{2,1,0:T(8,128)S(1)}, f32[16,32,128]{2,1,0:T(8,128)S(1)}, u32[]{:S(2)}, u32[]{:S(2)}) collective-permute-start(f32[16,32,128]{2,1,0:T(8,128)S(1)} %constant_dynamic-slice_fusion), channel_id=1, source_target_pairs={{0,1},{4,5},{8,9},{12,13},{16,17},{20,21},{24,25},{28,29},{33,34},... | collective-permute-start | bytes 786440 | tf_op jit(solution)/shard_map/ppermute | solution.py:29
  87.8 1.1 copy-start.1
  89.9 9.6 %copy-start.2 = (f32[96,16]{1,0:T(8,128)S(1)}, f32[96,16]{1,0:T(8,128)}, u32[]{:S(2)}) copy-start(f32[96,16]{1,0:T(8,128)} %convert_element_type.3.live_ref) | copy-start | bytes 18436
  89.9 2.5 %collective-permute-start.20 = (f32[16,96,128]{2,1,0:T(8,128)}, f32[16,96,128]{2,1,0:T(8,128)S(1)}, u32[]{:S(2)}, u32[]{:S(2)}) collective-permute-start(f32[16,96,128]{2,1,0:T(8,128)} %dynamic-slice_bitcast_fusion), channel_id=1, source_target_pairs={{0,4},{4,0},{1,5},{5,1},{2,6},{6,2},{3,7},{7,3},{8,12},{12,8},{9,1... | collective-permute-start | bytes 2359304 | tf_op jit(solution)/shard_map/ppermute | solution.py:42
  94.5 21.2 %all-to-all-start = ((f32[16,96,128]{2,1,0:T(8,128)}), f32[16,96,128]{2,1,0:T(8,128)S(1)}, u32[]{:S(2)}, u32[]{:S(2)}) async-start(f32[16,96,128]{2,1,0:T(8,128)} %bitcast_add_fusion), calls=%async_computation | async-start | bytes 1572864 | tf_op jit(solution)/shard_map/all_to_all | solution.py:43

commit v11 on v9

--- a/solution.py
+++ b/solution.py
@@ -86,7 +86,7 @@
     )
     cycle_part = cycle_reduce(partial_value)
 
-    flat = screened.reshape(first_rows * second_rows, width)
+    flat = amplitudes.reshape(first_rows * second_rows, width)
     ladder = jnp.dot(
         flat,
         lax.all_gather(ladder_integrals, PARTS, axis=0, tiled=True),

time: 88.2 us -> 88.1 us (level)
  no operation moved by 1% of the time
where the time goes in v11:
time: 88.1 us; the launch traced here: 87.4 us
  matrix products  23.9 us (27%)
  waiting for transfers between devices  17.9 us (20%)
  between operations  14.2 us (16%)
  starting transfers between devices  13.9 us (16%)
  Pallas kernels  10.3 us (12%)
  local copies, waits for them, and re-layouts  3.72 us (4%)
  other arithmetic  3.54 us (4%)
    all_gather x1, waiting for transfers between devices, local(): lax.all_gather(ladder_integrals, PARTS, axis=0, tiled=True)  15.1 us
    dot_general x1, matrix products, local(): jnp.dot(flat, lax.all_gather(ladder_integrals, PARTS, axis=0, tiled=True)...  14.7 us
    pallas_call x1, Pallas kernels, screened_by_a(): pl.pallas_call(screen_kernel, grid=(width // lanes,), out_shape=jax.Shape...  10.3 us
    dot_general x1, matrix products, local(): jnp.einsum('akci,kcm->aim', split, weights, precision=lax.Precision.HIGH,...  9.12 us
    ppermute x3, starting transfers between devices, cycle_piece(): got = lax.ppermute(piece, PARTS + ('vir',), pairs)  7.83 us
    all_to_all x1, starting transfers between devices, cycle_reduce(): lax.all_to_all(chip_share, CHIPS, split_axis=0, concat_axis=0, tiled=True)  5.04 us
    unnamed x7, local copies, waits for them, and re-layouts  2.76 us
    add x1, other arithmetic, cycle_reduce(): chip_share = mine + lax.ppermute(theirs, 'core', pairs)  2.25 us
  transfers between devices with their start and end apart: 6, of which 2 were waited for; matrix products, arithmetic and copies ran while one was open for 33% of the time, Pallas kernels for 12%

profile of v11, /device:TPU:1, one launch (start us, length us, event | category | flops | bytes accessed | tf_op | source)
XLA Modules:
  0.0 87.4 jit_solution(10898347052530403841)
XLA Ops:
  7.2 0.0 copy-start
  7.2 0.0 all-gather.2.cloned.1.call-start
  7.2 0.7 all-gather.2.cloned.1.call-update
  7.9 0.8 copy-done
  8.8 5.2 %collective-permute-start = (f32[16,32,128]{2,1,0:T(8,128)S(1)}, f32[16,32,128]{2,1,0:T(8,128)S(1)}, u32[]{:S(2)}, u32[]{:S(2)}) collective-permute-start(f32[16,32,128]{2,1,0:T(8,128)S(1)} %constant_dynamic-slice_fusion), channel_id=1, source_target_pairs={{0,3},{4,7},{8,11},{12,15},{16,19},{20,23},{24,27},{28,31},{33,32}... | collective-permute-start | bytes 786440 | tf_op jit(solution)/shard_map/ppermute | solution.py:29
  14.0 1.3 %collective-permute-start.1 = (f32[16,32,128]{2,1,0:T(8,128)S(1)}, f32[16,32,128]{2,1,0:T(8,128)S(1)}, u32[]{:S(2)}, u32[]{:S(2)}) collective-permute-start(f32[16,32,128]{2,1,0:T(8,128)S(1)} %constant_dynamic-slice_fusion), channel_id=1, source_target_pairs={{0,2},{4,6},{8,10},{12,14},{16,18},{20,22},{24,26},{28,30},{33,35}... | collective-permute-start | bytes 786440 | tf_op jit(solution)/shard_map/ppermute | solution.py:29
  15.3 1.3 %collective-permute-start.2 = (f32[16,32,128]{2,1,0:T(8,128)S(1)}, f32[16,32,128]{2,1,0:T(8,128)S(1)}, u32[]{:S(2)}, u32[]{:S(2)}) collective-permute-start(f32[16,32,128]{2,1,0:T(8,128)S(1)} %constant_dynamic-slice_fusion), channel_id=1, source_target_pairs={{0,1},{4,5},{8,9},{12,13},{16,17},{20,21},{24,25},{28,29},{33,34},... | collective-permute-start | bytes 786440 | tf_op jit(solution)/shard_map/ppermute | solution.py:29
  16.7 0.8 copy.6
  17.5 0.6 convert_element_type.3.live_ref
  18.1 10.3 %shard_map.59 = f32[32,512,96]{2,1,0:T(8,128)} custom-call(f32[96,16]{1,0:T(8,128)} %convert_element_type.3.live_ref, f32[96,16,1024]{2,1,0:T(8,128)} %amp_ref.1), custom_call_target="tpu_custom_call" | custom-call | tf_op jit(solution)/shard_map/pallas_call | solution.py:58
  28.4 0.0 collective-permute-done
  28.4 0.0 collective-permute-done.1
  28.5 0.0 collective-permute-done.2
  28.5 0.0 copy-start.2
  28.5 9.1 %convolution_bitcast_fusion = f32[16,2,96,128]{3,2,1,0:T(8,128)S(1)} fusion(f32[16,2,96,32,16]{2,3,4,1,0:T(8,128)} %bitcast.25, f32[16,32,128]{2,1,0:T(8,128)S(1)} %collective-permute-done, f32[16,32,128]{2,1,0:T(8,128)S(1)} %collective-permute-done.1, f32[16,32,128]{2,1,0:T(8,128)S(1)} %collective-permute-done.2, ...), kind=kOutput, calls=%fused_computation.3 | convolution fusion | flops 1208156160 | bytes 8912899 | tf_op jit(solution)/shard_map/akci,kcm->aim/dot_general | solution.py:80
  37.6 0.0 copy-start.1
  37.6 1.1 %copy-done.1 = f32[16,2,96,128]{3,2,1,0:T(8,128)} copy-done((f32[16,2,96,128]{3,2,1,0:T(8,128)}, f32[16,2,96,128]{3,2,1,0:T(8,128)S(1)}, u32[]{:S(2)}) %copy-start.1) | copy-done | bytes 1572888
  38.8 0.9 %dynamic-slice_bitcast_fusion = f32[16,96,128]{2,1,0:T(8,128)} fusion(f32[16,2,96,128]{3,2,1,0:T(8,128)S(1)} %convolution_bitcast_fusion, s32[]{:T(128)S(6)} %select_n.65), kind=kLoop, calls=%fused_computation.5 | loop fusion | bytes 1572868 | tf_op jit(solution)/shard_map/jit(dynamic_index_in_dim)/squeeze | solution.py:40
  39.7 1.0 %collective-permute-start.3 = (f32[16,96,128]{2,1,0:T(8,128)}, f32[16,96,128]{2,1,0:T(8,128)S(1)}, u32[]{:S(2)}, u32[]{:S(2)}) collective-permute-start(f32[16,96,128]{2,1,0:T(8,128)} %dynamic-slice_bitcast_fusion), channel_id=1, source_target_pairs={{0,4},{4,0},{1,5},{5,1},{2,6},{6,2},{3,7},{7,3},{8,12},{12,8},{9,1... | collective-permute-start | bytes 2359304 | tf_op jit(solution)/shard_map/ppermute | solution.py:42
  40.7 2.1 %collective-permute-done.3 = f32[16,96,128]{2,1,0:T(8,128)S(1)} collective-permute-done((f32[16,96,128]{2,1,0:T(8,128)}, f32[16,96,128]{2,1,0:T(8,128)S(1)}, u32[]{:S(2)}, u32[]{:S(2)}) %collective-permute-start.3) | collective-permute-done | bytes 786464 | tf_op jit(solution)/shard_map/ppermute | solution.py:42
  42.8 2.3 %bitcast_add_fusion = f32[16,96,128]{2,1,0:T(8,128)} fusion(f32[16,96,128]{2,1,0:T(8,128)S(1)} %collective-permute-done.3, f32[16,2,96,128]{3,2,1,0:T(8,128)} %copy-done.1, s32[]{:T(128)S(6)} %select_n.63), kind=kLoop, calls=%fused_computation.4 | loop fusion | flops 196608 | bytes 2359300 | tf_op jit(solution)/shard_map/add | solution.py:42
  45.0 5.0 %all-to-all-start = ((f32[16,96,128]{2,1,0:T(8,128)}), f32[16,96,128]{2,1,0:T(8,128)S(1)}, u32[]{:S(2)}, u32[]{:S(2)}) async-start(f32[16,96,128]{2,1,0:T(8,128)} %bitcast_add_fusion), calls=%async_computation | async-start | bytes 1572864 | tf_op jit(solution)/shard_map/all_to_all | solution.py:43
  50.1 15.1 %all-gather.2.cloned.1.call-done = f32[1024,1024]{1,0:T(8,128)} async-done(((f32[32,1024]{1,0:T(8,128)}), f32[1024,1024]{1,0:T(8,128)}) %all-gather.2.cloned.1.call-update) | async-done | bytes 4194320 | tf_op jit(solution)/shard_map/all_gather | solution.py:92
  65.2 0.0 copy-done.2
  65.2 14.7 %broadcast_multiply_fusion = f32[96,16,1024]{2,1,0:T(8,128)} fusion(f32[96,16]{1,0:T(8,128)S(1)} %copy-done.2, f32[96,16,1024]{2,1,0:T(8,128)} %amp_ref.1, f32[1024,1024]{1,0:T(8,128)} %all-gather.2.cloned.1.call-done), kind=kOutput, calls=%fused_computation.2 | convolution fusion | flops 9665249280 | bytes 16783360 | tf_op jit(solution)/shard_map/dot_general | solution.py:90
  79.9 0.0 all-to-all-done
  79.9 0.7 reduce_sum.9
  (1 shorter events, 0.0 us)
Async XLA Ops:
  7.2 1.6 %copy-start = (f32[128,32,128]{2,1,0:T(8,128)S(1)}, f32[128,32,128]{2,1,0:T(8,128)}, u32[]{:S(2)}) copy-start(f32[128,32,128]{2,1,0:T(8,128)} %param.7) | copy-start | bytes 6291460
  7.2 58.0 %all-gather.2.cloned.1.call-start = ((), (), s32[]{:S(2)}) async-start(), calls=%async_computation.1 | async-start | bytes 4325376 | tf_op jit(solution)/shard_map/all_gather | solution.py:92
  8.8 19.7 %collective-permute-start = (f32[16,32,128]{2,1,0:T(8,128)S(1)}, f32[16,32,128]{2,1,0:T(8,128)S(1)}, u32[]{:S(2)}, u32[]{:S(2)}) collective-permute-start(f32[16,32,128]{2,1,0:T(8,128)S(1)} %constant_dynamic-slice_fusion), channel_id=1, source_target_pairs={{0,3},{4,7},{8,11},{12,15},{16,19},{20,23},{24,27},{28,31},{33,32}... | collective-permute-start | bytes 786440 | tf_op jit(solution)/shard_map/ppermute | solution.py:29
  14.0 14.4 %collective-permute-start.1 = (f32[16,32,128]{2,1,0:T(8,128)S(1)}, f32[16,32,128]{2,1,0:T(8,128)S(1)}, u32[]{:S(2)}, u32[]{:S(2)}) collective-permute-start(f32[16,32,128]{2,1,0:T(8,128)S(1)} %constant_dynamic-slice_fusion), channel_id=1, source_target_pairs={{0,2},{4,6},{8,10},{12,14},{16,18},{20,22},{24,26},{28,30},{33,35}... | collective-permute-start | bytes 786440 | tf_op jit(solution)/shard_map/ppermute | solution.py:29
  15.3 13.1 %collective-permute-start.2 = (f32[16,32,128]{2,1,0:T(8,128)S(1)}, f32[16,32,128]{2,1,0:T(8,128)S(1)}, u32[]{:S(2)}, u32[]{:S(2)}) collective-permute-start(f32[16,32,128]{2,1,0:T(8,128)S(1)} %constant_dynamic-slice_fusion), channel_id=1, source_target_pairs={{0,1},{4,5},{8,9},{12,13},{16,17},{20,21},{24,25},{28,29},{33,34},... | collective-permute-start | bytes 786440 | tf_op jit(solution)/shard_map/ppermute | solution.py:29
  28.5 36.7 %copy-start.2 = (f32[96,16]{1,0:T(8,128)S(1)}, f32[96,16]{1,0:T(8,128)}, u32[]{:S(2)}) copy-start(f32[96,16]{1,0:T(8,128)} %convert_element_type.3.live_ref) | copy-start | bytes 18436
  37.6 1.1 %copy-start.1 = (f32[16,2,96,128]{3,2,1,0:T(8,128)}, f32[16,2,96,128]{3,2,1,0:T(8,128)S(1)}, u32[]{:S(2)}) copy-start(f32[16,2,96,128]{3,2,1,0:T(8,128)S(1)} %convolution_bitcast_fusion) | copy-start | bytes 4718596
  39.7 3.1 %collective-permute-start.3 = (f32[16,96,128]{2,1,0:T(8,128)}, f32[16,96,128]{2,1,0:T(8,128)S(1)}, u32[]{:S(2)}, u32[]{:S(2)}) collective-permute-start(f32[16,96,128]{2,1,0:T(8,128)} %dynamic-slice_bitcast_fusion), channel_id=1, source_target_pairs={{0,4},{4,0},{1,5},{5,1},{2,6},{6,2},{3,7},{7,3},{8,12},{12,8},{9,1... | collective-permute-start | bytes 2359304 | tf_op jit(solution)/shard_map/ppermute | solution.py:42
  45.0 34.9 %all-to-all-start = ((f32[16,96,128]{2,1,0:T(8,128)}), f32[16,96,128]{2,1,0:T(8,128)S(1)}, u32[]{:S(2)}, u32[]{:S(2)}) async-start(f32[16,96,128]{2,1,0:T(8,128)} %bitcast_add_fusion), calls=%async_computation | async-start | bytes 1572864 | tf_op jit(solution)/shard_map/all_to_all | solution.py:43
Sparse Core Ops, SparseCore 0:
  10.2 54.8 all-gather.1

commit v12 on v11

--- a/solution.py
+++ b/solution.py
@@ -40,7 +40,7 @@
     theirs = lax.dynamic_index_in_dim(by_core, (core + 1) % cores, axis=1, keepdims=False)
     pairs = [(c, (c + 1) % cores) for c in range(cores)]
     chip_share = mine + lax.ppermute(theirs, "core", pairs)
-    return lax.all_to_all(chip_share, CHIPS, split_axis=0, concat_axis=0, tiled=True)
+    return chip_share
 
 
 def screen_kernel(live_ref, amp_ref, out_ref):
@@ -87,9 +87,12 @@
     cycle_part = cycle_reduce(partial_value)
 
     flat = amplitudes.reshape(first_rows * second_rows, width)
+    full = lax.all_gather(ladder_integrals, PARTS, axis=0, tiled=True)
+    cycle_part, _ = lax.optimization_barrier((cycle_part, full))
+    cycle_part = lax.all_to_all(cycle_part, CHIPS, split_axis=0, concat_axis=0, tiled=True)
     ladder = jnp.dot(
         flat,
-        lax.all_gather(ladder_integrals, PARTS, axis=0, tiled=True),
+        full,
         precision=lax.Precision.HIGH,
         preferred_element_type=jnp.float32,
     )

time: 88.1 us -> 87.6 us (level)
  no operation moved by 1% of the time
where the time goes in v12:
time: 87.6 us; the launch traced here: 87.1 us
  matrix products  23.9 us (27%)
  waiting for transfers between devices  17.9 us (20%)
  between operations  14.2 us (16%)
  starting transfers between devices  13.5 us (15%)
  Pallas kernels  10.3 us (12%)
  local copies, waits for them, and re-layouts  3.72 us (4%)
  other arithmetic  3.54 us (4%)
    all_gather x1, waiting for transfers between devices, local(): full = lax.all_gather(ladder_integrals, PARTS, axis=0, tiled=True)  15 us
    dot_general x1, matrix products, local(): jnp.dot(flat, full, precision=lax.Precision.HIGH, preferred_element_type=...  14.8 us
    pallas_call x1, Pallas kernels, screened_by_a(): pl.pallas_call(screen_kernel, grid=(width // lanes,), out_shape=jax.Shape...  10.3 us
    dot_general x1, matrix products, local(): jnp.einsum('akci,kcm->aim', split, weights, precision=lax.Precision.HIGH,...  9.12 us
    ppermute x3, starting transfers between devices, cycle_piece(): got = lax.ppermute(piece, PARTS + ('vir',), pairs)  7.83 us
    all_to_all x1, starting transfers between devices, local(): lax.all_to_all(cycle_part, CHIPS, split_axis=0, concat_axis=0, tiled=True)  4.7 us
    unnamed x7, local copies, waits for them, and re-layouts  2.76 us
    add x1, other arithmetic, cycle_reduce(): chip_share = mine + lax.ppermute(theirs, 'core', pairs)  2.25 us
  transfers between devices with their start and end apart: 6, of which 2 were waited for; matrix products, arithmetic and copies ran while one was open for 33% of the time, Pallas kernels for 12%

profile of v12, /device:TPU:1, one launch (start us, length us, event | category | flops | bytes accessed | tf_op | source)
XLA Modules:
  0.0 87.1 jit_solution(18291620113037373609)
XLA Ops:
  7.2 0.0 copy-start
  7.2 0.0 all-gather.2.cloned.1.call-start
  7.2 0.7 all-gather.2.cloned.1.call-update
  7.9 0.8 copy-done
  8.8 5.2 %collective-permute-start = (f32[16,32,128]{2,1,0:T(8,128)S(1)}, f32[16,32,128]{2,1,0:T(8,128)S(1)}, u32[]{:S(2)}, u32[]{:S(2)}) collective-permute-start(f32[16,32,128]{2,1,0:T(8,128)S(1)} %constant_dynamic-slice_fusion), channel_id=1, source_target_pairs={{0,3},{4,7},{8,11},{12,15},{16,19},{20,23},{24,27},{28,31},{33,32}... | collective-permute-start | bytes 786440 | tf_op jit(solution)/shard_map/ppermute | solution.py:29
  14.0 1.3 %collective-permute-start.1 = (f32[16,32,128]{2,1,0:T(8,128)S(1)}, f32[16,32,128]{2,1,0:T(8,128)S(1)}, u32[]{:S(2)}, u32[]{:S(2)}) collective-permute-start(f32[16,32,128]{2,1,0:T(8,128)S(1)} %constant_dynamic-slice_fusion), channel_id=1, source_target_pairs={{0,2},{4,6},{8,10},{12,14},{16,18},{20,22},{24,26},{28,30},{33,35}... | collective-permute-start | bytes 786440 | tf_op jit(solution)/shard_map/ppermute | solution.py:29
  15.3 1.3 %collective-permute-start.2 = (f32[16,32,128]{2,1,0:T(8,128)S(1)}, f32[16,32,128]{2,1,0:T(8,128)S(1)}, u32[]{:S(2)}, u32[]{:S(2)}) collective-permute-start(f32[16,32,128]{2,1,0:T(8,128)S(1)} %constant_dynamic-slice_fusion), channel_id=1, source_target_pairs={{0,1},{4,5},{8,9},{12,13},{16,17},{20,21},{24,25},{28,29},{33,34},... | collective-permute-start | bytes 786440 | tf_op jit(solution)/shard_map/ppermute | solution.py:29
  16.7 0.8 copy.6
  17.5 0.6 convert_element_type.3.live_ref
  18.1 10.3 %shard_map.59 = f32[32,512,96]{2,1,0:T(8,128)} custom-call(f32[96,16]{1,0:T(8,128)} %convert_element_type.3.live_ref, f32[96,16,1024]{2,1,0:T(8,128)} %amp_ref.1), custom_call_target="tpu_custom_call" | custom-call | tf_op jit(solution)/shard_map/pallas_call | solution.py:58
  28.4 0.0 collective-permute-done
  28.4 0.0 collective-permute-done.1
  28.5 0.0 collective-permute-done.2
  28.5 0.0 copy-start.2
  28.5 9.1 %convolution_bitcast_fusion = f32[16,2,96,128]{3,2,1,0:T(8,128)S(1)} fusion(f32[16,2,96,32,16]{2,3,4,1,0:T(8,128)} %bitcast.25, f32[16,32,128]{2,1,0:T(8,128)S(1)} %collective-permute-done, f32[16,32,128]{2,1,0:T(8,128)S(1)} %collective-permute-done.1, f32[16,32,128]{2,1,0:T(8,128)S(1)} %collective-permute-done.2, ...), kind=kOutput, calls=%fused_computation.3 | convolution fusion | flops 1208156160 | bytes 8912899 | tf_op jit(solution)/shard_map/akci,kcm->aim/dot_general | solution.py:80
  37.6 0.0 copy-start.1
  37.6 1.1 %copy-done.1 = f32[16,2,96,128]{3,2,1,0:T(8,128)} copy-done((f32[16,2,96,128]{3,2,1,0:T(8,128)}, f32[16,2,96,128]{3,2,1,0:T(8,128)S(1)}, u32[]{:S(2)}) %copy-start.1) | copy-done | bytes 1572888
  38.8 0.9 %dynamic-slice_bitcast_fusion = f32[16,96,128]{2,1,0:T(8,128)} fusion(f32[16,2,96,128]{3,2,1,0:T(8,128)S(1)} %convolution_bitcast_fusion, s32[]{:T(128)S(6)} %select_n.65), kind=kLoop, calls=%fused_computation.5 | loop fusion | bytes 1572868 | tf_op jit(solution)/shard_map/jit(dynamic_index_in_dim)/squeeze | solution.py:40
  39.7 1.0 %collective-permute-start.3 = (f32[16,96,128]{2,1,0:T(8,128)}, f32[16,96,128]{2,1,0:T(8,128)S(1)}, u32[]{:S(2)}, u32[]{:S(2)}) collective-permute-start(f32[16,96,128]{2,1,0:T(8,128)} %dynamic-slice_bitcast_fusion), channel_id=1, source_target_pairs={{0,4},{4,0},{1,5},{5,1},{2,6},{6,2},{3,7},{7,3},{8,12},{12,8},{9,1... | collective-permute-start | bytes 2359304 | tf_op jit(solution)/shard_map/ppermute | solution.py:42
  40.7 2.1 %collective-permute-done.3 = f32[16,96,128]{2,1,0:T(8,128)S(1)} collective-permute-done((f32[16,96,128]{2,1,0:T(8,128)}, f32[16,96,128]{2,1,0:T(8,128)S(1)}, u32[]{:S(2)}, u32[]{:S(2)}) %collective-permute-start.3) | collective-permute-done | bytes 786464 | tf_op jit(solution)/shard_map/ppermute | solution.py:42
  42.8 2.3 %bitcast_add_fusion = f32[16,96,128]{2,1,0:T(8,128)} fusion(f32[16,96,128]{2,1,0:T(8,128)S(1)} %collective-permute-done.3, f32[16,2,96,128]{3,2,1,0:T(8,128)} %copy-done.1, s32[]{:T(128)S(6)} %select_n.63), kind=kLoop, calls=%fused_computation.4 | loop fusion | flops 196608 | bytes 2359300 | tf_op jit(solution)/shard_map/add | solution.py:42
  45.0 15.0 %all-gather.2.cloned.1.call-done = f32[1024,1024]{1,0:T(8,128)} async-done(((f32[32,1024]{1,0:T(8,128)}), f32[1024,1024]{1,0:T(8,128)}) %all-gather.2.cloned.1.call-update) | async-done | bytes 4194320 | tf_op jit(solution)/shard_map/all_gather | solution.py:90
  60.1 4.7 %all-to-all-start = ((f32[16,96,128]{2,1,0:T(8,128)}), f32[16,96,128]{2,1,0:T(8,128)S(1)}, u32[]{:S(2)}, u32[]{:S(2)}) async-start(f32[16,96,128]{2,1,0:T(8,128)} %bitcast_add_fusion), calls=%async_computation | async-start | bytes 1572864 | tf_op jit(solution)/shard_map/all_to_all | solution.py:92
  64.8 0.0 copy-done.2
  64.8 14.8 %broadcast_multiply_fusion = f32[96,16,1024]{2,1,0:T(8,128)} fusion(f32[96,16]{1,0:T(8,128)S(1)} %copy-done.2, f32[96,16,1024]{2,1,0:T(8,128)} %amp_ref.1, f32[1024,1024]{1,0:T(8,128)} %all-gather.2.cloned.1.call-done), kind=kOutput, calls=%fused_computation.2 | convolution fusion | flops 9665249280 | bytes 16783360 | tf_op jit(solution)/shard_map/dot_general | solution.py:93
  79.5 0.0 all-to-all-done
  79.5 0.7 reduce_sum.9
  (1 shorter events, 0.0 us)
Async XLA Ops:
  7.2 1.6 %copy-start = (f32[128,32,128]{2,1,0:T(8,128)S(1)}, f32[128,32,128]{2,1,0:T(8,128)}, u32[]{:S(2)}) copy-start(f32[128,32,128]{2,1,0:T(8,128)} %param.7) | copy-start | bytes 6291460
  7.2 52.9 %all-gather.2.cloned.1.call-start = ((), (), s32[]{:S(2)}) async-start(), calls=%async_computation.1 | async-start | bytes 4325376 | tf_op jit(solution)/shard_map/all_gather | solution.py:90
  8.8 19.7 %collective-permute-start = (f32[16,32,128]{2,1,0:T(8,128)S(1)}, f32[16,32,128]{2,1,0:T(8,128)S(1)}, u32[]{:S(2)}, u32[]{:S(2)}) collective-permute-start(f32[16,32,128]{2,1,0:T(8,128)S(1)} %constant_dynamic-slice_fusion), channel_id=1, source_target_pairs={{0,3},{4,7},{8,11},{12,15},{16,19},{20,23},{24,27},{28,31},{33,32}... | collective-permute-start | bytes 786440 | tf_op jit(solution)/shard_map/ppermute | solution.py:29
  14.0 14.4 %collective-permute-start.1 = (f32[16,32,128]{2,1,0:T(8,128)S(1)}, f32[16,32,128]{2,1,0:T(8,128)S(1)}, u32[]{:S(2)}, u32[]{:S(2)}) collective-permute-start(f32[16,32,128]{2,1,0:T(8,128)S(1)} %constant_dynamic-slice_fusion), channel_id=1, source_target_pairs={{0,2},{4,6},{8,10},{12,14},{16,18},{20,22},{24,26},{28,30},{33,35}... | collective-permute-start | bytes 786440 | tf_op jit(solution)/shard_map/ppermute | solution.py:29
  15.3 13.1 %collective-permute-start.2 = (f32[16,32,128]{2,1,0:T(8,128)S(1)}, f32[16,32,128]{2,1,0:T(8,128)S(1)}, u32[]{:S(2)}, u32[]{:S(2)}) collective-permute-start(f32[16,32,128]{2,1,0:T(8,128)S(1)} %constant_dynamic-slice_fusion), channel_id=1, source_target_pairs={{0,1},{4,5},{8,9},{12,13},{16,17},{20,21},{24,25},{28,29},{33,34},... | collective-permute-start | bytes 786440 | tf_op jit(solution)/shard_map/ppermute | solution.py:29
  28.5 36.3 %copy-start.2 = (f32[96,16]{1,0:T(8,128)S(1)}, f32[96,16]{1,0:T(8,128)}, u32[]{:S(2)}) copy-start(f32[96,16]{1,0:T(8,128)} %convert_element_type.3.live_ref) | copy-start | bytes 18436
  37.6 1.1 %copy-start.1 = (f32[16,2,96,128]{3,2,1,0:T(8,128)}, f32[16,2,96,128]{3,2,1,0:T(8,128)S(1)}, u32[]{:S(2)}) copy-start(f32[16,2,96,128]{3,2,1,0:T(8,128)S(1)} %convolution_bitcast_fusion) | copy-start | bytes 4718596
  39.7 3.1 %collective-permute-start.3 = (f32[16,96,128]{2,1,0:T(8,128)}, f32[16,96,128]{2,1,0:T(8,128)S(1)}, u32[]{:S(2)}, u32[]{:S(2)}) collective-permute-start(f32[16,96,128]{2,1,0:T(8,128)} %dynamic-slice_bitcast_fusion), channel_id=1, source_target_pairs={{0,4},{4,0},{1,5},{5,1},{2,6},{6,2},{3,7},{7,3},{8,12},{12,8},{9,1... | collective-permute-start | bytes 2359304 | tf_op jit(solution)/shard_map/ppermute | solution.py:42
  60.1 19.5 %all-to-all-start = ((f32[16,96,128]{2,1,0:T(8,128)}), f32[16,96,128]{2,1,0:T(8,128)S(1)}, u32[]{:S(2)}, u32[]{:S(2)}) async-start(f32[16,96,128]{2,1,0:T(8,128)} %bitcast_add_fusion), calls=%async_computation | async-start | bytes 1572864 | tf_op jit(solution)/shard_map/all_to_all | solution.py:92
Sparse Core Ops, SparseCore 0:
  10.2 49.7 all-gather.1

commit v13 on v11

--- a/solution.py
+++ b/solution.py
@@ -81,7 +81,7 @@
         "akci,kcm->aim",
         split,
         weights,
-        precision=lax.Precision.HIGH,
+        precision=lax.Precision.HIGHEST,
         preferred_element_type=jnp.float32,
     )
     cycle_part = cycle_reduce(partial_value)

time: 88.1 us -> 82.9 us (0.941)
  waiting for transfers between devices: 17.9 us -> 6.15 us
  matrix products: 23.9 us -> 30.6 us
    all_gather x1, waiting for transfers between devices: 15.1 us -> 2.96 us  [local(): lax.all_gather(ladder_integrals, PARTS, axis=0, tiled=True)]
    dot_general x1, matrix products: 9.12 us -> 15.8 us  [local(): jnp.einsum('akci,kcm->aim', split, weights, precision=lax.Precision.HIGHE...]
  transfers between devices with their start and end apart: 6 -> 6, of which waited for: 2 -> 2; matrix products, arithmetic and copies ran while one was open for 33% -> 43% of each run, Pallas kernels for 12% -> 13%
where the time goes in v13:
time: 82.9 us; the launch traced here: 82.3 us
  matrix products  30.6 us (37%)
  between operations  14.2 us (17%)
  starting transfers between devices  13.9 us (17%)
  Pallas kernels  10.3 us (12%)
  waiting for transfers between devices  6.15 us (7%)
  local copies, waits for them, and re-layouts  3.72 us (4%)
  other arithmetic  3.43 us (4%)
    dot_general x1, matrix products, local(): jnp.einsum('akci,kcm->aim', split, weights, precision=lax.Precision.HIGHE...  15.8 us
    dot_general x1, matrix products, local(): jnp.dot(flat, lax.all_gather(ladder_integrals, PARTS, axis=0, tiled=True)...  14.7 us
    pallas_call x1, Pallas kernels, screened_by_a(): pl.pallas_call(screen_kernel, grid=(width // lanes,), out_shape=jax.Shape...  10.3 us
    ppermute x3, starting transfers between devices, cycle_piece(): got = lax.ppermute(piece, PARTS + ('vir',), pairs)  7.83 us
    all_to_all x1, starting transfers between devices, cycle_reduce(): lax.all_to_all(chip_share, CHIPS, split_axis=0, concat_axis=0, tiled=True)  5.12 us
    all_gather x1, waiting for transfers between devices, local(): lax.all_gather(ladder_integrals, PARTS, axis=0, tiled=True)  2.96 us
    unnamed x7, local copies, waits for them, and re-layouts  2.76 us
    ppermute x1, waiting for transfers between devices, cycle_reduce(): chip_share = mine + lax.ppermute(theirs, 'core', pairs)  2.51 us
  transfers between devices with their start and end apart: 6, of which 2 were waited for; matrix products, arithmetic and copies ran while one was open for 43% of the time, Pallas kernels for 13%

profile of v13, /device:TPU:1, one launch (start us, length us, event | category | flops | bytes accessed | tf_op | source)
XLA Modules:
  0.0 82.3 jit_solution(1619513462920045166)
XLA Ops:
  7.2 0.0 copy-start
  7.2 0.0 all-gather.2.cloned.1.call-start
  7.2 0.7 all-gather.2.cloned.1.call-update
  7.9 0.8 copy-done
  8.8 5.2 %collective-permute-start = (f32[16,32,128]{2,1,0:T(8,128)S(1)}, f32[16,32,128]{2,1,0:T(8,128)S(1)}, u32[]{:S(2)}, u32[]{:S(2)}) collective-permute-start(f32[16,32,128]{2,1,0:T(8,128)S(1)} %constant_dynamic-slice_fusion), channel_id=1, source_target_pairs={{0,3},{4,7},{8,11},{12,15},{16,19},{20,23},{24,27},{28,31},{33,32}... | collective-permute-start | bytes 786440 | tf_op jit(solution)/shard_map/ppermute | solution.py:29
  14.0 1.3 %collective-permute-start.1 = (f32[16,32,128]{2,1,0:T(8,128)S(1)}, f32[16,32,128]{2,1,0:T(8,128)S(1)}, u32[]{:S(2)}, u32[]{:S(2)}) collective-permute-start(f32[16,32,128]{2,1,0:T(8,128)S(1)} %constant_dynamic-slice_fusion), channel_id=1, source_target_pairs={{0,2},{4,6},{8,10},{12,14},{16,18},{20,22},{24,26},{28,30},{33,35}... | collective-permute-start | bytes 786440 | tf_op jit(solution)/shard_map/ppermute | solution.py:29
  15.3 1.3 %collective-permute-start.2 = (f32[16,32,128]{2,1,0:T(8,128)S(1)}, f32[16,32,128]{2,1,0:T(8,128)S(1)}, u32[]{:S(2)}, u32[]{:S(2)}) collective-permute-start(f32[16,32,128]{2,1,0:T(8,128)S(1)} %constant_dynamic-slice_fusion), channel_id=1, source_target_pairs={{0,1},{4,5},{8,9},{12,13},{16,17},{20,21},{24,25},{28,29},{33,34},... | collective-permute-start | bytes 786440 | tf_op jit(solution)/shard_map/ppermute | solution.py:29
  16.7 0.8 copy.6
  17.5 0.6 convert_element_type.3.live_ref
  18.1 10.3 %shard_map.59 = f32[32,512,96]{2,1,0:T(8,128)} custom-call(f32[96,16]{1,0:T(8,128)} %convert_element_type.3.live_ref, f32[96,16,1024]{2,1,0:T(8,128)} %amp_ref.1), custom_call_target="tpu_custom_call" | custom-call | tf_op jit(solution)/shard_map/pallas_call | solution.py:58
  28.4 0.0 collective-permute-done
  28.4 0.0 collective-permute-done.1
  28.5 0.0 collective-permute-done.2
  28.5 0.0 copy-start.2
  28.5 15.8 %convolution_bitcast_fusion = f32[16,2,96,128]{3,2,1,0:T(8,128)S(1)} fusion(f32[16,2,96,32,16]{2,3,4,1,0:T(8,128)} %bitcast.25, f32[16,32,128]{2,1,0:T(8,128)S(1)} %collective-permute-done, f32[16,32,128]{2,1,0:T(8,128)S(1)} %collective-permute-done.1, f32[16,32,128]{2,1,0:T(8,128)S(1)} %collective-permute-done.2, ...), kind=kOutput, calls=%fused_computation.3 | convolution fusion | flops 2416115712 | bytes 8912899 | tf_op jit(solution)/shard_map/akci,kcm->aim/dot_general | solution.py:80
  44.3 0.0 copy-start.1
  44.3 1.1 %copy-done.1 = f32[16,2,96,128]{3,2,1,0:T(8,128)} copy-done((f32[16,2,96,128]{3,2,1,0:T(8,128)}, f32[16,2,96,128]{3,2,1,0:T(8,128)S(1)}, u32[]{:S(2)}) %copy-start.1) | copy-done | bytes 1572888
  45.4 0.9 %dynamic-slice_bitcast_fusion = f32[16,96,128]{2,1,0:T(8,128)} fusion(f32[16,2,96,128]{3,2,1,0:T(8,128)S(1)} %convolution_bitcast_fusion, s32[]{:T(128)S(6)} %select_n.65), kind=kLoop, calls=%fused_computation.5 | loop fusion | bytes 1572868 | tf_op jit(solution)/shard_map/jit(dynamic_index_in_dim)/squeeze | solution.py:40
  46.4 1.0 %collective-permute-start.3 = (f32[16,96,128]{2,1,0:T(8,128)}, f32[16,96,128]{2,1,0:T(8,128)S(1)}, u32[]{:S(2)}, u32[]{:S(2)}) collective-permute-start(f32[16,96,128]{2,1,0:T(8,128)} %dynamic-slice_bitcast_fusion), channel_id=1, source_target_pairs={{0,4},{4,0},{1,5},{5,1},{2,6},{6,2},{3,7},{7,3},{8,12},{12,8},{9,1... | collective-permute-start | bytes 2359304 | tf_op jit(solution)/shard_map/ppermute | solution.py:42
  47.3 2.5 %collective-permute-done.3 = f32[16,96,128]{2,1,0:T(8,128)S(1)} collective-permute-done((f32[16,96,128]{2,1,0:T(8,128)}, f32[16,96,128]{2,1,0:T(8,128)S(1)}, u32[]{:S(2)}, u32[]{:S(2)}) %collective-permute-start.3) | collective-permute-done | bytes 786464 | tf_op jit(solution)/shard_map/ppermute | solution.py:42
  49.8 2.1 %bitcast_add_fusion = f32[16,96,128]{2,1,0:T(8,128)} fusion(f32[16,96,128]{2,1,0:T(8,128)S(1)} %collective-permute-done.3, f32[16,2,96,128]{3,2,1,0:T(8,128)} %copy-done.1, s32[]{:T(128)S(6)} %select_n.63), kind=kLoop, calls=%fused_computation.4 | loop fusion | flops 196608 | bytes 2359300 | tf_op jit(solution)/shard_map/add | solution.py:42
  52.0 5.1 %all-to-all-start = ((f32[16,96,128]{2,1,0:T(8,128)}), f32[16,96,128]{2,1,0:T(8,128)S(1)}, u32[]{:S(2)}, u32[]{:S(2)}) async-start(f32[16,96,128]{2,1,0:T(8,128)} %bitcast_add_fusion), calls=%async_computation | async-start | bytes 1572864 | tf_op jit(solution)/shard_map/all_to_all | solution.py:43
  57.1 3.0 %all-gather.2.cloned.1.call-done = f32[1024,1024]{1,0:T(8,128)} async-done(((f32[32,1024]{1,0:T(8,128)}), f32[1024,1024]{1,0:T(8,128)}) %all-gather.2.cloned.1.call-update) | async-done | bytes 4194320 | tf_op jit(solution)/shard_map/all_gather | solution.py:92
  60.1 0.0 copy-done.2
  60.1 14.7 %broadcast_multiply_fusion = f32[96,16,1024]{2,1,0:T(8,128)} fusion(f32[96,16]{1,0:T(8,128)S(1)} %copy-done.2, f32[96,16,1024]{2,1,0:T(8,128)} %amp_ref.1, f32[1024,1024]{1,0:T(8,128)} %all-gather.2.cloned.1.call-done), kind=kOutput, calls=%fused_computation.2 | convolution fusion | flops 9665249280 | bytes 16783360 | tf_op jit(solution)/shard_map/dot_general | solution.py:90
  74.8 0.0 all-to-all-done
  74.8 0.7 reduce_sum.9
  (1 shorter events, 0.0 us)
Async XLA Ops:
  7.2 1.6 %copy-start = (f32[128,32,128]{2,1,0:T(8,128)S(1)}, f32[128,32,128]{2,1,0:T(8,128)}, u32[]{:S(2)}) copy-start(f32[128,32,128]{2,1,0:T(8,128)} %param.7) | copy-start | bytes 6291460
  7.2 52.9 %all-gather.2.cloned.1.call-start = ((), (), s32[]{:S(2)}) async-start(), calls=%async_computation.1 | async-start | bytes 4325376 | tf_op jit(solution)/shard_map/all_gather | solution.py:92
  8.8 19.7 %collective-permute-start = (f32[16,32,128]{2,1,0:T(8,128)S(1)}, f32[16,32,128]{2,1,0:T(8,128)S(1)}, u32[]{:S(2)}, u32[]{:S(2)}) collective-permute-start(f32[16,32,128]{2,1,0:T(8,128)S(1)} %constant_dynamic-slice_fusion), channel_id=1, source_target_pairs={{0,3},{4,7},{8,11},{12,15},{16,19},{20,23},{24,27},{28,31},{33,32}... | collective-permute-start | bytes 786440 | tf_op jit(solution)/shard_map/ppermute | solution.py:29
  14.0 14.4 %collective-permute-start.1 = (f32[16,32,128]{2,1,0:T(8,128)S(1)}, f32[16,32,128]{2,1,0:T(8,128)S(1)}, u32[]{:S(2)}, u32[]{:S(2)}) collective-permute-start(f32[16,32,128]{2,1,0:T(8,128)S(1)} %constant_dynamic-slice_fusion), channel_id=1, source_target_pairs={{0,2},{4,6},{8,10},{12,14},{16,18},{20,22},{24,26},{28,30},{33,35}... | collective-permute-start | bytes 786440 | tf_op jit(solution)/shard_map/ppermute | solution.py:29
  15.3 13.1 %collective-permute-start.2 = (f32[16,32,128]{2,1,0:T(8,128)S(1)}, f32[16,32,128]{2,1,0:T(8,128)S(1)}, u32[]{:S(2)}, u32[]{:S(2)}) collective-permute-start(f32[16,32,128]{2,1,0:T(8,128)S(1)} %constant_dynamic-slice_fusion), channel_id=1, source_target_pairs={{0,1},{4,5},{8,9},{12,13},{16,17},{20,21},{24,25},{28,29},{33,34},... | collective-permute-start | bytes 786440 | tf_op jit(solution)/shard_map/ppermute | solution.py:29
  28.5 31.6 %copy-start.2 = (f32[96,16]{1,0:T(8,128)S(1)}, f32[96,16]{1,0:T(8,128)}, u32[]{:S(2)}) copy-start(f32[96,16]{1,0:T(8,128)} %convert_element_type.3.live_ref) | copy-start | bytes 18436
  44.3 1.1 %copy-start.1 = (f32[16,2,96,128]{3,2,1,0:T(8,128)}, f32[16,2,96,128]{3,2,1,0:T(8,128)S(1)}, u32[]{:S(2)}) copy-start(f32[16,2,96,128]{3,2,1,0:T(8,128)S(1)} %convolution_bitcast_fusion) | copy-start | bytes 4718596
  46.4 3.5 %collective-permute-start.3 = (f32[16,96,128]{2,1,0:T(8,128)}, f32[16,96,128]{2,1,0:T(8,128)S(1)}, u32[]{:S(2)}, u32[]{:S(2)}) collective-permute-start(f32[16,96,128]{2,1,0:T(8,128)} %dynamic-slice_bitcast_fusion), channel_id=1, source_target_pairs={{0,4},{4,0},{1,5},{5,1},{2,6},{6,2},{3,7},{7,3},{8,12},{12,8},{9,1... | collective-permute-start | bytes 2359304 | tf_op jit(solution)/shard_map/ppermute | solution.py:42
  52.0 22.8 %all-to-all-start = ((f32[16,96,128]{2,1,0:T(8,128)}), f32[16,96,128]{2,1,0:T(8,128)S(1)}, u32[]{:S(2)}, u32[]{:S(2)}) async-start(f32[16,96,128]{2,1,0:T(8,128)} %bitcast_add_fusion), calls=%async_computation | async-start | bytes 1572864 | tf_op jit(solution)/shard_map/all_to_all | solution.py:43
Sparse Core Ops, SparseCore 0:
  10.2 49.7 all-gather.1

commit v14 on v13

--- a/solution.py
+++ b/solution.py
@@ -75,8 +75,10 @@
     width = screened.shape[2]
     virtuals = cycle_integrals.shape[1]
 
-    weights = cycle_piece(cycle_integrals, second_rows)
-    split = screened_by_a(amplitudes, live, virtuals).reshape(width // virtuals, second_rows, virtuals, first_rows)
+    by_a = screened_by_a(amplitudes, live, virtuals)
+    held, by_a = lax.optimization_barrier((cycle_integrals, by_a))
+    weights = cycle_piece(held, second_rows)
+    split = by_a.reshape(width // virtuals, second_rows, virtuals, first_rows)
     partial_value = jnp.einsum(
         "akci,kcm->aim",
         split,

time: 82.9 us -> 89.7 us (1.082); the launches traced: 82.3 us -> 88.1 us
  waiting for transfers between devices: 6.15 us -> 12.1 us
    ppermute x3, waiting for transfers between devices: 0.01 us -> 9.21 us  [cycle_piece(): got = lax.ppermute(piece, PARTS + ('vir',), pairs)]
    all_gather x1, waiting for transfers between devices: 2.96 us -> 0.02 us  [local(): lax.all_gather(ladder_integrals, PARTS, axis=0, tiled=True)]
  transfers between devices with their start and end apart: 6 -> 6, of which waited for: 2 -> 4; matrix products, arithmetic and copies ran while one was open for 43% -> 40% of each run, Pallas kernels for 13% -> 12%
where the time goes in v14:
time: 89.7 us; the launch traced here: 88.1 us
  matrix products  30.6 us (34%)
  starting transfers between devices  14.6 us (16%)
  between operations  14.2 us (16%)
  waiting for transfers between devices  12.1 us (13%)
  Pallas kernels  10.3 us (11%)
  other arithmetic  3.4 us (4%)
  local copies, waits for them, and re-layouts  2.9 us (3%)
    dot_general x1, matrix products, local(): jnp.einsum('akci,kcm->aim', split, weights, precision=lax.Precision.HIGHE...  15.8 us
    dot_general x1, matrix products, local(): jnp.dot(flat, lax.all_gather(ladder_integrals, PARTS, axis=0, tiled=True)...  14.8 us
    pallas_call x1, Pallas kernels, screened_by_a(): pl.pallas_call(screen_kernel, grid=(width // lanes,), out_shape=jax.Shape...  10.3 us
    ppermute x3, waiting for transfers between devices, cycle_piece(): got = lax.ppermute(piece, PARTS + ('vir',), pairs)  9.21 us
    ppermute x3, starting transfers between devices, cycle_piece(): got = lax.ppermute(piece, PARTS + ('vir',), pairs)  7.83 us
    all_to_all x1, starting transfers between devices, cycle_reduce(): lax.all_to_all(chip_share, CHIPS, split_axis=0, concat_axis=0, tiled=True)  5.19 us
    ppermute x1, waiting for transfers between devices, cycle_reduce(): chip_share = mine + lax.ppermute(theirs, 'core', pairs)  2.22 us
    add x1, other arithmetic, cycle_reduce(): chip_share = mine + lax.ppermute(theirs, 'core', pairs)  2.11 us
  transfers between devices with their start and end apart: 6, of which 4 were waited for; matrix products, arithmetic and copies ran while one was open for 40% of the time, Pallas kernels for 12%

profile of v14, /device:TPU:1, one launch (start us, length us, event | category | flops | bytes accessed | tf_op | source)
XLA Modules:
  0.0 88.1 jit_solution(4318435094393689753)
XLA Ops:
  7.2 0.0 copy-start
  7.2 0.0 all-gather.2.cloned.1.call-start
  7.2 0.7 all-gather.2.cloned.1.call-update
  7.9 0.8 copy.6
  8.7 0.6 convert_element_type.3.live_ref
  9.4 10.3 %shard_map.59 = f32[32,512,96]{2,1,0:T(8,128)} custom-call(f32[96,16]{1,0:T(8,128)} %convert_element_type.3.live_ref, f32[96,16,1024]{2,1,0:T(8,128)} %amp_ref.1), custom_call_target="tpu_custom_call" | custom-call | tf_op jit(solution)/shard_map/pallas_call | solution.py:58
  19.7 0.0 copy-done
  19.7 5.2 %collective-permute-start = (f32[16,32,128]{2,1,0:T(8,128)S(1)}, f32[16,32,128]{2,1,0:T(8,128)S(1)}, u32[]{:S(2)}, u32[]{:S(2)}) collective-permute-start(f32[16,32,128]{2,1,0:T(8,128)S(1)} %constant_dynamic-slice_fusion), channel_id=1, source_target_pairs={{0,3},{4,7},{8,11},{12,15},{16,19},{20,23},{24,27},{28,31},{33,32}... | collective-permute-start | bytes 786440 | tf_op jit(solution)/shard_map/ppermute | solution.py:29
  24.9 1.3 %collective-permute-start.1 = (f32[16,32,128]{2,1,0:T(8,128)S(1)}, f32[16,32,128]{2,1,0:T(8,128)S(1)}, u32[]{:S(2)}, u32[]{:S(2)}) collective-permute-start(f32[16,32,128]{2,1,0:T(8,128)S(1)} %constant_dynamic-slice_fusion), channel_id=1, source_target_pairs={{0,2},{4,6},{8,10},{12,14},{16,18},{20,22},{24,26},{28,30},{33,35}... | collective-permute-start | bytes 786440 | tf_op jit(solution)/shard_map/ppermute | solution.py:29
  26.2 1.3 %collective-permute-start.2 = (f32[16,32,128]{2,1,0:T(8,128)S(1)}, f32[16,32,128]{2,1,0:T(8,128)S(1)}, u32[]{:S(2)}, u32[]{:S(2)}) collective-permute-start(f32[16,32,128]{2,1,0:T(8,128)S(1)} %constant_dynamic-slice_fusion), channel_id=1, source_target_pairs={{0,1},{4,5},{8,9},{12,13},{16,17},{20,21},{24,25},{28,29},{33,34},... | collective-permute-start | bytes 786440 | tf_op jit(solution)/shard_map/ppermute | solution.py:29
  27.6 2.3 %collective-permute-done = f32[16,32,128]{2,1,0:T(8,128)S(1)} collective-permute-done((f32[16,32,128]{2,1,0:T(8,128)S(1)}, f32[16,32,128]{2,1,0:T(8,128)S(1)}, u32[]{:S(2)}, u32[]{:S(2)}) %collective-permute-start) | collective-permute-done | bytes 262176 | tf_op jit(solution)/shard_map/ppermute | solution.py:29
  29.9 1.3 %collective-permute-done.1 = f32[16,32,128]{2,1,0:T(8,128)S(1)} collective-permute-done((f32[16,32,128]{2,1,0:T(8,128)S(1)}, f32[16,32,128]{2,1,0:T(8,128)S(1)}, u32[]{:S(2)}, u32[]{:S(2)}) %collective-permute-start.1) | collective-permute-done | bytes 262176 | tf_op jit(solution)/shard_map/ppermute | solution.py:29
  31.2 5.6 %collective-permute-done.2 = f32[16,32,128]{2,1,0:T(8,128)S(1)} collective-permute-done((f32[16,32,128]{2,1,0:T(8,128)S(1)}, f32[16,32,128]{2,1,0:T(8,128)S(1)}, u32[]{:S(2)}, u32[]{:S(2)}) %collective-permute-start.2) | collective-permute-done | bytes 262176 | tf_op jit(solution)/shard_map/ppermute | solution.py:29
  36.8 0.0 copy-start.2
  36.8 15.8 %convolution_bitcast_fusion = f32[16,2,96,128]{3,2,1,0:T(8,128)S(1)} fusion(f32[16,2,96,32,16]{2,3,4,1,0:T(8,128)} %bitcast.25, f32[16,32,128]{2,1,0:T(8,128)S(1)} %collective-permute-done, f32[16,32,128]{2,1,0:T(8,128)S(1)} %collective-permute-done.1, f32[16,32,128]{2,1,0:T(8,128)S(1)} %collective-permute-done.2, ...), kind=kOutput, calls=%fused_computation.3 | convolution fusion | flops 2416115712 | bytes 8912899 | tf_op jit(solution)/shard_map/akci,kcm->aim/dot_general | solution.py:82
  52.6 0.0 copy-start.1
  52.6 1.1 %copy-done.1 = f32[16,2,96,128]{3,2,1,0:T(8,128)} copy-done((f32[16,2,96,128]{3,2,1,0:T(8,128)}, f32[16,2,96,128]{3,2,1,0:T(8,128)S(1)}, u32[]{:S(2)}) %copy-start.1) | copy-done | bytes 1572888
  53.8 0.9 %dynamic-slice_bitcast_fusion = f32[16,96,128]{2,1,0:T(8,128)} fusion(f32[16,2,96,128]{3,2,1,0:T(8,128)S(1)} %convolution_bitcast_fusion, s32[]{:T(128)S(6)} %select_n.65), kind=kLoop, calls=%fused_computation.5 | loop fusion | bytes 1572868 | tf_op jit(solution)/shard_map/jit(dynamic_index_in_dim)/squeeze | solution.py:40
  54.7 1.5 %collective-permute-start.3 = (f32[16,96,128]{2,1,0:T(8,128)}, f32[16,96,128]{2,1,0:T(8,128)S(1)}, u32[]{:S(2)}, u32[]{:S(2)}) collective-permute-start(f32[16,96,128]{2,1,0:T(8,128)} %dynamic-slice_bitcast_fusion), channel_id=1, source_target_pairs={{0,4},{4,0},{1,5},{5,1},{2,6},{6,2},{3,7},{7,3},{8,12},{12,8},{9,1... | collective-permute-start | bytes 2359304 | tf_op jit(solution)/shard_map/ppermute | solution.py:42
  56.2 2.2 %collective-permute-done.3 = f32[16,96,128]{2,1,0:T(8,128)S(1)} collective-permute-done((f32[16,96,128]{2,1,0:T(8,128)}, f32[16,96,128]{2,1,0:T(8,128)S(1)}, u32[]{:S(2)}, u32[]{:S(2)}) %collective-permute-start.3) | collective-permute-done | bytes 786464 | tf_op jit(solution)/shard_map/ppermute | solution.py:42
  58.5 2.1 %bitcast_add_fusion = f32[16,96,128]{2,1,0:T(8,128)} fusion(f32[16,96,128]{2,1,0:T(8,128)S(1)} %collective-permute-done.3, f32[16,2,96,128]{3,2,1,0:T(8,128)} %copy-done.1, s32[]{:T(128)S(6)} %select_n.63), kind=kLoop, calls=%fused_computation.4 | loop fusion | flops 196608 | bytes 2359300 | tf_op jit(solution)/shard_map/add | solution.py:42
  60.6 5.2 %all-to-all-start = ((f32[16,96,128]{2,1,0:T(8,128)}), f32[16,96,128]{2,1,0:T(8,128)S(1)}, u32[]{:S(2)}, u32[]{:S(2)}) async-start(f32[16,96,128]{2,1,0:T(8,128)} %bitcast_add_fusion), calls=%async_computation | async-start | bytes 1572864 | tf_op jit(solution)/shard_map/all_to_all | solution.py:43
  65.8 0.0 all-gather.2.cloned.1.call-done
  65.8 0.0 copy-done.2
  65.8 14.8 %broadcast_multiply_fusion = f32[96,16,1024]{2,1,0:T(8,128)} fusion(f32[96,16]{1,0:T(8,128)S(1)} %copy-done.2, f32[96,16,1024]{2,1,0:T(8,128)} %amp_ref.1, f32[1024,1024]{1,0:T(8,128)} %all-gather.2.cloned.1.call-done), kind=kOutput, calls=%fused_computation.2 | convolution fusion | flops 9665249280 | bytes 16783360 | tf_op jit(solution)/shard_map/dot_general | solution.py:92
  80.6 0.0 all-to-all-done
  80.6 0.7 reduce_sum.9
  (1 shorter events, 0.0 us)
Async XLA Ops:
  7.2 12.5 %copy-start = (f32[128,32,128]{2,1,0:T(8,128)S(1)}, f32[128,32,128]{2,1,0:T(8,128)}, u32[]{:S(2)}) copy-start(f32[128,32,128]{2,1,0:T(8,128)} %param.7) | copy-start | bytes 6291460
  7.2 58.6 %all-gather.2.cloned.1.call-start = ((), (), s32[]{:S(2)}) async-start(), calls=%async_computation.1 | async-start | bytes 4325376 | tf_op jit(solution)/shard_map/all_gather | solution.py:94
  19.7 10.2 %collective-permute-start = (f32[16,32,128]{2,1,0:T(8,128)S(1)}, f32[16,32,128]{2,1,0:T(8,128)S(1)}, u32[]{:S(2)}, u32[]{:S(2)}) collective-permute-start(f32[16,32,128]{2,1,0:T(8,128)S(1)} %constant_dynamic-slice_fusion), channel_id=1, source_target_pairs={{0,3},{4,7},{8,11},{12,15},{16,19},{20,23},{24,27},{28,31},{33,32}... | collective-permute-start | bytes 786440 | tf_op jit(solution)/shard_map/ppermute | solution.py:29
  24.9 6.3 %collective-permute-start.1 = (f32[16,32,128]{2,1,0:T(8,128)S(1)}, f32[16,32,128]{2,1,0:T(8,128)S(1)}, u32[]{:S(2)}, u32[]{:S(2)}) collective-permute-start(f32[16,32,128]{2,1,0:T(8,128)S(1)} %constant_dynamic-slice_fusion), channel_id=1, source_target_pairs={{0,2},{4,6},{8,10},{12,14},{16,18},{20,22},{24,26},{28,30},{33,35}... | collective-permute-start | bytes 786440 | tf_op jit(solution)/shard_map/ppermute | solution.py:29
  26.2 10.6 %collective-permute-start.2 = (f32[16,32,128]{2,1,0:T(8,128)S(1)}, f32[16,32,128]{2,1,0:T(8,128)S(1)}, u32[]{:S(2)}, u32[]{:S(2)}) collective-permute-start(f32[16,32,128]{2,1,0:T(8,128)S(1)} %constant_dynamic-slice_fusion), channel_id=1, source_target_pairs={{0,1},{4,5},{8,9},{12,13},{16,17},{20,21},{24,25},{28,29},{33,34},... | collective-permute-start | bytes 786440 | tf_op jit(solution)/shard_map/ppermute | solution.py:29
  36.8 29.0 %copy-start.2 = (f32[96,16]{1,0:T(8,128)S(1)}, f32[96,16]{1,0:T(8,128)}, u32[]{:S(2)}) copy-start(f32[96,16]{1,0:T(8,128)} %convert_element_type.3.live_ref) | copy-start | bytes 18436
  52.6 1.1 %copy-start.1 = (f32[16,2,96,128]{3,2,1,0:T(8,128)}, f32[16,2,96,128]{3,2,1,0:T(8,128)S(1)}, u32[]{:S(2)}) copy-start(f32[16,2,96,128]{3,2,1,0:T(8,128)S(1)} %convolution_bitcast_fusion) | copy-start | bytes 4718596
  54.7 3.7 %collective-permute-start.3 = (f32[16,96,128]{2,1,0:T(8,128)}, f32[16,96,128]{2,1,0:T(8,128)S(1)}, u32[]{:S(2)}, u32[]{:S(2)}) collective-permute-start(f32[16,96,128]{2,1,0:T(8,128)} %dynamic-slice_bitcast_fusion), channel_id=1, source_target_pairs={{0,4},{4,0},{1,5},{5,1},{2,6},{6,2},{3,7},{7,3},{8,12},{12,8},{9,1... | collective-permute-start | bytes 2359304 | tf_op jit(solution)/shard_map/ppermute | solution.py:42
  60.6 20.0 %all-to-all-start = ((f32[16,96,128]{2,1,0:T(8,128)}), f32[16,96,128]{2,1,0:T(8,128)S(1)}, u32[]{:S(2)}, u32[]{:S(2)}) async-start(f32[16,96,128]{2,1,0:T(8,128)} %bitcast_add_fusion), calls=%async_computation | async-start | bytes 1572864 | tf_op jit(solution)/shard_map/all_to_all | solution.py:43
Sparse Core Ops, SparseCore 0:
  10.2 49.7 all-gather.1

commit v15 on v13

--- a/solution.py
+++ b/solution.py
@@ -53,7 +53,7 @@
 
 def screened_by_a(amplitudes, live, virtuals):
     rows, kblock, width = amplitudes.shape
-    lanes = 128
+    lanes = 256
     per_step = lanes // virtuals
     return pl.pallas_call(
         screen_kernel,

time: 82.9 us -> 84 us (1.013); the launches traced: 82.3 us -> 82.3 us
  Pallas kernels: 10.3 us -> 8.52 us
  waiting for transfers between devices: 6.15 us -> 7.6 us
    all_gather x1, waiting for transfers between devices: 2.96 us -> 4.79 us  [local(): lax.all_gather(ladder_integrals, PARTS, axis=0, tiled=True)]
    pallas_call x1, Pallas kernels: 10.3 us -> 8.52 us  [screened_by_a(): pl.pallas_call(screen_kernel, grid=(width // lanes,), out_shape=jax.Shape...]
  transfers between devices with their start and end apart: 6 -> 6, of which waited for: 2 -> 2; matrix products, arithmetic and copies ran while one was open for 43% -> 43% of each run, Pallas kernels for 13% -> 10%
where the time goes in v15:
time: 84 us; the launch traced here: 82.3 us
  matrix products  30.6 us (36%)
  starting transfers between devices  14.3 us (17%)
  between operations  14.2 us (17%)
  Pallas kernels  8.52 us (10%)
  waiting for transfers between devices  7.6 us (9%)
  local copies, waits for them, and re-layouts  3.72 us (4%)
  other arithmetic  3.46 us (4%)
    dot_general x1, matrix products, local(): jnp.einsum('akci,kcm->aim', split, weights, precision=lax.Precision.HIGHE...  15.8 us
    dot_general x1, matrix products, local(): jnp.dot(flat, lax.all_gather(ladder_integrals, PARTS, axis=0, tiled=True)...  14.7 us
    pallas_call x1, Pallas kernels, screened_by_a(): pl.pallas_call(screen_kernel, grid=(width // lanes,), out_shape=jax.Shape...  8.52 us
    ppermute x3, starting transfers between devices, cycle_piece(): got = lax.ppermute(piece, PARTS + ('vir',), pairs)  7.83 us
    all_to_all x1, starting transfers between devices, cycle_reduce(): lax.all_to_all(chip_share, CHIPS, split_axis=0, concat_axis=0, tiled=True)  5.44 us
    all_gather x1, waiting for transfers between devices, local(): lax.all_gather(ladder_integrals, PARTS, axis=0, tiled=True)  4.79 us
    unnamed x7, local copies, waits for them, and re-layouts  2.76 us
    add x1, other arithmetic, cycle_reduce(): chip_share = mine + lax.ppermute(theirs, 'core', pairs)  2.17 us
  transfers between devices with their start and end apart: 6, of which 2 were waited for; matrix products, arithmetic and copies ran while one was open for 43% of the time, Pallas kernels for 10%

profile of v15, /device:TPU:1, one launch (start us, length us, event | category | flops | bytes accessed | tf_op | source)
XLA Modules:
  0.0 82.3 jit_solution(15590736849015077823)
XLA Ops:
  7.2 0.0 copy-start
  7.2 0.0 all-gather.2.cloned.1.call-start
  7.2 0.7 all-gather.2.cloned.1.call-update
  7.9 0.8 copy-done
  8.8 5.2 %collective-permute-start = (f32[16,32,128]{2,1,0:T(8,128)S(1)}, f32[16,32,128]{2,1,0:T(8,128)S(1)}, u32[]{:S(2)}, u32[]{:S(2)}) collective-permute-start(f32[16,32,128]{2,1,0:T(8,128)S(1)} %constant_dynamic-slice_fusion), channel_id=1, source_target_pairs={{0,3},{4,7},{8,11},{12,15},{16,19},{20,23},{24,27},{28,31},{33,32}... | collective-permute-start | bytes 786440 | tf_op jit(solution)/shard_map/ppermute | solution.py:29
  14.0 1.3 %collective-permute-start.1 = (f32[16,32,128]{2,1,0:T(8,128)S(1)}, f32[16,32,128]{2,1,0:T(8,128)S(1)}, u32[]{:S(2)}, u32[]{:S(2)}) collective-permute-start(f32[16,32,128]{2,1,0:T(8,128)S(1)} %constant_dynamic-slice_fusion), channel_id=1, source_target_pairs={{0,2},{4,6},{8,10},{12,14},{16,18},{20,22},{24,26},{28,30},{33,35}... | collective-permute-start | bytes 786440 | tf_op jit(solution)/shard_map/ppermute | solution.py:29
  15.3 1.3 %collective-permute-start.2 = (f32[16,32,128]{2,1,0:T(8,128)S(1)}, f32[16,32,128]{2,1,0:T(8,128)S(1)}, u32[]{:S(2)}, u32[]{:S(2)}) collective-permute-start(f32[16,32,128]{2,1,0:T(8,128)S(1)} %constant_dynamic-slice_fusion), channel_id=1, source_target_pairs={{0,1},{4,5},{8,9},{12,13},{16,17},{20,21},{24,25},{28,29},{33,34},... | collective-permute-start | bytes 786440 | tf_op jit(solution)/shard_map/ppermute | solution.py:29
  16.7 0.8 copy.6
  17.5 0.6 convert_element_type.3.live_ref
  18.1 8.5 %shard_map.59 = f32[32,512,96]{2,1,0:T(8,128)} custom-call(f32[96,16]{1,0:T(8,128)} %convert_element_type.3.live_ref, f32[96,16,1024]{2,1,0:T(8,128)} %amp_ref.1), custom_call_target="tpu_custom_call" | custom-call | tf_op jit(solution)/shard_map/pallas_call | solution.py:58
  26.6 0.0 collective-permute-done
  26.6 0.0 collective-permute-done.1
  26.6 0.0 collective-permute-done.2
  26.6 0.0 copy-start.2
  26.7 15.8 %convolution_bitcast_fusion = f32[16,2,96,128]{3,2,1,0:T(8,128)S(1)} fusion(f32[16,2,96,32,16]{2,3,4,1,0:T(8,128)} %bitcast.25, f32[16,32,128]{2,1,0:T(8,128)S(1)} %collective-permute-done, f32[16,32,128]{2,1,0:T(8,128)S(1)} %collective-permute-done.1, f32[16,32,128]{2,1,0:T(8,128)S(1)} %collective-permute-done.2, ...), kind=kOutput, calls=%fused_computation.3 | convolution fusion | flops 2416115712 | bytes 8912899 | tf_op jit(solution)/shard_map/akci,kcm->aim/dot_general | solution.py:80
  42.5 0.0 copy-start.1
  42.5 1.1 %copy-done.1 = f32[16,2,96,128]{3,2,1,0:T(8,128)} copy-done((f32[16,2,96,128]{3,2,1,0:T(8,128)}, f32[16,2,96,128]{3,2,1,0:T(8,128)S(1)}, u32[]{:S(2)}) %copy-start.1) | copy-done | bytes 1572888
  43.6 0.9 %dynamic-slice_bitcast_fusion = f32[16,96,128]{2,1,0:T(8,128)} fusion(f32[16,2,96,128]{3,2,1,0:T(8,128)S(1)} %convolution_bitcast_fusion, s32[]{:T(128)S(6)} %select_n.65), kind=kLoop, calls=%fused_computation.5 | loop fusion | bytes 1572868 | tf_op jit(solution)/shard_map/jit(dynamic_index_in_dim)/squeeze | solution.py:40
  44.6 1.0 %collective-permute-start.3 = (f32[16,96,128]{2,1,0:T(8,128)}, f32[16,96,128]{2,1,0:T(8,128)S(1)}, u32[]{:S(2)}, u32[]{:S(2)}) collective-permute-start(f32[16,96,128]{2,1,0:T(8,128)} %dynamic-slice_bitcast_fusion), channel_id=1, source_target_pairs={{0,4},{4,0},{1,5},{5,1},{2,6},{6,2},{3,7},{7,3},{8,12},{12,8},{9,1... | collective-permute-start | bytes 2359304 | tf_op jit(solution)/shard_map/ppermute | solution.py:42
  45.5 2.1 %collective-permute-done.3 = f32[16,96,128]{2,1,0:T(8,128)S(1)} collective-permute-done((f32[16,96,128]{2,1,0:T(8,128)}, f32[16,96,128]{2,1,0:T(8,128)S(1)}, u32[]{:S(2)}, u32[]{:S(2)}) %collective-permute-start.3) | collective-permute-done | bytes 786464 | tf_op jit(solution)/shard_map/ppermute | solution.py:42
  47.7 2.2 %bitcast_add_fusion = f32[16,96,128]{2,1,0:T(8,128)} fusion(f32[16,96,128]{2,1,0:T(8,128)S(1)} %collective-permute-done.3, f32[16,2,96,128]{3,2,1,0:T(8,128)} %copy-done.1, s32[]{:T(128)S(6)} %select_n.63), kind=kLoop, calls=%fused_computation.4 | loop fusion | flops 196608 | bytes 2359300 | tf_op jit(solution)/shard_map/add | solution.py:42
  49.8 5.4 %all-to-all-start = ((f32[16,96,128]{2,1,0:T(8,128)}), f32[16,96,128]{2,1,0:T(8,128)S(1)}, u32[]{:S(2)}, u32[]{:S(2)}) async-start(f32[16,96,128]{2,1,0:T(8,128)} %bitcast_add_fusion), calls=%async_computation | async-start | bytes 1572864 | tf_op jit(solution)/shard_map/all_to_all | solution.py:43
  55.3 4.8 %all-gather.2.cloned.1.call-done = f32[1024,1024]{1,0:T(8,128)} async-done(((f32[32,1024]{1,0:T(8,128)}), f32[1024,1024]{1,0:T(8,128)}) %all-gather.2.cloned.1.call-update) | async-done | bytes 4194320 | tf_op jit(solution)/shard_map/all_gather | solution.py:92
  60.1 0.0 copy-done.2
  60.1 14.7 %broadcast_multiply_fusion = f32[96,16,1024]{2,1,0:T(8,128)} fusion(f32[96,16]{1,0:T(8,128)S(1)} %copy-done.2, f32[96,16,1024]{2,1,0:T(8,128)} %amp_ref.1, f32[1024,1024]{1,0:T(8,128)} %all-gather.2.cloned.1.call-done), kind=kOutput, calls=%fused_computation.2 | convolution fusion | flops 9665249280 | bytes 16783360 | tf_op jit(solution)/shard_map/dot_general | solution.py:90
  74.8 0.0 all-to-all-done
  74.8 0.7 reduce_sum.9
  (1 shorter events, 0.0 us)
Async XLA Ops:
  7.2 1.6 %copy-start = (f32[128,32,128]{2,1,0:T(8,128)S(1)}, f32[128,32,128]{2,1,0:T(8,128)}, u32[]{:S(2)}) copy-start(f32[128,32,128]{2,1,0:T(8,128)} %param.7) | copy-start | bytes 6291460
  7.2 52.9 %all-gather.2.cloned.1.call-start = ((), (), s32[]{:S(2)}) async-start(), calls=%async_computation.1 | async-start | bytes 4325376 | tf_op jit(solution)/shard_map/all_gather | solution.py:92
  8.8 17.8 %collective-permute-start = (f32[16,32,128]{2,1,0:T(8,128)S(1)}, f32[16,32,128]{2,1,0:T(8,128)S(1)}, u32[]{:S(2)}, u32[]{:S(2)}) collective-permute-start(f32[16,32,128]{2,1,0:T(8,128)S(1)} %constant_dynamic-slice_fusion), channel_id=1, source_target_pairs={{0,3},{4,7},{8,11},{12,15},{16,19},{20,23},{24,27},{28,31},{33,32}... | collective-permute-start | bytes 786440 | tf_op jit(solution)/shard_map/ppermute | solution.py:29
  14.0 12.6 %collective-permute-start.1 = (f32[16,32,128]{2,1,0:T(8,128)S(1)}, f32[16,32,128]{2,1,0:T(8,128)S(1)}, u32[]{:S(2)}, u32[]{:S(2)}) collective-permute-start(f32[16,32,128]{2,1,0:T(8,128)S(1)} %constant_dynamic-slice_fusion), channel_id=1, source_target_pairs={{0,2},{4,6},{8,10},{12,14},{16,18},{20,22},{24,26},{28,30},{33,35}... | collective-permute-start | bytes 786440 | tf_op jit(solution)/shard_map/ppermute | solution.py:29
  15.3 11.3 %collective-permute-start.2 = (f32[16,32,128]{2,1,0:T(8,128)S(1)}, f32[16,32,128]{2,1,0:T(8,128)S(1)}, u32[]{:S(2)}, u32[]{:S(2)}) collective-permute-start(f32[16,32,128]{2,1,0:T(8,128)S(1)} %constant_dynamic-slice_fusion), channel_id=1, source_target_pairs={{0,1},{4,5},{8,9},{12,13},{16,17},{20,21},{24,25},{28,29},{33,34},... | collective-permute-start | bytes 786440 | tf_op jit(solution)/shard_map/ppermute | solution.py:29
  26.6 33.4 %copy-start.2 = (f32[96,16]{1,0:T(8,128)S(1)}, f32[96,16]{1,0:T(8,128)}, u32[]{:S(2)}) copy-start(f32[96,16]{1,0:T(8,128)} %convert_element_type.3.live_ref) | copy-start | bytes 18436
  42.5 1.1 %copy-start.1 = (f32[16,2,96,128]{3,2,1,0:T(8,128)}, f32[16,2,96,128]{3,2,1,0:T(8,128)S(1)}, u32[]{:S(2)}) copy-start(f32[16,2,96,128]{3,2,1,0:T(8,128)S(1)} %convolution_bitcast_fusion) | copy-start | bytes 4718596
  44.6 3.1 %collective-permute-start.3 = (f32[16,96,128]{2,1,0:T(8,128)}, f32[16,96,128]{2,1,0:T(8,128)S(1)}, u32[]{:S(2)}, u32[]{:S(2)}) collective-permute-start(f32[16,96,128]{2,1,0:T(8,128)} %dynamic-slice_bitcast_fusion), channel_id=1, source_target_pairs={{0,4},{4,0},{1,5},{5,1},{2,6},{6,2},{3,7},{7,3},{8,12},{12,8},{9,1... | collective-permute-start | bytes 2359304 | tf_op jit(solution)/shard_map/ppermute | solution.py:42
  49.8 25.0 %all-to-all-start = ((f32[16,96,128]{2,1,0:T(8,128)}), f32[16,96,128]{2,1,0:T(8,128)S(1)}, u32[]{:S(2)}, u32[]{:S(2)}) async-start(f32[16,96,128]{2,1,0:T(8,128)} %bitcast_add_fusion), calls=%async_computation | async-start | bytes 1572864 | tf_op jit(solution)/shard_map/all_to_all | solution.py:43
Sparse Core Ops, SparseCore 0:
  10.2 49.7 all-gather.1
